TPU v7x, 256 devices: a whole 4x4x8 slice. The times are simulated.
256 devices in a mesh: cam: 8 (over z_lo, x), pt: 32 (over y, z_hi, core).
Axes of the slice: x: 4, y: 4, z: 8 (z_hi: 4, z_lo: 2; z = z_hi * 2 + z_lo), core: 2. Of those that a mesh axis runs over, the one named last changes fastest.
Arguments:
- cameras: float32 [9, 32768], P(None, ('cam', 'pt')), as said below
- cam_first: float32 [9, 32768], P(None, ('cam', 'pt')), may hold values from -0.03 to 0.03
- cam_second: float32 [9, 32768], P(None, ('cam', 'pt')), may hold values from 0.001 to 0.1
- points: float32 [3, 1048576], P(None, ('pt', 'cam')), may hold values from -1 to 1
- pt_first: float32 [3, 1048576], P(None, ('pt', 'cam')), may hold values from -0.03 to 0.03
- pt_second: float32 [3, 1048576], P(None, ('pt', 'cam')), may hold values from 0.001 to 0.1
- observed: float32 [2, 3145728], P(None, ('cam', 'pt')), may hold values from -3 to 3
- tile_camera: int32 [12288], P(('cam', 'pt')), may hold values from 0 to 4095
- point_index: int32 [3145728], P(('cam', 'pt')), may hold values from 0 to 32767
- tile_count: int32 [12288], P(('cam', 'pt')), may hold values from 1 to 256, as said below
Outputs:
- new_cameras: float32 [9, 32768], P(None, ('cam', 'pt'))
- new_cam_first: float32 [9, 32768], P(None, ('cam', 'pt'))
- new_cam_second: float32 [9, 32768], P(None, ('cam', 'pt'))
- new_points: float32 [3, 1048576], P(None, ('pt', 'cam'))
- new_pt_first: float32 [3, 1048576], P(None, ('pt', 'cam'))
- new_pt_second: float32 [3, 1048576], P(None, ('pt', 'cam'))
- final_residual: float32 [2, 3145728], P(None, ('cam', 'pt'))
- final_weight: float32 [3145728], P(('cam', 'pt'))
Inputs may be any that keep to these rules, and one draw needn't show every extreme that they name: `cameras`: rotation vectors within 0.2 a component, translations within 1 sideways and 4 to 6 in depth, focal lengths 0.8 to 1.2, distortion coefficients within 0.05. `tile_count`: some tile holds exactly 256 live slots; the loads differ from device to device.
All inputs are finite; a program needn't handle non-finite values.
Results may differ from a plain program's by a relative error of at most 0.00002.
Values sent between devices are 32-bit elements; how exact they have to be, the bound alone decides.
No kernel may reach another device: no remote copies, remote signals or barrier semaphores. Data moves between devices by JAX's collectives and lax.ppermute only.
A program may use at most 64 MiB of HBM per device.

v0:
```python
import jax
import jax.numpy as jnp
from jax import lax
from jax.sharding import PartitionSpec as P

STEP = 10


def project(camera_tile, point_obs, observed):
    axis_angle = camera_tile[0:3]
    theta_sq = jnp.sum(axis_angle * axis_angle, axis=0)
    sine_term = (
        1.0
        - theta_sq / 6.0
        + theta_sq * theta_sq / 120.0
        - theta_sq * theta_sq * theta_sq / 5040.0
        + theta_sq * theta_sq * theta_sq * theta_sq / 362880.0
    )
    cosine_term = (
        0.5
        - theta_sq / 24.0
        + theta_sq * theta_sq / 720.0
        - theta_sq * theta_sq * theta_sq / 40320.0
        + theta_sq * theta_sq * theta_sq * theta_sq / 3628800.0
    )
    crossed = jnp.stack(
        [
            axis_angle[1] * point_obs[2] - axis_angle[2] * point_obs[1],
            axis_angle[2] * point_obs[0] - axis_angle[0] * point_obs[2],
            axis_angle[0] * point_obs[1] - axis_angle[1] * point_obs[0],
        ]
    )
    inner = jnp.sum(axis_angle * point_obs, axis=0)
    camera_frame = (
        point_obs
        + sine_term * crossed
        + cosine_term * (axis_angle * inner - theta_sq * point_obs)
        + camera_tile[3:6]
    )
    horizontal = camera_frame[0] / camera_frame[2]
    vertical = camera_frame[1] / camera_frame[2]
    radius_sq = horizontal * horizontal + vertical * vertical
    scale_term = camera_tile[6] * (
        1.0 + camera_tile[7] * radius_sq + camera_tile[8] * radius_sq * radius_sq
    )
    return jnp.stack([scale_term * horizontal - observed[0], scale_term * vertical - observed[1]])


def reweight(residual):
    return 1.0 / (1.0 + residual[0] * residual[0] + residual[1] * residual[1])


def adam_step(current, moment_one, moment_two, gradient):
    moment_one = 0.9 * moment_one + 0.1 * gradient
    moment_two = 0.999 * moment_two + 0.001 * gradient * gradient
    corrected_one = moment_one / (1.0 - 0.9**STEP)
    corrected_two = moment_two / (1.0 - 0.999**STEP)
    return (
        current - 0.05 * corrected_one / (jnp.sqrt(corrected_two) + 1e-08),
        moment_one,
        moment_two,
    )


def on_device(
    cameras,
    cam_first,
    cam_second,
    points,
    pt_first,
    pt_second,
    observed,
    tile_camera,
    point_index,
    tile_count,
):
    tile_num = tile_count.shape[0]
    tile_len = observed.shape[1] // tile_num
    obs_grid = observed.reshape(2, tile_num, tile_len)
    slot = lax.broadcasted_iota(jnp.int32, (tile_num, tile_len), 1)
    valid_mask = (slot < tile_count[:, None]).astype(jnp.float32)

    def residuals(camera_block, point_block):
        camera_tile = jnp.take(camera_block, tile_camera, axis=1)[:, :, None]
        point_obs = jnp.take(point_block, point_index, axis=1).reshape(3, tile_num, tile_len)
        return project(camera_tile, point_obs, obs_grid)

    camera_block = lax.all_gather(cameras, "pt", axis=1, tiled=True)
    point_block = lax.all_gather(points, "cam", axis=1, tiled=True)
    residual, pullback = jax.vjp(residuals, camera_block, point_block)
    cotangent = residual * (reweight(residual) * valid_mask)
    camera_grad, point_grad = pullback(cotangent)
    camera_share = lax.psum_scatter(camera_grad, "pt", scatter_dimension=1, tiled=True)
    point_share = lax.psum_scatter(point_grad, "cam", scatter_dimension=1, tiled=True)
    new_cameras, new_cam_first, new_cam_second = adam_step(
        cameras, cam_first, cam_second, camera_share
    )
    new_points, new_pt_first, new_pt_second = adam_step(points, pt_first, pt_second, point_share)
    new_cam_block = lax.all_gather(new_cameras, "pt", axis=1, tiled=True)
    new_pt_block = lax.all_gather(new_points, "cam", axis=1, tiled=True)
    final = residuals(new_cam_block, new_pt_block)
    final_weight = (reweight(final) * valid_mask).reshape(-1)
    final_residual = (final * valid_mask).reshape(2, -1)
    return (
        new_cameras,
        new_cam_first,
        new_cam_second,
        new_points,
        new_pt_first,
        new_pt_second,
        final_residual,
        final_weight,
    )


def solution(mesh):
    placed = (
        P(None, ("cam", "pt")),
        P(None, ("cam", "pt")),
        P(None, ("cam", "pt")),
        P(None, ("pt", "cam")),
        P(None, ("pt", "cam")),
        P(None, ("pt", "cam")),
        P(None, ("cam", "pt")),
        P(("cam", "pt")),
        P(("cam", "pt")),
        P(("cam", "pt")),
    )
    return jax.shard_map(
        on_device,
        mesh=mesh,
        in_specs=placed,
        out_specs=(
            P(None, ("cam", "pt")),
            P(None, ("cam", "pt")),
            P(None, ("cam", "pt")),
            P(None, ("pt", "cam")),
            P(None, ("pt", "cam")),
            P(None, ("pt", "cam")),
            P(None, ("cam", "pt")),
            P(("cam", "pt")),
        ),
        check_vma=False,
    )
```

profile of v0, /device:TPU:6, one launch (start us, length us, event | category | flops | bytes accessed | tf_op | source)
XLA Modules:
  0.0 670.2 jit_solution(13271368073493325494)
XLA Ops:
  8.5 0.8 compare_select_fusion
  9.3 0.8 compare_and_fusion
  10.2 0.8 copy.192
  11.0 56.5 %all_gather.12 = f32[9,4096]{0,1:T(8,128)S(1)} all-gather(f32[9,128]{0,1:T(8,128)S(1)} %copy.192), channel_id=1, replica_groups=mesh['cam'=8,'pt'=32] {'pt'}, dimensions={1}, use_global_device_ids=true | all-gather | bytes 152064 | tf_op jit(solution)/shard_map/all_gather | solution.py:88
  68.2 1.5 copy.194
  69.7 163.1 %all_gather.13 = f32[3,32768]{0,1:T(8,128)} all-gather(f32[3,4096]{0,1:T(8,128)S(1)} %copy.194), channel_id=1, replica_groups=mesh['cam'=8,'pt'=32] {'cam'}, dimensions={1}, use_global_device_ids=true | all-gather | bytes 442368 | tf_op jit(solution)/shard_map/all_gather | solution.py:89
  232.8 46.8 %gather_fusion.1 = f32[12288,3]{1,0:T(8,128)} fusion(f32[3,32768]{0,1:T(8,128)} %all_gather.13, s32[12288]{0:T(1024)S(1)} %get-tuple-element.109), kind=kCustom, calls=%fused_computation.1 | custom fusion | bytes 344064 | tf_op jit(solution)/shard_map/jvp(jit(_take))/gather | solution.py:85
  279.6 6.4 fusion.3
  286.0 8.3 %slice_reduce_fusion.4 = (f32[12288]{0:T(1024)S(1)}, f32[12288]{0:T(1024)S(1)}, f32[12288]{0:T(1024)S(1)}) fusion(f32[3,12288]{0,1:T(8,128)S(1)} %get-tuple-element.80), kind=kLoop, calls=%fused_computation.12 | loop fusion | bytes 294912 | tf_op jit(solution)/shard_map/jvp()/slice | solution.py:28
  294.5 4.4 copy.195
  301.2 1.3 scatter_custom_fusion
  302.4 1.3 copy.207
  303.8 4.0 copy.217
  307.8 72.7 %scatter_custom_fusion.1 = f32[3,32768]{0,1:T(8,128)} fusion(s32[12288]{0:T(1024)S(1)} %get-tuple-element.108, f32[12288,3]{1,0:T(8,128)} %bitcast.185, f32[]{:T(128)} %constant.113.clone.1), kind=kCustom, calls=%fused_computation.6 | custom fusion | flops 36864 | bytes 393728 | tf_op jit(solution)/shard_map/transpose(jvp(jit(_take)))/scatter-add | solution.py:85
  381.2 1.3 divide_subtract_fusion.1
  382.6 44.2 %all_gather.14 = f32[9,4096]{1,0:T(8,128)S(1)} all-gather(f32[9,128]{1,0:T(8,128)S(1)} %get-tuple-element.65), channel_id=1, replica_groups=mesh['cam'=8,'pt'=32] {'pt'}, dimensions={1}, use_global_device_ids=true | all-gather | bytes 152064 | tf_op jit(solution)/shard_map/all_gather | solution.py:99
  428.5 126.3 %reduce-scatter.7.cloned.1.call-done = f32[4096,3]{1,0:T(8,128)} async-done(((f32[32768,3]{1,0:T(8,128)}), f32[4096,3]{1,0:T(8,128)}) %reduce-scatter.7.cloned.1.call-update) | async-done | bytes 49168
  554.8 2.2 copy.216
  557.8 29.1 %all_gather.15 = f32[3,32768]{1,0:T(4,128)S(1)} all-gather(f32[3,4096]{1,0:T(4,128)S(1)} %get-tuple-element.62), channel_id=1, replica_groups=mesh['cam'=8,'pt'=32] {'cam'}, dimensions={1}, use_global_device_ids=true | all-gather | bytes 442368 | tf_op jit(solution)/shard_map/all_gather | solution.py:100
  586.8 8.5 %copy.212 = f32[3,32768]{0,1:T(8,128)} copy(f32[3,32768]{1,0:T(4,128)S(1)} %all_gather.15) | data formatting | bytes 786432 | tf_op jit(solution)/shard_map/all_gather | solution.py:100
  595.4 46.8 %gather_fusion.3 = f32[12288,3]{1,0:T(8,128)} fusion(f32[3,32768]{0,1:T(8,128)} %copy.212, s32[12288]{0:T(1024)S(1)} %get-tuple-element.109), kind=kCustom, calls=%fused_computation.3 | custom fusion | bytes 344064 | tf_op jit(solution)/shard_map/jit(_take)/gather | solution.py:85
  642.1 6.4 fusion.2
  648.5 8.3 %slice_reduce_fusion.2 = (f32[12288]{0:T(1024)S(1)}, f32[12288]{0:T(1024)S(1)}, f32[12288]{0:T(1024)S(1)}) fusion(f32[3,12288]{0,1:T(8,128)S(1)} %get-tuple-element.61), kind=kLoop, calls=%fused_computation.10 | loop fusion | bytes 294912 | tf_op jit(solution)/shard_map/slice | solution.py:28
  657.0 4.4 copy.213
  (95 shorter events, 9.4 us)
Async XLA Ops:
  7.2 374.1 %reduce-scatter.5.cloned.1.call-start = ((), (), s32[]{:S(2)}) async-start(), calls=%async_computation.2 | async-start | bytes 270336 | tf_op jit(solution)/shard_map/reduce_scatter | solution.py:93
  294.3 4.7 copy-start.2
  294.3 5.2 copy-start.9
  303.8 251.0 %reduce-scatter.7.cloned.1.call-start = ((), (), s32[]{:S(2)}) async-start(), calls=%async_computation.3 | async-start | bytes 18874368
  380.5 0.7 copy-start.5
  380.5 0.7 copy-start.7
  380.5 0.7 copy-start.8
  380.5 176.5 %copy-start = (f32[3,4096]{1,0:T(4,128)S(1)}, f32[3,4096]{1,0:T(4,128)}, u32[]{:S(2)}) copy-start(f32[3,4096]{1,0:T(4,128)} %param.13) | copy-start | bytes 147460
  380.5 176.5 %copy-start.3 = (f32[3,4096]{1,0:T(4,128)S(1)}, f32[3,4096]{1,0:T(4,128)}, u32[]{:S(2)}) copy-start(f32[3,4096]{1,0:T(4,128)} %param.14) | copy-start | bytes 147460
  380.5 176.5 %copy-start.4 = (f32[3,4096]{1,0:T(4,128)S(1)}, f32[3,4096]{1,0:T(4,128)}, u32[]{:S(2)}) copy-start(f32[3,4096]{1,0:T(4,128)} %param.15) | copy-start | bytes 147460
  382.6 212.8 %copy-start.6 = (f32[9,128]{1,0:T(8,128)}, f32[9,128]{1,0:T(8,128)S(1)}, u32[]{:S(2)}) copy-start(f32[9,128]{1,0:T(8,128)S(1)} %get-tuple-element.65) | copy-start | bytes 13828
  557.8 37.6 %copy-start.1 = (f32[3,4096]{1,0:T(4,128)}, f32[3,4096]{1,0:T(4,128)S(1)}, u32[]{:S(2)}) copy-start(f32[3,4096]{1,0:T(4,128)S(1)} %get-tuple-element.62) | copy-start | bytes 147460
Sparse Core Ops, SparseCore 0:
  303.9 77.2 reduce-scatter.4
  383.8 170.8 reduce-scatter.6
where the time goes:
time: 673 us; the launch traced here: 670 us
  blocking collectives  293 us (44%)
  local copies, waits for them, and re-layouts  141 us (21%)
  waiting for transfers between devices  127 us (19%)
  other arithmetic  95.2 us (14%)
  between operations  14.5 us (2%)
    all_gather x1, blocking collectives, on_device(): point_block = lax.all_gather(points, 'cam', axis=1, tiled=True)  163 us
    unnamed x3, waiting for transfers between devices  126 us
    gather x4, local copies, waits for them, and re-layouts, residuals(): jnp.take(point_block, point_index, axis=1).reshape(3, tile_num, tile_len)  102 us
    scatter-add x1, other arithmetic, residuals(): jnp.take(point_block, point_index, axis=1).reshape(3, tile_num, tile_len)  72.7 us
    all_gather x1, blocking collectives, on_device(): camera_block = lax.all_gather(cameras, 'pt', axis=1, tiled=True)  56.5 us
    all_gather x1, blocking collectives, on_device(): new_cam_block = lax.all_gather(new_cameras, 'pt', axis=1, tiled=True)  44.2 us
    all_gather x1, blocking collectives, on_device(): new_pt_block = lax.all_gather(new_points, 'cam', axis=1, tiled=True)  29.1 us
  transfers between devices with their start and end apart: 2, of which 2 were waited for; matrix products, arithmetic and copies ran while one was open for 12% of the time, Pallas kernels for 0%

commit v1 on v0

--- a/solution.py
+++ b/solution.py
@@ -85,19 +85,44 @@
         point_obs = jnp.take(point_block, point_index, axis=1).reshape(3, tile_num, tile_len)
         return project(camera_tile, point_obs, obs_grid)
 
-    camera_block = lax.all_gather(cameras, "pt", axis=1, tiled=True)
-    point_block = lax.all_gather(points, "cam", axis=1, tiled=True)
+    cam_rows, cam_cols = cameras.shape
+    pt_rows, pt_cols = points.shape
+    n_pt = lax.axis_size("pt")
+    n_cam = lax.axis_size("cam")
+
+    def gather_cams(local):
+        stacked = lax.all_gather(local, "pt", axis=0)
+        return stacked.transpose(1, 0, 2).reshape(cam_rows, n_pt * cam_cols)
+
+    def gather_pts(local):
+        flat = local.reshape(pt_rows * pt_cols // 128, 128)
+        stacked = lax.all_gather(flat, "cam", axis=0)
+        stacked = stacked.reshape(n_cam, pt_rows, pt_cols)
+        return stacked.transpose(1, 0, 2).reshape(pt_rows, n_cam * pt_cols)
+
+    def scatter_cams(grad):
+        parts = grad.reshape(cam_rows, n_pt, cam_cols).transpose(1, 0, 2)
+        return lax.psum_scatter(parts, "pt", scatter_dimension=0, tiled=False)
+
+    def scatter_pts(grad):
+        parts = grad.reshape(pt_rows, n_cam, pt_cols).transpose(1, 0, 2)
+        parts = parts.reshape(n_cam, pt_rows * pt_cols // 128, 128)
+        share = lax.psum_scatter(parts, "cam", scatter_dimension=0, tiled=False)
+        return share.reshape(pt_rows, pt_cols)
+
+    camera_block = gather_cams(cameras)
+    point_block = gather_pts(points)
     residual, pullback = jax.vjp(residuals, camera_block, point_block)
     cotangent = residual * (reweight(residual) * valid_mask)
     camera_grad, point_grad = pullback(cotangent)
-    camera_share = lax.psum_scatter(camera_grad, "pt", scatter_dimension=1, tiled=True)
-    point_share = lax.psum_scatter(point_grad, "cam", scatter_dimension=1, tiled=True)
+    camera_share = scatter_cams(camera_grad)
+    point_share = scatter_pts(point_grad)
     new_cameras, new_cam_first, new_cam_second = adam_step(
         cameras, cam_first, cam_second, camera_share
     )
     new_points, new_pt_first, new_pt_second = adam_step(points, pt_first, pt_second, point_share)
-    new_cam_block = lax.all_gather(new_cameras, "pt", axis=1, tiled=True)
-    new_pt_block = lax.all_gather(new_points, "cam", axis=1, tiled=True)
+    new_cam_block = gather_cams(new_cameras)
+    new_pt_block = gather_pts(new_points)
     final = residuals(new_cam_block, new_pt_block)
     final_weight = (reweight(final) * valid_mask).reshape(-1)
     final_residual = (final * valid_mask).reshape(2, -1)

time: 673 us -> 414 us (0.62)
  blocking collectives: 293 us -> 146 us
  waiting for transfers between devices: 127 us -> 0.07 us
  local copies, waits for them, and re-layouts: 141 us -> 157 us
    all_gather x4, blocking collectives: 293 us -> 146 us  [the longest x2 88.1 us: gather_cams(): stacked = lax.all_gather(local, 'pt', axis=0)]
    unnamed x3 -> x2, waiting for transfers between devices: 126 us -> 0.03 us
    transpose x0 -> x4, local copies, waits for them, and re-layouts: none -> 17.6 us  [the longest x2 16.3 us: gather_pts(): return stacked.transpose(1, 0, 2).reshape(pt_rows, n_cam * pt_cols)]
    reshape x0 -> x5, local copies, waits for them, and re-layouts: none -> 12 us  [the longest x1 9.37 us: scatter_pts(): parts = grad.reshape(pt_rows, n_cam, pt_cols).transpose(1, 0, 2)]
    all_gather x2 -> x0, local copies, waits for them, and re-layouts: 9.15 us -> none  [the longest x1 8.52 us: on_device(): new_pt_block = lax.all_gather(new_points, 'cam', axis=1, tiled=True)]
  transfers between devices with their start and end apart: 2 -> 2, of which waited for: 2 -> 0; matrix products, arithmetic and copies ran while one was open for 12% -> 22% of each run, Pallas kernels for 0% -> 0%
where the time goes in v1:
time: 414 us; the launch traced here: 413 us
  local copies, waits for them, and re-layouts  157 us (38%)
  blocking collectives  146 us (35%)
  other arithmetic  95.2 us (23%)
  between operations  14.6 us (4%)
    gather x4, local copies, waits for them, and re-layouts, residuals(): jnp.take(point_block, point_index, axis=1).reshape(3, tile_num, tile_len)  102 us
    all_gather x2, blocking collectives, gather_cams(): stacked = lax.all_gather(local, 'pt', axis=0)  88.1 us
    scatter-add x1, other arithmetic, residuals(): jnp.take(point_block, point_index, axis=1).reshape(3, tile_num, tile_len)  72.7 us
    all_gather x2, blocking collectives, gather_pts(): stacked = lax.all_gather(flat, 'cam', axis=0)  57.6 us
    transpose x2, local copies, waits for them, and re-layouts, gather_pts(): return stacked.transpose(1, 0, 2).reshape(pt_rows, n_cam * pt_cols)  16.3 us
    reduce_sum x2, other arithmetic, project(): inner = jnp.sum(axis_angle * point_obs, axis=0)  12.8 us
    reshape x1, local copies, waits for them, and re-layouts, scatter_pts(): parts = grad.reshape(pt_rows, n_cam, pt_cols).transpose(1, 0, 2)  9.37 us
    slice x1, local copies, waits for them, and re-layouts, project(): point_obs[1]  8.34 us
  transfers between devices with their start and end apart: 2, of which 0 were waited for; matrix products, arithmetic and copies ran while one was open for 22% of the time, Pallas kernels for 0%

profile of v1, /device:TPU:6, one launch (start us, length us, event | category | flops | bytes accessed | tf_op | source)
XLA Modules:
  0.0 413.1 jit_solution(14320589316737526829)
XLA Ops:
  9.3 0.8 compare_and_fusion
  10.2 48.5 %all-gather.2 = f32[32,9,128]{2,1,0:T(8,128)S(1)} all-gather(f32[1,9,128]{2,1,0:T(8,128)} %bitcast.229), channel_id=2, replica_groups=mesh['cam'=8,'pt'=32] {'pt'}, dimensions={0}, use_global_device_ids=true | all-gather | bytes 152064 | tf_op jit(solution)/shard_map/all_gather | solution.py:94
  60.1 0.9 all_gather_reshape.6
  61.0 28.7 %all_gather.20 = f32[8,96,128]{2,1,0:T(8,128)S(1)} all-gather(f32[1,96,128]{2,1,0:T(8,128)S(1)} %all_gather_reshape.6), channel_id=1, replica_groups=mesh['cam'=8,'pt'=32] {'cam'}, dimensions={0}, use_global_device_ids=true | all-gather | bytes 442368 | tf_op jit(solution)/shard_map/all_gather | solution.py:99
  89.9 8.2 %copy.132 = f32[3,8,4096]{0,2,1:T(8,128)} copy(f32[3,8,4096]{2,0,1:T(4,128)S(1)} %bitcast.210) | data formatting | bytes 786432 | tf_op jit(solution)/shard_map/transpose | solution.py:101
  98.0 46.8 %gather_fusion.1 = f32[12288,3]{1,0:T(8,128)} fusion(f32[3,32768]{0,1:T(8,128)} %bitcast.205, s32[12288]{0:T(1024)S(1)} %get-tuple-element.85), kind=kCustom, calls=%fused_computation.1 | custom fusion | bytes 344064 | tf_op jit(solution)/shard_map/jvp(jit(_take))/gather | solution.py:85
  144.8 6.4 %fusion.3 = (f32[12288]{0:T(1024)S(1)}, f32[3,12288]{0,1:T(8,128)S(1)}) fusion(f32[3,48]{0,1:T(8,128)S(1)} %copy.156, f32[12288,3]{1,0:T(8,128)} %gather_fusion.1, pred[12288]{0:T(1024)(128)(4,1)S(1)} %compare_and_fusion), kind=kLoop, calls=%fused_computation.18 | loop fusion | flops 98304 | bytes 356928 | tf_op jit(solution)/shard_map/jvp()/reduce_sum | solution.py:33
  151.2 8.3 %slice_reduce_fusion.4 = (f32[12288]{0:T(1024)S(1)}, f32[12288]{0:T(1024)S(1)}, f32[12288]{0:T(1024)S(1)}) fusion(f32[3,12288]{0,1:T(8,128)S(1)} %get-tuple-element.56), kind=kLoop, calls=%fused_computation.12 | loop fusion | bytes 294912 | tf_op jit(solution)/shard_map/jvp()/slice | solution.py:28
  159.8 4.4 %copy.133 = f32[3,48,256]{2,1,0:T(8,128)S(1)} copy(f32[3,48,256]{0,2,1:T(8,128)} %bitcast.202) | data formatting | bytes 294912 | tf_op jit(solution)/shard_map/jvp(jit(_take))/gather | solution.py:85
  166.4 1.3 scatter_custom_fusion
  167.7 1.3 copy.145
  169.2 4.0 copy.153
  173.2 72.7 %scatter_custom_fusion.1 = f32[3,32768]{0,1:T(8,128)} fusion(s32[12288]{0:T(1024)S(1)} %get-tuple-element.84, f32[12288,3]{1,0:T(8,128)} %bitcast.207, f32[]{:T(128)} %constant.113.clone.1), kind=kCustom, calls=%fused_computation.6 | custom fusion | flops 36864 | bytes 393728 | tf_op jit(solution)/shard_map/transpose(jvp(jit(_take)))/scatter-add | solution.py:85
  246.0 9.4 %copy.147 = f32[3,8,4096]{2,0,1:T(4,128)S(1)} copy(f32[3,8,4096]{0,2,1:T(8,128)} %bitcast.201) | data formatting | bytes 786432 | tf_op jit(solution)/shard_map/reshape | solution.py:108
  255.3 1.0 reshape.1190
  256.7 1.3 divide_subtract_fusion.1
  258.1 39.6 %all-gather.3 = f32[32,9,128]{2,1,0:T(8,128)S(1)} all-gather(f32[1,9,128]{2,1,0:T(8,128)S(1)} %bitcast.230), channel_id=3, replica_groups=mesh['cam'=8,'pt'=32] {'pt'}, dimensions={0}, use_global_device_ids=true | all-gather | bytes 152064 | tf_op jit(solution)/shard_map/all_gather | solution.py:94
  299.4 0.8 reshape_reduce_scatter.3
  301.0 28.9 %all_gather.23 = f32[8,96,128]{2,1,0:T(8,128)S(1)} all-gather(f32[1,96,128]{2,1,0:T(8,128)S(1)} %all_gather_reshape.7), channel_id=1, replica_groups=mesh['cam'=8,'pt'=32] {'cam'}, dimensions={0}, use_global_device_ids=true | all-gather | bytes 442368 | tf_op jit(solution)/shard_map/all_gather | solution.py:99
  330.1 8.2 %copy.150 = f32[3,8,4096]{0,2,1:T(8,128)} copy(f32[3,8,4096]{2,0,1:T(4,128)S(1)} %bitcast.212) | data formatting | bytes 786432 | tf_op jit(solution)/shard_map/transpose | solution.py:101
  338.2 46.8 %gather_fusion.3 = f32[12288,3]{1,0:T(8,128)} fusion(f32[3,32768]{0,1:T(8,128)} %bitcast.204, s32[12288]{0:T(1024)S(1)} %get-tuple-element.85), kind=kCustom, calls=%fused_computation.3 | custom fusion | bytes 344064 | tf_op jit(solution)/shard_map/jit(_take)/gather | solution.py:85
  385.0 6.4 %fusion.2 = (f32[12288]{0:T(1024)S(1)}, f32[3,12288]{0,1:T(8,128)S(1)}) fusion(f32[3,48]{0,1:T(8,128)S(1)} %copy.158, f32[12288,3]{1,0:T(8,128)} %gather_fusion.3, pred[12288]{0:T(1024)(128)(4,1)S(1)} %compare_and_fusion), kind=kLoop, calls=%fused_computation.15 | loop fusion | flops 98304 | bytes 356928 | tf_op jit(solution)/shard_map/reduce_sum | solution.py:33
  391.4 8.3 %slice_reduce_fusion.2 = (f32[12288]{0:T(1024)S(1)}, f32[12288]{0:T(1024)S(1)}, f32[12288]{0:T(1024)S(1)}) fusion(f32[3,12288]{0,1:T(8,128)S(1)} %get-tuple-element.37), kind=kLoop, calls=%fused_computation.10 | loop fusion | bytes 294912 | tf_op jit(solution)/shard_map/slice | solution.py:28
  399.8 4.4 %copy.151 = f32[3,48,256]{2,1,0:T(8,128)S(1)} copy(f32[3,48,256]{0,2,1:T(8,128)} %bitcast.203) | data formatting | bytes 294912 | tf_op jit(solution)/shard_map/jit(_take)/gather | solution.py:85
  (101 shorter events, 11.1 us)
Async XLA Ops:
  7.2 249.5 %reduce-scatter.3.cloned.1.call-start = ((), (), s32[]{:S(2)}) async-start(), calls=%async_computation.2 | async-start | bytes 270336 | tf_op jit(solution)/shard_map/reduce_scatter | solution.py:105
  159.6 4.7 %copy-start.2 = (f32[2,12288]{1,0:T(2,128)S(1)}, f32[2,12288]{1,0:T(2,128)}, u32[]{:S(2)}) copy-start(f32[2,12288]{1,0:T(2,128)} %param.16) | copy-start | bytes 294916
  159.6 5.2 %copy-start.9 = (s32[48]{0:T(128)S(1)}, s32[48]{0:T(128)}, u32[]{:S(2)}) copy-start(s32[48]{0:T(128)} %param.19) | copy-start | bytes 580
  169.0 130.3 %reduce-scatter.5.cloned.1.call-start = ((), (), s32[]{:S(2)}) async-start(), calls=%async_computation.3 | async-start | bytes 442368 | tf_op jit(solution)/shard_map/reduce_scatter | solution.py:110
  245.9 10.8 %copy-start.5 = (f32[9,128]{1,0:T(8,128)S(1)}, f32[9,128]{1,0:T(8,128)}, u32[]{:S(2)}) copy-start(f32[9,128]{1,0:T(8,128)} %param.10) | copy-start | bytes 13828
  245.9 10.8 %copy-start.7 = (f32[9,128]{1,0:T(8,128)S(1)}, f32[9,128]{1,0:T(8,128)}, u32[]{:S(2)}) copy-start(f32[9,128]{1,0:T(8,128)} %param.11) | copy-start | bytes 13828
  245.9 10.8 %copy-start.8 = (f32[9,128]{1,0:T(8,128)S(1)}, f32[9,128]{1,0:T(8,128)}, u32[]{:S(2)}) copy-start(f32[9,128]{1,0:T(8,128)} %param.12) | copy-start | bytes 13828
  245.9 54.3 %copy-start = (f32[3,4096]{1,0:T(4,128)S(1)}, f32[3,4096]{1,0:T(4,128)}, u32[]{:S(2)}) copy-start(f32[3,4096]{1,0:T(4,128)} %param.13) | copy-start | bytes 147460
  245.9 54.3 %copy-start.3 = (f32[3,4096]{1,0:T(4,128)S(1)}, f32[3,4096]{1,0:T(4,128)}, u32[]{:S(2)}) copy-start(f32[3,4096]{1,0:T(4,128)} %param.14) | copy-start | bytes 147460
  246.0 54.3 %copy-start.4 = (f32[3,4096]{1,0:T(4,128)S(1)}, f32[3,4096]{1,0:T(4,128)}, u32[]{:S(2)}) copy-start(f32[3,4096]{1,0:T(4,128)} %param.15) | copy-start | bytes 147460
  258.0 80.2 %copy-start.6 = (f32[9,128]{1,0:T(8,128)}, f32[9,128]{1,0:T(8,128)S(1)}, u32[]{:S(2)}) copy-start(f32[9,128]{1,0:T(8,128)S(1)} %get-tuple-element.41) | copy-start | bytes 13828
  301.0 37.3 %copy-start.1 = (f32[3,4096]{1,0:T(4,128)}, f32[3,4096]{1,0:T(4,128)S(1)}, u32[]{:S(2)}) copy-start(f32[3,4096]{1,0:T(4,128)S(1)} %get-tuple-element.38) | copy-start | bytes 147460
Sparse Core Ops, SparseCore 0:
  169.1 82.5 reduce-scatter.2
  256.5 33.7 reduce-scatter.4

commit v2 on v1

--- a/solution.py
+++ b/solution.py
@@ -1,9 +1,127 @@
+import functools
+
 import jax
 import jax.numpy as jnp
 from jax import lax
 from jax.sharding import PartitionSpec as P
+from jax.experimental import pallas as pl
+from jax.experimental.pallas import tpu as pltpu
 
 STEP = 10
+from jax.experimental import pallas as pl
+from jax.experimental.pallas import tpu as pltpu
+
+LANES = 128
+SLOT_BLK = 1024
+
+
+def _split3(x):
+    first = x.astype(jnp.bfloat16)
+    rest = x - first.astype(jnp.float32)
+    second = rest.astype(jnp.bfloat16)
+    third = (rest - second.astype(jnp.float32)).astype(jnp.bfloat16)
+    return first, second, third
+
+
+def _gather_kernel(table_ref, index_ref, out_ref, pieces_ref):
+    rows = table_ref.shape[0]
+    highs = table_ref.shape[1]
+
+    @pl.when(pl.program_id(0) == 0)
+    def _():
+        first, second, third = _split3(table_ref[...])
+        pieces_ref[0:rows, :] = first
+        pieces_ref[rows:2 * rows, :] = second
+        pieces_ref[2 * rows:3 * rows, :] = third
+
+    index = index_ref[...]
+    blk = index.shape[1]
+    high = index // LANES
+    low = index % LANES
+    onehot = (lax.broadcasted_iota(jnp.int32, (highs, blk), 0) == high).astype(jnp.bfloat16)
+    picked = jnp.dot(pieces_ref[...], onehot, preferred_element_type=jnp.float32)
+    match = lax.broadcasted_iota(jnp.int32, (LANES, blk), 0) == low
+    ncoord = rows // LANES
+    sums = []
+    for g in range(3 * ncoord):
+        part = picked[g * LANES:(g + 1) * LANES, :]
+        sums.append(jnp.sum(jnp.where(match, part, 0.0), axis=0, keepdims=True))
+    for c in range(ncoord):
+        out_ref[c:c + 1, :] = sums[c] + sums[ncoord + c] + sums[2 * ncoord + c]
+
+
+def gather_points(table, index):
+    ncoord = table.shape[0] // LANES
+    highs = table.shape[1]
+    slots = index.shape[0]
+    blk = min(SLOT_BLK, slots)
+    return pl.pallas_call(
+        _gather_kernel,
+        grid=(slots // blk,),
+        in_specs=[
+            pl.BlockSpec((ncoord * LANES, highs), lambda i: (0, 0)),
+            pl.BlockSpec((1, blk), lambda i: (0, i)),
+        ],
+        out_specs=pl.BlockSpec((ncoord, blk), lambda i: (0, i)),
+        out_shape=jax.ShapeDtypeStruct((ncoord, slots), jnp.float32),
+        scratch_shapes=[pltpu.VMEM((3 * ncoord * LANES, highs), jnp.bfloat16)],
+        compiler_params=pltpu.CompilerParams(dimension_semantics=("arbitrary",)),
+    )(table, index.reshape(1, slots))
+
+
+def _scatter_kernel(grad_ref, index_ref, out_ref, acc_ref):
+    ncoord, slots = grad_ref.shape
+    highs = out_ref.shape[1]
+    rows = ncoord * LANES
+    blk = min(SLOT_BLK, slots)
+
+    def chunk(step, carry):
+        start = pl.multiple_of(step * blk, blk)
+        index = index_ref[:, pl.ds(start, blk)]
+        high = index // LANES
+        low = index % LANES
+        onehot = (lax.broadcasted_iota(jnp.int32, (highs, blk), 0) == high).astype(jnp.bfloat16)
+        match = lax.broadcasted_iota(jnp.int32, (LANES, blk), 0) == low
+        grad = grad_ref[:, pl.ds(start, blk)]
+        spread = jnp.concatenate(
+            [jnp.where(match, grad[c:c + 1, :], 0.0) for c in range(ncoord)], axis=0
+        )
+        first, second, third = _split3(spread)
+        weights = jnp.concatenate([first, second, third], axis=0)
+        acc_ref[...] += lax.dot_general(
+            weights, onehot, (((1,), (1,)), ((), ())), preferred_element_type=jnp.float32
+        )
+        return carry
+
+    acc_ref[...] = jnp.zeros(acc_ref.shape, jnp.float32)
+    lax.fori_loop(0, slots // blk, chunk, 0)
+    acc = acc_ref[...]
+    out_ref[...] = (acc[0:rows] + acc[rows:2 * rows]) + acc[2 * rows:3 * rows]
+
+
+def scatter_points(grad, index, highs):
+    ncoord, slots = grad.shape
+    return pl.pallas_call(
+        _scatter_kernel,
+        out_shape=jax.ShapeDtypeStruct((ncoord * LANES, highs), jnp.float32),
+        scratch_shapes=[pltpu.VMEM((3 * ncoord * LANES, highs), jnp.float32)],
+    )(grad, index.reshape(1, slots))
+
+
+@functools.partial(jax.custom_vjp, nondiff_argnums=(2,))
+def take_points(table, index, highs):
+    return gather_points(table, index)
+
+
+def _take_fwd(table, index, highs):
+    return gather_points(table, index), index
+
+
+def _take_bwd(highs, index, grad):
+    return scatter_points(grad, index, highs), None
+
+
+take_points.defvjp(_take_fwd, _take_bwd)
 
 
 def project(camera_tile, point_obs, observed):
@@ -82,7 +200,7 @@
 
     def residuals(camera_block, point_block):
         camera_tile = jnp.take(camera_block, tile_camera, axis=1)[:, :, None]
-        point_obs = jnp.take(point_block, point_index, axis=1).reshape(3, tile_num, tile_len)
+        point_obs = take_points(point_block, point_index, point_block.shape[1]).reshape(3, tile_num, tile_len)
         return project(camera_tile, point_obs, obs_grid)
 
     cam_rows, cam_cols = cameras.shape
@@ -95,18 +213,18 @@
         return stacked.transpose(1, 0, 2).reshape(cam_rows, n_pt * cam_cols)
 
     def gather_pts(local):
-        flat = local.reshape(pt_rows * pt_cols // 128, 128)
+        flat = local.reshape(pt_rows * pt_cols // LANES, LANES)
         stacked = lax.all_gather(flat, "cam", axis=0)
-        stacked = stacked.reshape(n_cam, pt_rows, pt_cols)
-        return stacked.transpose(1, 0, 2).reshape(pt_rows, n_cam * pt_cols)
+        stacked = stacked.reshape(n_cam, pt_rows, pt_cols // LANES, LANES)
+        return stacked.transpose(1, 3, 0, 2).reshape(pt_rows * LANES, n_cam * pt_cols // LANES)
 
     def scatter_cams(grad):
         parts = grad.reshape(cam_rows, n_pt, cam_cols).transpose(1, 0, 2)
         return lax.psum_scatter(parts, "pt", scatter_dimension=0, tiled=False)
 
     def scatter_pts(grad):
-        parts = grad.reshape(pt_rows, n_cam, pt_cols).transpose(1, 0, 2)
-        parts = parts.reshape(n_cam, pt_rows * pt_cols // 128, 128)
+        parts = grad.reshape(pt_rows, LANES, n_cam, pt_cols // LANES).transpose(2, 0, 3, 1)
+        parts = parts.reshape(n_cam, pt_rows * pt_cols // LANES, LANES)
         share = lax.psum_scatter(parts, "cam", scatter_dimension=0, tiled=False)
         return share.reshape(pt_rows, pt_cols)
 

time: 414 us -> 294 us (0.71)
  local copies, waits for them, and re-layouts: 157 us -> 15 us
  other arithmetic: 95.2 us -> 11.1 us
  waiting for transfers between devices: 0.07 us -> 67.2 us
  Pallas kernels: 0 us -> 36.1 us
    gather x4 -> x0, local copies, waits for them, and re-layouts: 102 us -> none  [residuals(): jnp.take(point_block, point_index, axis=1).reshape(3, tile_num, tile_len)]
    scatter-add x1 -> x0, other arithmetic: 72.7 us -> none  [residuals(): jnp.take(point_block, point_index, axis=1).reshape(3, tile_num, tile_len)]
    reduce_scatter x1, waiting for transfers between devices: 0.02 us -> 67.1 us  [scatter_cams(): return lax.psum_scatter(parts, 'pt', scatter_dimension=0, tiled=False)]
    pallas_call x0 -> x3, Pallas kernels: none -> 36.1 us  [the longest x2 23.8 us: gather_points(): pl.pallas_call(_gather_kernel, grid=(slots // blk,), in_specs=[pl.BlockSp...]
    transpose x2 -> x3, local copies, waits for them, and re-layouts: 16.3 us -> 1.33 us  [the longest x1 0.78 us: scatter_pts(): grad.reshape(pt_rows, LANES, n_cam, pt_cols // LANES).transpose(2, 0, 3, 1)]
    reshape x5 -> x3, local copies, waits for them, and re-layouts: 14.7 us -> 1.97 us  [the longest x2 1.81 us: gather_pts(): stacked.transpose(1, 3, 0, 2)]
    reduce_sum x2, other arithmetic: 12.8 us -> 2.15 us  [project(): inner = jnp.sum(axis_angle * point_obs, axis=0)]
    slice x2 -> x0, local copies, waits for them, and re-layouts: 8.62 us -> none  [the longest x1 8.34 us: project(): point_obs[1]]
  transfers between devices with their start and end apart: 2 -> 2, of which waited for: 0 -> 1; matrix products, arithmetic and copies ran while one was open for 22% -> 2% of each run, Pallas kernels for 0% -> 4%
where the time goes in v2:
time: 294 us; the launch traced here: 293 us
  blocking collectives  149 us (51%)
  waiting for transfers between devices  67.2 us (23%)
  Pallas kernels  36.1 us (12%)
  local copies, waits for them, and re-layouts  15 us (5%)
  between operations  14.6 us (5%)
  other arithmetic  11.1 us (4%)
    all_gather x2, blocking collectives, gather_cams(): stacked = lax.all_gather(local, 'pt', axis=0)  91.5 us
    reduce_scatter x1, waiting for transfers between devices, scatter_cams(): return lax.psum_scatter(parts, 'pt', scatter_dimension=0, tiled=False)  67.1 us
    all_gather x2, blocking collectives, gather_pts(): stacked = lax.all_gather(flat, 'cam', axis=0)  57.5 us
    pallas_call x2, Pallas kernels, gather_points(): pl.pallas_call(_gather_kernel, grid=(slots // blk,), in_specs=[pl.BlockSp...  23.8 us
    pallas_call x1, Pallas kernels, residuals(): take_points(point_block, point_index, point_block.shape[1])  12.3 us
  transfers between devices with their start and end apart: 2, of which 1 were waited for; matrix products, arithmetic and copies ran while one was open for 2% of the time, Pallas kernels for 4%

profile of v2, /device:TPU:6, one launch (start us, length us, event | category | flops | bytes accessed | tf_op | source)
XLA Modules:
  0.0 293.2 jit_solution(304823326155215760)
XLA Ops:
  8.5 48.5 %all-gather.2 = f32[32,9,128]{2,1,0:T(8,128)S(1)} all-gather(f32[1,9,128]{2,1,0:T(8,128)} %bitcast.284), channel_id=2, replica_groups=mesh['cam'=8,'pt'=32] {'pt'}, dimensions={0}, use_global_device_ids=true | all-gather | bytes 152064 | tf_op jit(solution)/shard_map/all_gather | solution.py:212
  58.4 28.7 %all_gather.20 = f32[8,96,128]{2,1,0:T(8,128)S(1)} all-gather(f32[1,96,128]{2,1,0:T(8,128)S(1)} %all_gather_reshape.6), channel_id=1, replica_groups=mesh['cam'=8,'pt'=32] {'cam'}, dimensions={0}, use_global_device_ids=true | all-gather | bytes 442368 | tf_op jit(solution)/shard_map/all_gather | solution.py:217
  87.5 0.9 copy.84.table_ref
  88.4 11.9 %jvp__.1 = f32[3,12288]{1,0:T(4,128)} custom-call(f32[384,256]{1,0:T(8,128)} %copy.84.table_ref, s32[1,12288]{1,0:T(1,128)} %bitcast.265), custom_call_target="tpu_custom_call" | custom-call | tf_op jit(solution)/shard_map/jvp()/pallas_call | solution.py:58
  100.3 1.9 slice_reduce_fusion.5
  102.5 1.1 multiply_reduce_fusion.1
  105.5 1.3 scatter_custom_fusion
  106.8 1.3 copy.95
  108.2 0.8 copy.105
  109.0 12.3 %transpose_jvp___.1 = f32[384,256]{1,0:T(8,128)} custom-call(f32[3,12288]{1,0:T(4,128)} %bitcast.264, s32[1,12288]{1,0:T(1,128)} %bitcast.266), custom_call_target="tpu_custom_call" | custom-call | tf_op jit(solution)/shard_map/transpose(jvp())/pallas_call | solution.py:203
  121.3 1.2 copy.96
  122.6 0.8 copy.97
  123.7 67.1 %reduce-scatter.3.cloned.1.call-done = f32[1,9,128]{2,1,0:T(8,128)} async-done(((f32[32,9,128]{2,1,0:T(8,128)}), f32[1,9,128]{2,1,0:T(8,128)}) %reduce-scatter.3.cloned.1.call-update) | async-done | bytes 4624 | tf_op jit(solution)/shard_map/reduce_scatter | solution.py:223
  190.9 1.3 divide_subtract_fusion.1
  192.2 43.1 %all-gather.3 = f32[32,9,128]{2,1,0:T(8,128)S(1)} all-gather(f32[1,9,128]{2,1,0:T(8,128)S(1)} %bitcast.285), channel_id=3, replica_groups=mesh['cam'=8,'pt'=32] {'pt'}, dimensions={0}, use_global_device_ids=true | all-gather | bytes 152064 | tf_op jit(solution)/shard_map/all_gather | solution.py:212
  237.2 0.8 reshape_reduce_scatter.3
  238.0 0.7 divide_subtract_fusion
  238.8 28.8 %all_gather.23 = f32[8,96,128]{2,1,0:T(8,128)S(1)} all-gather(f32[1,96,128]{2,1,0:T(8,128)S(1)} %all_gather_reshape.7), channel_id=1, replica_groups=mesh['cam'=8,'pt'=32] {'cam'}, dimensions={0}, use_global_device_ids=true | all-gather | bytes 442368 | tf_op jit(solution)/shard_map/all_gather | solution.py:217
  268.0 0.9 copy.101.table_ref
  268.9 11.9 %shard_map.161 = f32[3,12288]{1,0:T(4,128)} custom-call(f32[384,256]{1,0:T(8,128)} %copy.101.table_ref, s32[1,12288]{1,0:T(1,128)} %bitcast.267), custom_call_target="tpu_custom_call" | custom-call | tf_op jit(solution)/shard_map/pallas_call | solution.py:58
  280.8 1.5 slice_reduce_fusion.2
  282.4 1.1 multiply_reduce_fusion
  283.6 1.1 fusion.3
  284.9 0.8 maximum_multiply_fusion.2
  (103 shorter events, 8.9 us)
Async XLA Ops:
  7.2 51.2 %copy-start.1 = (f32[3,4096]{1,0:T(4,128)S(1)}, f32[3,4096]{1,0:T(4,128)}, u32[]{:S(2)}) copy-start(f32[3,4096]{1,0:T(4,128)} %param.13) | copy-start | bytes 147460
  7.2 183.7 %reduce-scatter.3.cloned.1.call-start = ((), (), s32[]{:S(2)}) async-start(), calls=%async_computation.2 | async-start | bytes 270336 | tf_op jit(solution)/shard_map/reduce_scatter | solution.py:223
  57.7 42.6 %copy-start.3 = (f32[2,12288]{1,0:T(2,128)S(1)}, f32[2,12288]{1,0:T(2,128)}, u32[]{:S(2)}) copy-start(f32[2,12288]{1,0:T(2,128)} %param.16) | copy-start | bytes 294916
  88.4 15.6 %copy-start.10 = (s32[48]{0:T(128)S(1)}, s32[48]{0:T(128)}, u32[]{:S(2)}) copy-start(s32[48]{0:T(128)} %param.19) | copy-start | bytes 580
  100.3 3.5 %copy-start = (f32[3,12288]{1,0:T(4,128)S(1)}, f32[3,12288]{1,0:T(4,128)}, u32[]{:S(2)}) copy-start(f32[3,12288]{1,0:T(4,128)} %jvp__.1) | copy-start | bytes 442372
  108.2 129.0 %reduce-scatter.5.cloned.1.call-start = ((), (), s32[]{:S(2)}) async-start(), calls=%async_computation.3 | async-start | bytes 442368 | tf_op jit(solution)/shard_map/reduce_scatter | solution.py:228
  109.0 81.9 %copy-start.6 = (f32[9,128]{1,0:T(8,128)S(1)}, f32[9,128]{1,0:T(8,128)}, u32[]{:S(2)}) copy-start(f32[9,128]{1,0:T(8,128)} %param.10) | copy-start | bytes 13828
  109.0 81.9 %copy-start.8 = (f32[9,128]{1,0:T(8,128)S(1)}, f32[9,128]{1,0:T(8,128)}, u32[]{:S(2)}) copy-start(f32[9,128]{1,0:T(8,128)} %param.11) | copy-start | bytes 13828
  109.0 81.9 %copy-start.9 = (f32[9,128]{1,0:T(8,128)S(1)}, f32[9,128]{1,0:T(8,128)}, u32[]{:S(2)}) copy-start(f32[9,128]{1,0:T(8,128)} %param.12) | copy-start | bytes 13828
  123.5 114.5 %copy-start.4 = (f32[3,4096]{1,0:T(4,128)S(1)}, f32[3,4096]{1,0:T(4,128)}, u32[]{:S(2)}) copy-start(f32[3,4096]{1,0:T(4,128)} %param.14) | copy-start | bytes 147460
  123.5 114.5 %copy-start.5 = (f32[3,4096]{1,0:T(4,128)S(1)}, f32[3,4096]{1,0:T(4,128)}, u32[]{:S(2)}) copy-start(f32[3,4096]{1,0:T(4,128)} %param.15) | copy-start | bytes 147460
  192.2 46.6 %copy-start.7 = (f32[9,128]{1,0:T(8,128)}, f32[9,128]{1,0:T(8,128)S(1)}, u32[]{:S(2)}) copy-start(f32[9,128]{1,0:T(8,128)S(1)} %get-tuple-element.39) | copy-start | bytes 13828
  238.7 43.6 %copy-start.2 = (f32[3,4096]{1,0:T(4,128)}, f32[3,4096]{1,0:T(4,128)S(1)}, u32[]{:S(2)}) copy-start(f32[3,4096]{1,0:T(4,128)S(1)} %get-tuple-element.36) | copy-start | bytes 147460
Sparse Core Ops, SparseCore 0:
  108.3 82.5 reduce-scatter.2
  193.4 36.0 reduce-scatter.4

commit v3 on v2

--- a/solution.py
+++ b/solution.py
@@ -208,24 +208,55 @@
     n_pt = lax.axis_size("pt")
     n_cam = lax.axis_size("cam")
 
+    def doubling_gather(local, axis_name, size):
+        me = lax.axis_index(axis_name)
+        buf = local[None]
+        dist = 1
+        while dist < size:
+            pairs = [(i, i ^ dist) for i in range(size)]
+            other = lax.ppermute(buf, axis_name, pairs)
+            low_half = (me // dist) % 2 == 0
+            buf = jnp.where(
+                low_half,
+                jnp.concatenate([buf, other], axis=0),
+                jnp.concatenate([other, buf], axis=0),
+            )
+            dist *= 2
+        return buf
+
+    def halving_scatter(parts, axis_name, size):
+        me = lax.axis_index(axis_name)
+        buf = parts
+        dist = size // 2
+        while dist >= 1:
+            pairs = [(i, i ^ dist) for i in range(size)]
+            low_half = (me // dist) % 2 == 0
+            half = buf.shape[0] // 2
+            first, second = buf[:half], buf[half:]
+            keep = jnp.where(low_half, first, second)
+            send = jnp.where(low_half, second, first)
+            buf = keep + lax.ppermute(send, axis_name, pairs)
+            dist //= 2
+        return buf[0]
+
     def gather_cams(local):
-        stacked = lax.all_gather(local, "pt", axis=0)
+        stacked = doubling_gather(local, "pt", n_pt)
         return stacked.transpose(1, 0, 2).reshape(cam_rows, n_pt * cam_cols)
 
     def gather_pts(local):
         flat = local.reshape(pt_rows * pt_cols // LANES, LANES)
-        stacked = lax.all_gather(flat, "cam", axis=0)
+        stacked = doubling_gather(flat, "cam", n_cam)
         stacked = stacked.reshape(n_cam, pt_rows, pt_cols // LANES, LANES)
         return stacked.transpose(1, 3, 0, 2).reshape(pt_rows * LANES, n_cam * pt_cols // LANES)
 
     def scatter_cams(grad):
         parts = grad.reshape(cam_rows, n_pt, cam_cols).transpose(1, 0, 2)
-        return lax.psum_scatter(parts, "pt", scatter_dimension=0, tiled=False)
+        return halving_scatter(parts, "pt", n_pt)
 
     def scatter_pts(grad):
         parts = grad.reshape(pt_rows, LANES, n_cam, pt_cols // LANES).transpose(2, 0, 3, 1)
         parts = parts.reshape(n_cam, pt_rows * pt_cols // LANES, LANES)
-        share = lax.psum_scatter(parts, "cam", scatter_dimension=0, tiled=False)
+        share = halving_scatter(parts, "cam", n_cam)
         return share.reshape(pt_rows, pt_cols)
 
     camera_block = gather_cams(cameras)

time: 294 us -> 166 us (0.56)
  blocking collectives: 149 us -> 0 us
  starting transfers between devices: 0.08 us -> 52.4 us
  waiting for transfers between devices: 67.2 us -> 49.3 us
  between operations: 14.6 us -> 1.42 us
    all_gather x4 -> x0, blocking collectives: 149 us -> none  [the longest x2 91.5 us: gather_cams(): stacked = lax.all_gather(local, 'pt', axis=0)]
    reduce_scatter x2 -> x0, waiting for transfers between devices: 67.2 us -> none  [the longest x1 67.1 us: scatter_cams(): return lax.psum_scatter(parts, 'pt', scatter_dimension=0, tiled=False)]
    ppermute x0 -> x24, starting transfers between devices: none -> 52.4 us  [the longest x16 34.8 us: doubling_gather(): other = lax.ppermute(buf, axis_name, pairs)]
    ppermute x0 -> x24, waiting for transfers between devices: none -> 49.3 us  [the longest x16 32.7 us: doubling_gather(): other = lax.ppermute(buf, axis_name, pairs)]
  transfers between devices with their start and end apart: 2 -> 24, of which waited for: 1 -> 19; matrix products, arithmetic and copies ran while one was open for 2% -> 6% of each run, Pallas kernels for 4% -> 7%
where the time goes in v3:
time: 166 us; the launch traced here: 165 us
  starting transfers between devices  52.4 us (32%)
  waiting for transfers between devices  49.3 us (30%)
  Pallas kernels  36.1 us (22%)
  local copies, waits for them, and re-layouts  14.4 us (9%)
  other arithmetic  11.8 us (7%)
    ppermute x16, starting transfers between devices, doubling_gather(): other = lax.ppermute(buf, axis_name, pairs)  34.8 us
    ppermute x16, waiting for transfers between devices, doubling_gather(): other = lax.ppermute(buf, axis_name, pairs)  32.7 us
    pallas_call x2, Pallas kernels, gather_points(): pl.pallas_call(_gather_kernel, grid=(slots // blk,), in_specs=[pl.BlockSp...  23.8 us
    ppermute x8, starting transfers between devices, halving_scatter(): buf = keep + lax.ppermute(send, axis_name, pairs)  17.6 us
    ppermute x8, waiting for transfers between devices, halving_scatter(): buf = keep + lax.ppermute(send, axis_name, pairs)  16.7 us
    pallas_call x1, Pallas kernels, residuals(): take_points(point_block, point_index, point_block.shape[1])  12.2 us
    slice x2, local copies, waits for them, and re-layouts, project(): point_obs[2]  3.41 us
  transfers between devices with their start and end apart: 24, of which 19 were waited for; matrix products, arithmetic and copies ran while one was open for 6% of the time, Pallas kernels for 7%

profile of v3, /device:TPU:6, one launch (start us, length us, event | category | flops | bytes accessed | tf_op | source)
XLA Modules:
  0.0 165.4 jit_solution(18445792808814426117)
XLA Ops:
  4.0 3.3 %collective-permute-start.1 = (f32[2,9,128]{2,1,0:T(8,128)S(1)}, f32[2,9,128]{2,1,0:T(8,128)S(1)}, u32[]{:S(2)}, u32[]{:S(2)}) collective-permute-start(f32[2,9,128]{2,1,0:T(8,128)S(1)} %maximum_select_fusion.18), channel_id=1, source_target_pairs={{0,2},{1,3},{2,0},{3,1},{4,6},{5,7},{6,4},{7,5},{8,10},{9,11},{10,... | collective-permute-start | bytes 27656 | tf_op jit(solution)/shard_map/ppermute | solution.py:217
  9.0 6.8 %collective-permute-start.2 = (f32[4,9,128]{2,1,0:T(8,128)S(1)}, f32[4,9,128]{2,1,0:T(8,128)S(1)}, u32[]{:S(2)}, u32[]{:S(2)}) collective-permute-start(f32[4,9,128]{2,1,0:T(8,128)S(1)} %maximum_select_fusion.16), channel_id=1, source_target_pairs={{0,4},{1,5},{2,6},{3,7},{4,0},{5,1},{6,2},{7,3},{8,12},{9,13},{10,... | collective-permute-start | bytes 55304 | tf_op jit(solution)/shard_map/ppermute | solution.py:217
  22.1 3.3 %collective-permute-start.4 = (f32[16,9,128]{2,1,0:T(8,128)S(1)}, f32[16,9,128]{2,1,0:T(8,128)S(1)}, u32[]{:S(2)}, u32[]{:S(2)}) collective-permute-start(f32[16,9,128]{2,1,0:T(8,128)S(1)} %maximum_select_fusion.8), channel_id=1, source_target_pairs={{0,16},{1,17},{2,18},{3,19},{4,20},{5,21},{6,22},{7,23},{8,24},{9,... | collective-permute-start | bytes 221192 | tf_op jit(solution)/shard_map/ppermute | solution.py:217
  25.4 3.3 %collective-permute-done.4 = f32[16,9,128]{2,1,0:T(8,128)S(1)} collective-permute-done((f32[16,9,128]{2,1,0:T(8,128)S(1)}, f32[16,9,128]{2,1,0:T(8,128)S(1)}, u32[]{:S(2)}, u32[]{:S(2)}) %collective-permute-start.4) | collective-permute-done | bytes 73760 | tf_op jit(solution)/shard_map/ppermute | solution.py:217
  31.4 4.5 %collective-permute-done.7 = f32[4,96,128]{2,1,0:T(8,128)S(1)} collective-permute-done((f32[4,96,128]{2,1,0:T(8,128)S(1)}, f32[4,96,128]{2,1,0:T(8,128)S(1)}, u32[]{:S(2)}, u32[]{:S(2)}) %collective-permute-start.7) | collective-permute-done | bytes 196640 | tf_op jit(solution)/shard_map/ppermute | solution.py:217
  37.2 11.9 %jvp__.1 = f32[3,12288]{1,0:T(4,128)} custom-call(f32[384,256]{1,0:T(8,128)} %copy.90.table_ref, s32[1,12288]{1,0:T(1,128)} %bitcast.281), custom_call_target="tpu_custom_call" | custom-call | tf_op jit(solution)/shard_map/jvp()/pallas_call | solution.py:58
  56.1 3.3 %collective-permute-start.8 = (f32[16,9,128]{2,1,0:T(8,128)S(1)}, f32[16,9,128]{2,1,0:T(8,128)S(1)}, u32[]{:S(2)}, u32[]{:S(2)}) collective-permute-start(f32[16,9,128]{2,1,0:T(8,128)S(1)} %slice_select_fusion.2), channel_id=1, source_target_pairs={{0,16},{1,17},{2,18},{3,19},{4,20},{5,21},{6,22},{7,23},{8,24},{9,... | collective-permute-start | bytes 221192 | tf_op jit(solution)/shard_map/ppermute | solution.py:238
  59.4 4.0 %collective-permute-done.8 = f32[16,9,128]{2,1,0:T(8,128)S(1)} collective-permute-done((f32[16,9,128]{2,1,0:T(8,128)S(1)}, f32[16,9,128]{2,1,0:T(8,128)S(1)}, u32[]{:S(2)}, u32[]{:S(2)}) %collective-permute-start.8) | collective-permute-done | bytes 73760 | tf_op jit(solution)/shard_map/ppermute | solution.py:238
  64.4 3.4 %collective-permute-done.9 = f32[8,9,128]{2,1,0:T(8,128)S(1)} collective-permute-done((f32[8,9,128]{2,1,0:T(8,128)S(1)}, f32[8,9,128]{2,1,0:T(8,128)S(1)}, u32[]{:S(2)}, u32[]{:S(2)}) %collective-permute-start.9) | collective-permute-done | bytes 36896 | tf_op jit(solution)/shard_map/ppermute | solution.py:238
  67.8 6.0 %collective-permute-start.10 = (f32[4,9,128]{2,1,0:T(8,128)S(1)}, f32[4,9,128]{2,1,0:T(8,128)S(1)}, u32[]{:S(2)}, u32[]{:S(2)}) collective-permute-start(f32[4,9,128]{2,1,0:T(8,128)S(1)} %slice_select_fusion.6), channel_id=1, source_target_pairs={{0,4},{1,5},{2,6},{3,7},{4,0},{5,1},{6,2},{7,3},{8,12},{9,13},{10,... | collective-permute-start | bytes 55304 | tf_op jit(solution)/shard_map/ppermute | solution.py:238
  75.8 2.3 %collective-permute-start.11 = (f32[2,9,128]{2,1,0:T(8,128)S(1)}, f32[2,9,128]{2,1,0:T(8,128)S(1)}, u32[]{:S(2)}, u32[]{:S(2)}) collective-permute-start(f32[2,9,128]{2,1,0:T(8,128)S(1)} %slice_select_fusion.7), channel_id=1, source_target_pairs={{0,2},{1,3},{2,0},{3,1},{4,6},{5,7},{6,4},{7,5},{8,10},{9,11},{10,... | collective-permute-start | bytes 27656 | tf_op jit(solution)/shard_map/ppermute | solution.py:238
  78.0 2.6 %collective-permute-done.11 = f32[2,9,128]{2,1,0:T(8,128)S(1)} collective-permute-done((f32[2,9,128]{2,1,0:T(8,128)S(1)}, f32[2,9,128]{2,1,0:T(8,128)S(1)}, u32[]{:S(2)}, u32[]{:S(2)}) %collective-permute-start.11) | collective-permute-done | bytes 9248 | tf_op jit(solution)/shard_map/ppermute | solution.py:238
  83.6 12.2 %transpose_jvp___.1 = f32[384,256]{1,0:T(8,128)} custom-call(f32[3,12288]{1,0:T(4,128)} %bitcast.278, s32[1,12288]{1,0:T(1,128)} %bitcast.282), custom_call_target="tpu_custom_call" | custom-call | tf_op jit(solution)/shard_map/transpose(jvp())/pallas_call | solution.py:203
  97.2 2.1 %collective-permute-start.17 = (f32[2,9,128]{2,1,0:T(8,128)S(1)}, f32[2,9,128]{2,1,0:T(8,128)S(1)}, u32[]{:S(2)}, u32[]{:S(2)}) collective-permute-start(f32[2,9,128]{2,1,0:T(8,128)S(1)} %maximum_select_fusion.19), channel_id=1, source_target_pairs={{0,2},{1,3},{2,0},{3,1},{4,6},{5,7},{6,4},{7,5},{8,10},{9,11},{10,... | collective-permute-start | bytes 27656 | tf_op jit(solution)/shard_map/ppermute | solution.py:217
  102.1 5.8 %collective-permute-start.18 = (f32[4,9,128]{2,1,0:T(8,128)S(1)}, f32[4,9,128]{2,1,0:T(8,128)S(1)}, u32[]{:S(2)}, u32[]{:S(2)}) collective-permute-start(f32[4,9,128]{2,1,0:T(8,128)S(1)} %maximum_select_fusion.17), channel_id=1, source_target_pairs={{0,4},{1,5},{2,6},{3,7},{4,0},{5,1},{6,2},{7,3},{8,12},{9,13},{10,... | collective-permute-start | bytes 55304 | tf_op jit(solution)/shard_map/ppermute | solution.py:217
  108.1 3.4 %collective-permute-done.18 = f32[4,9,128]{2,1,0:T(8,128)S(1)} collective-permute-done((f32[4,9,128]{2,1,0:T(8,128)S(1)}, f32[4,9,128]{2,1,0:T(8,128)S(1)}, u32[]{:S(2)}, u32[]{:S(2)}) %collective-permute-start.18) | collective-permute-done | bytes 18464 | tf_op jit(solution)/shard_map/ppermute | solution.py:217
  112.5 3.4 %collective-permute-done.19 = f32[8,9,128]{2,1,0:T(8,128)S(1)} collective-permute-done((f32[8,9,128]{2,1,0:T(8,128)S(1)}, f32[8,9,128]{2,1,0:T(8,128)S(1)}, u32[]{:S(2)}, u32[]{:S(2)}) %collective-permute-start.19) | collective-permute-done | bytes 36896 | tf_op jit(solution)/shard_map/ppermute | solution.py:217
  115.9 2.6 %collective-permute-start.20 = (f32[16,9,128]{2,1,0:T(8,128)S(1)}, f32[16,9,128]{2,1,0:T(8,128)S(1)}, u32[]{:S(2)}, u32[]{:S(2)}) collective-permute-start(f32[16,9,128]{2,1,0:T(8,128)S(1)} %maximum_select_fusion.9), channel_id=1, source_target_pairs={{0,16},{1,17},{2,18},{3,19},{4,20},{5,21},{6,22},{7,23},{8,24},{9,... | collective-permute-start | bytes 221192 | tf_op jit(solution)/shard_map/ppermute | solution.py:217
  119.8 2.6 %collective-permute-done.20 = f32[16,9,128]{2,1,0:T(8,128)S(1)} collective-permute-done((f32[16,9,128]{2,1,0:T(8,128)S(1)}, f32[16,9,128]{2,1,0:T(8,128)S(1)}, u32[]{:S(2)}, u32[]{:S(2)}) %collective-permute-start.20) | collective-permute-done | bytes 73760 | tf_op jit(solution)/shard_map/ppermute | solution.py:217
  126.6 2.9 %collective-permute-done.15 = f32[1,96,128]{2,1,0:T(8,128)S(1)} collective-permute-done((f32[1,96,128]{2,1,0:T(8,128)S(1)}, f32[1,96,128]{2,1,0:T(8,128)S(1)}, u32[]{:S(2)}, u32[]{:S(2)}) %collective-permute-start.15) | collective-permute-done | bytes 49184 | tf_op jit(solution)/shard_map/ppermute | solution.py:238
  131.6 2.8 %collective-permute-done.21 = f32[1,96,128]{2,1,0:T(8,128)S(1)} collective-permute-done((f32[1,96,128]{2,1,0:T(8,128)S(1)}, f32[1,96,128]{2,1,0:T(8,128)S(1)}, u32[]{:S(2)}, u32[]{:S(2)}) %collective-permute-start.21) | collective-permute-done | bytes 49184 | tf_op jit(solution)/shard_map/ppermute | solution.py:217
  136.4 4.3 %collective-permute-done.22 = f32[2,96,128]{2,1,0:T(8,128)S(1)} collective-permute-done((f32[2,96,128]{2,1,0:T(8,128)S(1)}, f32[2,96,128]{2,1,0:T(8,128)S(1)}, u32[]{:S(2)}, u32[]{:S(2)}) %collective-permute-start.22) | collective-permute-done | bytes 98336 | tf_op jit(solution)/shard_map/ppermute | solution.py:217
  142.5 4.2 %collective-permute-done.23 = f32[4,96,128]{2,1,0:T(8,128)S(1)} collective-permute-done((f32[4,96,128]{2,1,0:T(8,128)S(1)}, f32[4,96,128]{2,1,0:T(8,128)S(1)}, u32[]{:S(2)}, u32[]{:S(2)}) %collective-permute-start.23) | collective-permute-done | bytes 196640 | tf_op jit(solution)/shard_map/ppermute | solution.py:217
  148.0 11.9 %shard_map.161 = f32[3,12288]{1,0:T(4,128)} custom-call(f32[384,256]{1,0:T(8,128)} %copy.108.table_ref, s32[1,12288]{1,0:T(1,128)} %bitcast.283), custom_call_target="tpu_custom_call" | custom-call | tf_op jit(solution)/shard_map/pallas_call | solution.py:58
  (179 shorter events, 51.2 us)
Async XLA Ops:
  0.6 2.6 %collective-permute-start = (f32[1,9,128]{2,1,0:T(8,128)}, f32[1,9,128]{2,1,0:T(8,128)S(1)}, u32[]{:S(2)}, u32[]{:S(2)}) collective-permute-start(f32[1,9,128]{2,1,0:T(8,128)} %bitcast.307), channel_id=1, source_target_pairs={{0,1},{1,0},{2,3},{3,2},{4,5},{5,4},{6,7},{7,6},{8,9},{9,8},{10,11... | collective-permute-start | bytes 13832 | tf_op jit(solution)/shard_map/ppermute | solution.py:217
  1.6 17.8 %collective-permute-start.5 = (f32[1,96,128]{2,1,0:T(8,128)S(1)}, f32[1,96,128]{2,1,0:T(8,128)S(1)}, u32[]{:S(2)}, u32[]{:S(2)}) collective-permute-start(f32[1,96,128]{2,1,0:T(8,128)S(1)} %broadcast_in_dim_reshape.6), channel_id=1, source_target_pairs={{0,32},{32,0},{64,96},{96,64},{128,160},{160,128},{192,224},{224,1... | collective-permute-start | bytes 147464 | tf_op jit(solution)/shard_map/ppermute | solution.py:217
  4.0 5.0 %collective-permute-start.1 = (f32[2,9,128]{2,1,0:T(8,128)S(1)}, f32[2,9,128]{2,1,0:T(8,128)S(1)}, u32[]{:S(2)}, u32[]{:S(2)}) collective-permute-start(f32[2,9,128]{2,1,0:T(8,128)S(1)} %maximum_select_fusion.18), channel_id=1, source_target_pairs={{0,2},{1,3},{2,0},{3,1},{4,6},{5,7},{6,4},{7,5},{8,10},{9,11},{10,... | collective-permute-start | bytes 27656 | tf_op jit(solution)/shard_map/ppermute | solution.py:217
  9.0 8.7 %collective-permute-start.2 = (f32[4,9,128]{2,1,0:T(8,128)S(1)}, f32[4,9,128]{2,1,0:T(8,128)S(1)}, u32[]{:S(2)}, u32[]{:S(2)}) collective-permute-start(f32[4,9,128]{2,1,0:T(8,128)S(1)} %maximum_select_fusion.16), channel_id=1, source_target_pairs={{0,4},{1,5},{2,6},{3,7},{4,0},{5,1},{6,2},{7,3},{8,12},{9,13},{10,... | collective-permute-start | bytes 55304 | tf_op jit(solution)/shard_map/ppermute | solution.py:217
  17.7 4.4 %collective-permute-start.3 = (f32[8,9,128]{2,1,0:T(8,128)S(1)}, f32[8,9,128]{2,1,0:T(8,128)S(1)}, u32[]{:S(2)}, u32[]{:S(2)}) collective-permute-start(f32[8,9,128]{2,1,0:T(8,128)S(1)} %maximum_select_fusion.14), channel_id=1, source_target_pairs={{0,8},{1,9},{2,10},{3,11},{4,12},{5,13},{6,14},{7,15},{8,0},{9,1},... | collective-permute-start | bytes 110600 | tf_op jit(solution)/shard_map/ppermute | solution.py:217
  19.4 10.7 %collective-permute-start.6 = (f32[2,96,128]{2,1,0:T(8,128)S(1)}, f32[2,96,128]{2,1,0:T(8,128)S(1)}, u32[]{:S(2)}, u32[]{:S(2)}) collective-permute-start(f32[2,96,128]{2,1,0:T(8,128)S(1)} %maximum_select_fusion.11), channel_id=1, source_target_pairs={{0,64},{32,96},{64,0},{96,32},{128,192},{160,224},{192,128},{224,1... | collective-permute-start | bytes 294920 | tf_op jit(solution)/shard_map/ppermute | solution.py:217
  22.1 6.6 %collective-permute-start.4 = (f32[16,9,128]{2,1,0:T(8,128)S(1)}, f32[16,9,128]{2,1,0:T(8,128)S(1)}, u32[]{:S(2)}, u32[]{:S(2)}) collective-permute-start(f32[16,9,128]{2,1,0:T(8,128)S(1)} %maximum_select_fusion.8), channel_id=1, source_target_pairs={{0,16},{1,17},{2,18},{3,19},{4,20},{5,21},{6,22},{7,23},{8,24},{9,... | collective-permute-start | bytes 221192 | tf_op jit(solution)/shard_map/ppermute | solution.py:217
  30.2 5.8 %collective-permute-start.7 = (f32[4,96,128]{2,1,0:T(8,128)S(1)}, f32[4,96,128]{2,1,0:T(8,128)S(1)}, u32[]{:S(2)}, u32[]{:S(2)}) collective-permute-start(f32[4,96,128]{2,1,0:T(8,128)S(1)} %maximum_select_fusion.5), channel_id=1, source_target_pairs={{0,128},{32,160},{64,192},{96,224},{128,0},{160,32},{192,64},{224,... | collective-permute-start | bytes 589832 | tf_op jit(solution)/shard_map/ppermute | solution.py:217
  56.1 7.3 %collective-permute-start.8 = (f32[16,9,128]{2,1,0:T(8,128)S(1)}, f32[16,9,128]{2,1,0:T(8,128)S(1)}, u32[]{:S(2)}, u32[]{:S(2)}) collective-permute-start(f32[16,9,128]{2,1,0:T(8,128)S(1)} %slice_select_fusion.2), channel_id=1, source_target_pairs={{0,16},{1,17},{2,18},{3,19},{4,20},{5,21},{6,22},{7,23},{8,24},{9,... | collective-permute-start | bytes 221192 | tf_op jit(solution)/shard_map/ppermute | solution.py:238
  63.4 4.4 %collective-permute-start.9 = (f32[8,9,128]{2,1,0:T(8,128)S(1)}, f32[8,9,128]{2,1,0:T(8,128)S(1)}, u32[]{:S(2)}, u32[]{:S(2)}) collective-permute-start(f32[8,9,128]{2,1,0:T(8,128)S(1)} %slice_select_fusion.4), channel_id=1, source_target_pairs={{0,8},{1,9},{2,10},{3,11},{4,12},{5,13},{6,14},{7,15},{8,0},{9,1},... | collective-permute-start | bytes 110600 | tf_op jit(solution)/shard_map/ppermute | solution.py:238
  67.8 7.9 %collective-permute-start.10 = (f32[4,9,128]{2,1,0:T(8,128)S(1)}, f32[4,9,128]{2,1,0:T(8,128)S(1)}, u32[]{:S(2)}, u32[]{:S(2)}) collective-permute-start(f32[4,9,128]{2,1,0:T(8,128)S(1)} %slice_select_fusion.6), channel_id=1, source_target_pairs={{0,4},{1,5},{2,6},{3,7},{4,0},{5,1},{6,2},{7,3},{8,12},{9,13},{10,... | collective-permute-start | bytes 55304 | tf_op jit(solution)/shard_map/ppermute | solution.py:238
  75.8 4.9 %collective-permute-start.11 = (f32[2,9,128]{2,1,0:T(8,128)S(1)}, f32[2,9,128]{2,1,0:T(8,128)S(1)}, u32[]{:S(2)}, u32[]{:S(2)}) collective-permute-start(f32[2,9,128]{2,1,0:T(8,128)S(1)} %slice_select_fusion.7), channel_id=1, source_target_pairs={{0,2},{1,3},{2,0},{3,1},{4,6},{5,7},{6,4},{7,5},{8,10},{9,11},{10,... | collective-permute-start | bytes 27656 | tf_op jit(solution)/shard_map/ppermute | solution.py:238
  80.7 1.3 collective-permute-start.12
  82.6 14.6 %collective-permute-start.16 = (f32[1,9,128]{2,1,0:T(8,128)S(1)}, f32[1,9,128]{2,1,0:T(8,128)S(1)}, u32[]{:S(2)}, u32[]{:S(2)}) collective-permute-start(f32[1,9,128]{2,1,0:T(8,128)S(1)} %bitcast.309), channel_id=1, source_target_pairs={{0,1},{1,0},{2,3},{3,2},{4,5},{5,4},{6,7},{7,6},{8,9},{9,8},{10,11... | collective-permute-start | bytes 13832 | tf_op jit(solution)/shard_map/ppermute | solution.py:217
  97.2 4.9 %collective-permute-start.17 = (f32[2,9,128]{2,1,0:T(8,128)S(1)}, f32[2,9,128]{2,1,0:T(8,128)S(1)}, u32[]{:S(2)}, u32[]{:S(2)}) collective-permute-start(f32[2,9,128]{2,1,0:T(8,128)S(1)} %maximum_select_fusion.19), channel_id=1, source_target_pairs={{0,2},{1,3},{2,0},{3,1},{4,6},{5,7},{6,4},{7,5},{8,10},{9,11},{10,... | collective-permute-start | bytes 27656 | tf_op jit(solution)/shard_map/ppermute | solution.py:217
  99.4 13.0 %collective-permute-start.13 = (f32[4,96,128]{2,1,0:T(8,128)S(1)}, f32[4,96,128]{2,1,0:T(8,128)S(1)}, u32[]{:S(2)}, u32[]{:S(2)}) collective-permute-start(f32[4,96,128]{2,1,0:T(8,128)S(1)} %bitcast.288), channel_id=1, source_target_pairs={{0,128},{32,160},{64,192},{96,224},{128,0},{160,32},{192,64},{224,... | collective-permute-start | bytes 589832 | tf_op jit(solution)/shard_map/ppermute | solution.py:238
  102.1 9.3 %collective-permute-start.18 = (f32[4,9,128]{2,1,0:T(8,128)S(1)}, f32[4,9,128]{2,1,0:T(8,128)S(1)}, u32[]{:S(2)}, u32[]{:S(2)}) collective-permute-start(f32[4,9,128]{2,1,0:T(8,128)S(1)} %maximum_select_fusion.17), channel_id=1, source_target_pairs={{0,4},{1,5},{2,6},{3,7},{4,0},{5,1},{6,2},{7,3},{8,12},{9,13},{10,... | collective-permute-start | bytes 55304 | tf_op jit(solution)/shard_map/ppermute | solution.py:217
  111.5 4.4 %collective-permute-start.19 = (f32[8,9,128]{2,1,0:T(8,128)S(1)}, f32[8,9,128]{2,1,0:T(8,128)S(1)}, u32[]{:S(2)}, u32[]{:S(2)}) collective-permute-start(f32[8,9,128]{2,1,0:T(8,128)S(1)} %maximum_select_fusion.15), channel_id=1, source_target_pairs={{0,8},{1,9},{2,10},{3,11},{4,12},{5,13},{6,14},{7,15},{8,0},{9,1},... | collective-permute-start | bytes 110600 | tf_op jit(solution)/shard_map/ppermute | solution.py:217
  115.9 6.6 %collective-permute-start.20 = (f32[16,9,128]{2,1,0:T(8,128)S(1)}, f32[16,9,128]{2,1,0:T(8,128)S(1)}, u32[]{:S(2)}, u32[]{:S(2)}) collective-permute-start(f32[16,9,128]{2,1,0:T(8,128)S(1)} %maximum_select_fusion.9), channel_id=1, source_target_pairs={{0,16},{1,17},{2,18},{3,19},{4,20},{5,21},{6,22},{7,23},{8,24},{9,... | collective-permute-start | bytes 221192 | tf_op jit(solution)/shard_map/ppermute | solution.py:217
  118.5 6.2 %collective-permute-start.14 = (f32[2,96,128]{2,1,0:T(8,128)S(1)}, f32[2,96,128]{2,1,0:T(8,128)S(1)}, u32[]{:S(2)}, u32[]{:S(2)}) collective-permute-start(f32[2,96,128]{2,1,0:T(8,128)S(1)} %slice_select_fusion.3), channel_id=1, source_target_pairs={{0,64},{32,96},{64,0},{96,32},{128,192},{160,224},{192,128},{224,1... | collective-permute-start | bytes 294920 | tf_op jit(solution)/shard_map/ppermute | solution.py:238
  124.8 4.6 %collective-permute-start.15 = (f32[1,96,128]{2,1,0:T(8,128)S(1)}, f32[1,96,128]{2,1,0:T(8,128)S(1)}, u32[]{:S(2)}, u32[]{:S(2)}) collective-permute-start(f32[1,96,128]{2,1,0:T(8,128)S(1)} %slice_select_fusion.5), channel_id=1, source_target_pairs={{0,32},{32,0},{64,96},{96,64},{128,160},{160,128},{192,224},{224,1... | collective-permute-start | bytes 147464 | tf_op jit(solution)/shard_map/ppermute | solution.py:238
  130.3 4.2 %collective-permute-start.21 = (f32[1,96,128]{2,1,0:T(8,128)S(1)}, f32[1,96,128]{2,1,0:T(8,128)S(1)}, u32[]{:S(2)}, u32[]{:S(2)}) collective-permute-start(f32[1,96,128]{2,1,0:T(8,128)S(1)} %broadcast_in_dim_reshape.7), channel_id=1, source_target_pairs={{0,32},{32,0},{64,96},{96,64},{128,160},{160,128},{192,224},{224,1... | collective-permute-start | bytes 147464 | tf_op jit(solution)/shard_map/ppermute | solution.py:217
  134.5 6.2 %collective-permute-start.22 = (f32[2,96,128]{2,1,0:T(8,128)S(1)}, f32[2,96,128]{2,1,0:T(8,128)S(1)}, u32[]{:S(2)}, u32[]{:S(2)}) collective-permute-start(f32[2,96,128]{2,1,0:T(8,128)S(1)} %maximum_select_fusion.13), channel_id=1, source_target_pairs={{0,64},{32,96},{64,0},{96,32},{128,192},{160,224},{192,128},{224,1... | collective-permute-start | bytes 294920 | tf_op jit(solution)/shard_map/ppermute | solution.py:217
  140.7 6.0 %collective-permute-start.23 = (f32[4,96,128]{2,1,0:T(8,128)S(1)}, f32[4,96,128]{2,1,0:T(8,128)S(1)}, u32[]{:S(2)}, u32[]{:S(2)}) collective-permute-start(f32[4,96,128]{2,1,0:T(8,128)S(1)} %maximum_select_fusion.7), channel_id=1, source_target_pairs={{0,128},{32,160},{64,192},{96,224},{128,0},{160,32},{192,64},{224,... | collective-permute-start | bytes 589832 | tf_op jit(solution)/shard_map/ppermute | solution.py:217
  (11 other events, 179.9 us)

commit v4 on v3

--- a/solution.py
+++ b/solution.py
@@ -224,24 +224,13 @@
             dist *= 2
         return buf
 
-    def halving_scatter(parts, axis_name, size):
-        me = lax.axis_index(axis_name)
-        buf = parts
-        dist = size // 2
-        while dist >= 1:
+    def butterfly_sum(value, axis_name, size):
+        dist = 1
+        while dist < size:
             pairs = [(i, i ^ dist) for i in range(size)]
-            low_half = (me // dist) % 2 == 0
-            half = buf.shape[0] // 2
-            first, second = buf[:half], buf[half:]
-            keep = jnp.where(low_half, first, second)
-            send = jnp.where(low_half, second, first)
-            buf = keep + lax.ppermute(send, axis_name, pairs)
-            dist //= 2
-        return buf[0]
-
-    def gather_cams(local):
-        stacked = doubling_gather(local, "pt", n_pt)
-        return stacked.transpose(1, 0, 2).reshape(cam_rows, n_pt * cam_cols)
+            value = value + lax.ppermute(value, axis_name, pairs)
+            dist *= 2
+        return value
 
     def gather_pts(local):
         flat = local.reshape(pt_rows * pt_cols // LANES, LANES)
@@ -249,29 +238,39 @@
         stacked = stacked.reshape(n_cam, pt_rows, pt_cols // LANES, LANES)
         return stacked.transpose(1, 3, 0, 2).reshape(pt_rows * LANES, n_cam * pt_cols // LANES)
 
-    def scatter_cams(grad):
-        parts = grad.reshape(cam_rows, n_pt, cam_cols).transpose(1, 0, 2)
-        return halving_scatter(parts, "pt", n_pt)
-
-    def scatter_pts(grad):
-        parts = grad.reshape(pt_rows, LANES, n_cam, pt_cols // LANES).transpose(2, 0, 3, 1)
-        parts = parts.reshape(n_cam, pt_rows * pt_cols // LANES, LANES)
-        share = halving_scatter(parts, "cam", n_cam)
-        return share.reshape(pt_rows, pt_cols)
-
-    camera_block = gather_cams(cameras)
+    def own_pts(table):
+        parts = table.reshape(pt_rows, LANES, n_cam, pt_cols // LANES)
+        mine = lax.dynamic_index_in_dim(parts, lax.axis_index("cam"), axis=2, keepdims=False)
+        return mine.transpose(0, 2, 1).reshape(pt_rows, pt_cols)
+
+    def own_cams(block):
+        start = lax.axis_index("pt") * cam_cols
+        return lax.dynamic_slice_in_dim(block, start, cam_cols, axis=1)
+
+    cam_state = jnp.concatenate([cameras, cam_first, cam_second], axis=0)
+    cam_state = doubling_gather(cam_state, "pt", n_pt)
+    cam_state = cam_state.transpose(1, 0, 2).reshape(3, cam_rows, n_pt * cam_cols)
+    camera_block, first_block, second_block = cam_state[0], cam_state[1], cam_state[2]
     point_block = gather_pts(points)
     residual, pullback = jax.vjp(residuals, camera_block, point_block)
     cotangent = residual * (reweight(residual) * valid_mask)
     camera_grad, point_grad = pullback(cotangent)
-    camera_share = scatter_cams(camera_grad)
-    point_share = scatter_pts(point_grad)
-    new_cameras, new_cam_first, new_cam_second = adam_step(
-        cameras, cam_first, cam_second, camera_share
-    )
-    new_points, new_pt_first, new_pt_second = adam_step(points, pt_first, pt_second, point_share)
-    new_cam_block = gather_cams(new_cameras)
-    new_pt_block = gather_pts(new_points)
+    camera_grad = butterfly_sum(
+        camera_grad.reshape(cam_rows * n_pt, cam_cols), "pt", n_pt
+    ).reshape(cam_rows, n_pt * cam_cols)
+    point_grad = butterfly_sum(point_grad, "cam", n_cam)
+    new_cam_block, new_cam_first, new_cam_second = adam_step(
+        camera_block, first_block, second_block, camera_grad
+    )
+    new_pt_block, new_pt_first, new_pt_second = adam_step(
+        point_block, gather_pts(pt_first), gather_pts(pt_second), point_grad
+    )
+    new_cameras = own_cams(new_cam_block)
+    new_cam_first = own_cams(new_cam_first)
+    new_cam_second = own_cams(new_cam_second)
+    new_points = own_pts(new_pt_block)
+    new_pt_first = own_pts(new_pt_first)
+    new_pt_second = own_pts(new_pt_second)
     final = residuals(new_cam_block, new_pt_block)
     final_weight = (reweight(final) * valid_mask).reshape(-1)
     final_residual = (final * valid_mask).reshape(2, -1)

time: 166 us -> 141 us (0.85)
  waiting for transfers between devices: 49.3 us -> 25.3 us
  starting transfers between devices: 52.4 us -> 40.5 us
  local copies, waits for them, and re-layouts: 14.4 us -> 23.9 us
    ppermute x16 -> x14, waiting for transfers between devices: 32.7 us -> 5.6 us  [doubling_gather(): other = lax.ppermute(buf, axis_name, pairs)]
    ppermute x16 -> x14, starting transfers between devices: 34.8 us -> 26.6 us  [doubling_gather(): other = lax.ppermute(buf, axis_name, pairs)]
    dynamic_slice x0 -> x9, local copies, waits for them, and re-layouts: none -> 3.98 us  [the longest x3 3.91 us: own_cams(): return lax.dynamic_slice_in_dim(block, start, cam_cols, axis=1)]
    unnamed x45 -> x72, local copies, waits for them, and re-layouts: 2.71 us -> 6.48 us
    ppermute x8, starting transfers between devices: 17.6 us -> 13.9 us  [butterfly_sum(): value = value + lax.ppermute(value, axis_name, pairs)]
    ppermute x8, waiting for transfers between devices: 16.7 us -> 19.7 us  [butterfly_sum(): value = value + lax.ppermute(value, axis_name, pairs)]
    add x7, other arithmetic: 0.1 us -> 2.05 us  [butterfly_sum(): value = value + lax.ppermute(value, axis_name, pairs)]
    reduce_sum x2, other arithmetic: 2.2 us -> 0.27 us  [project(): inner = jnp.sum(axis_angle * point_obs, axis=0)]
  transfers between devices with their start and end apart: 24 -> 22, of which waited for: 19 -> 9; matrix products, arithmetic and copies ran while one was open for 6% -> 19% of each run, Pallas kernels for 7% -> 17%
where the time goes in v4:
time: 141 us; the launch traced here: 139 us
  starting transfers between devices  40.5 us (29%)
  Pallas kernels  36 us (26%)
  waiting for transfers between devices  25.3 us (18%)
  local copies, waits for them, and re-layouts  23.9 us (17%)
  other arithmetic  11.4 us (8%)
  between operations  1.64 us (1%)
    ppermute x14, starting transfers between devices, doubling_gather(): other = lax.ppermute(buf, axis_name, pairs)  26.6 us
    pallas_call x2, Pallas kernels, gather_points(): pl.pallas_call(_gather_kernel, grid=(slots // blk,), in_specs=[pl.BlockSp...  23.8 us
    ppermute x8, waiting for transfers between devices, butterfly_sum(): value = value + lax.ppermute(value, axis_name, pairs)  19.7 us
    ppermute x8, starting transfers between devices, butterfly_sum(): value = value + lax.ppermute(value, axis_name, pairs)  13.9 us
    pallas_call x1, Pallas kernels, residuals(): take_points(point_block, point_index, point_block.shape[1])  12.2 us
    unnamed x72, local copies, waits for them, and re-layouts  6.48 us
    ppermute x14, waiting for transfers between devices, doubling_gather(): other = lax.ppermute(buf, axis_name, pairs)  5.6 us
    dynamic_slice x3, local copies, waits for them, and re-layouts, own_cams(): return lax.dynamic_slice_in_dim(block, start, cam_cols, axis=1)  3.91 us
  transfers between devices with their start and end apart: 22, of which 9 were waited for; matrix products, arithmetic and copies ran while one was open for 19% of the time, Pallas kernels for 17%

profile of v4, /device:TPU:6, one launch (start us, length us, event | category | flops | bytes accessed | tf_op | source)
XLA Modules:
  0.0 138.9 jit_solution(14303902311061159146)
XLA Ops:
  4.2 1.3 collective-permute-start.13
  10.1 3.4 %collective-permute-start.1 = (f32[2,27,128]{2,0,1:T(2,128)S(1)}, f32[2,27,128]{2,0,1:T(2,128)S(1)}, u32[]{:S(2)}, u32[]{:S(2)}) collective-permute-start(f32[2,27,128]{2,0,1:T(2,128)S(1)} %maximum_select_fusion.19), channel_id=1, source_target_pairs={{0,2},{1,3},{2,0},{3,1},{4,6},{5,7},{6,4},{7,5},{8,10},{9,11},{10,... | collective-permute-start | bytes 82952 | tf_op jit(solution)/shard_map/ppermute | solution.py:217
  15.3 6.9 %collective-permute-start.2 = (f32[4,27,128]{2,0,1:T(4,128)S(1)}, f32[4,27,128]{2,0,1:T(4,128)S(1)}, u32[]{:S(2)}, u32[]{:S(2)}) collective-permute-start(f32[4,27,128]{2,0,1:T(4,128)S(1)} %maximum_select_fusion.18), channel_id=1, source_target_pairs={{0,4},{1,5},{2,6},{3,7},{4,0},{5,1},{6,2},{7,3},{8,12},{9,13},{10,... | collective-permute-start | bytes 165896 | tf_op jit(solution)/shard_map/ppermute | solution.py:217
  24.5 1.7 %collective-permute-start.3 = (f32[8,27,128]{2,0,1:T(8,128)S(1)}, f32[8,27,128]{2,0,1:T(8,128)S(1)}, u32[]{:S(2)}, u32[]{:S(2)}) collective-permute-start(f32[8,27,128]{2,0,1:T(8,128)S(1)} %maximum_select_fusion.11), channel_id=1, source_target_pairs={{0,8},{1,9},{2,10},{3,11},{4,12},{5,13},{6,14},{7,15},{8,0},{9,1},... | collective-permute-start | bytes 331784 | tf_op jit(solution)/shard_map/ppermute | solution.py:217
  26.2 2.3 %collective-permute-done.6 = f32[2,96,128]{2,1,0:T(8,128)S(1)} collective-permute-done((f32[2,96,128]{2,1,0:T(8,128)S(1)}, f32[2,96,128]{2,1,0:T(8,128)S(1)}, u32[]{:S(2)}, u32[]{:S(2)}) %collective-permute-start.6) | collective-permute-done | bytes 98336 | tf_op jit(solution)/shard_map/ppermute | solution.py:217
  29.7 3.3 %collective-permute-start.4 = (f32[16,27,128]{2,0,1:T(8,128)S(1)}, f32[16,27,128]{2,0,1:T(8,128)S(1)}, u32[]{:S(2)}, u32[]{:S(2)}) collective-permute-start(f32[16,27,128]{2,0,1:T(8,128)S(1)} %maximum_select_fusion.4), channel_id=1, source_target_pairs={{0,16},{1,17},{2,18},{3,19},{4,20},{5,21},{6,22},{7,23},{8,24},{9,... | collective-permute-start | bytes 663560 | tf_op jit(solution)/shard_map/ppermute | solution.py:217
  33.0 1.3 collective-permute-done.7
  35.5 11.9 %jvp__.1 = f32[3,12288]{1,0:T(4,128)} custom-call(f32[384,256]{1,0:T(8,128)} %copy.121.table_ref, s32[1,12288]{1,0:T(1,128)} %bitcast.320), custom_call_target="tpu_custom_call" | custom-call | tf_op jit(solution)/shard_map/jvp()/pallas_call | solution.py:58
  47.4 2.1 %slice_reduce_fusion.5 = (f32[12288]{0:T(1024)S(1)}, f32[12288]{0:T(1024)S(1)}, f32[12288]{0:T(1024)S(1)}, f32[1,12288]{1,0:T(1,128)S(1)}, f32[1,12288]{1,0:T(1,...) fusion(f32[3,12288]{1,0:T(4,128)} %jvp__.1, ...), kind=kLoop, calls=%fused_computation.219 | loop fusion | bytes 737280 | tf_op jit(solution)/shard_map/jvp()/slice | solution.py:146
  57.8 1.7 %collective-permute-start.9 = (f32[288,128]{1,0:T(8,128)S(1)}, f32[288,128]{1,0:T(8,128)S(1)}, u32[]{:S(2)}, u32[]{:S(2)}) collective-permute-start(f32[288,128]{1,0:T(8,128)S(1)} %add.357), channel_id=1, source_target_pairs={{0,2},{1,3},{2,0},{3,1},{4,6},{5,7},{6,4},{7,5},{8,10},{9,11},{10,... | collective-permute-start | bytes 442376 | tf_op jit(solution)/shard_map/ppermute | solution.py:231
  59.5 2.5 %collective-permute-start.20 = (f32[2,96,128]{2,1,0:T(8,128)S(1)}, f32[2,96,128]{2,1,0:T(8,128)S(1)}, u32[]{:S(2)}, u32[]{:S(2)}) collective-permute-start(f32[2,96,128]{2,1,0:T(8,128)S(1)} %maximum_select_fusion.17), channel_id=1, source_target_pairs={{0,64},{32,96},{64,0},{96,32},{128,192},{160,224},{192,128},{224,1... | collective-permute-start | bytes 294920 | tf_op jit(solution)/shard_map/ppermute | solution.py:217
  62.1 5.9 %collective-permute-done.9 = f32[288,128]{1,0:T(8,128)S(1)} collective-permute-done((f32[288,128]{1,0:T(8,128)S(1)}, f32[288,128]{1,0:T(8,128)S(1)}, u32[]{:S(2)}, u32[]{:S(2)}) %collective-permute-start.9) | collective-permute-done | bytes 147488 | tf_op jit(solution)/shard_map/ppermute | solution.py:231
  68.0 5.2 %collective-permute-start.10 = (f32[288,128]{1,0:T(8,128)S(1)}, f32[288,128]{1,0:T(8,128)S(1)}, u32[]{:S(2)}, u32[]{:S(2)}) collective-permute-start(f32[288,128]{1,0:T(8,128)S(1)} %add.358), channel_id=1, source_target_pairs={{0,4},{1,5},{2,6},{3,7},{4,0},{5,1},{6,2},{7,3},{8,12},{9,13},{10,... | collective-permute-start | bytes 442376 | tf_op jit(solution)/shard_map/ppermute | solution.py:231
  73.3 2.1 %collective-permute-start.21 = (f32[4,96,128]{2,1,0:T(8,128)S(1)}, f32[4,96,128]{2,1,0:T(8,128)S(1)}, u32[]{:S(2)}, u32[]{:S(2)}) collective-permute-start(f32[4,96,128]{2,1,0:T(8,128)S(1)} %maximum_select_fusion.10), channel_id=1, source_target_pairs={{0,128},{32,160},{64,192},{96,224},{128,0},{160,32},{192,64},{224,... | collective-permute-start | bytes 589832 | tf_op jit(solution)/shard_map/ppermute | solution.py:217
  76.2 12.2 %transpose_jvp___.1 = f32[384,256]{1,0:T(8,128)} custom-call(f32[3,12288]{1,0:T(4,128)} %bitcast.319, s32[1,12288]{1,0:T(1,128)} %bitcast.321), custom_call_target="tpu_custom_call" | custom-call | tf_op jit(solution)/shard_map/transpose(jvp())/pallas_call | solution.py:203
  90.6 4.3 %collective-permute-done.11 = f32[288,128]{1,0:T(8,128)S(1)} collective-permute-done((f32[288,128]{1,0:T(8,128)S(1)}, f32[288,128]{1,0:T(8,128)S(1)}, u32[]{:S(2)}, u32[]{:S(2)}) %collective-permute-start.11) | collective-permute-done | bytes 147488 | tf_op jit(solution)/shard_map/ppermute | solution.py:231
  99.5 2.5 %collective-permute-start.17 = (f32[384,256]{1,0:T(8,128)}, f32[384,256]{1,0:T(8,128)}, u32[]{:S(2)}, u32[]{:S(2)}) collective-permute-start(f32[384,256]{1,0:T(8,128)} %add.367), channel_id=1, source_target_pairs={{0,64},{32,96},{64,0},{96,32},{128,192},{160,224},{192,128},{224,1... | collective-permute-start | bytes 1179656 | tf_op jit(solution)/shard_map/ppermute | solution.py:231
  103.0 1.6 %copy.144 = f32[9,4096]{0,1:T(8,128)S(1)} copy(f32[9,4096]{1,0:T(8,128)} %get-tuple-element.63) | data formatting | bytes 294912 | tf_op jit(solution)/shard_map/sub | solution.py:177
  105.9 1.3 constant_dynamic-slice_fusion.5
  107.2 3.4 %collective-permute-done.17 = f32[384,256]{1,0:T(8,128)} collective-permute-done((f32[384,256]{1,0:T(8,128)}, f32[384,256]{1,0:T(8,128)}, u32[]{:S(2)}, u32[]{:S(2)}) %collective-permute-start.17) | collective-permute-done | bytes 393248 | tf_op jit(solution)/shard_map/ppermute | solution.py:231
  112.6 1.3 constant_dynamic-slice_fusion.4
  113.9 1.3 constant_dynamic-slice_fusion.3
  115.2 5.1 %collective-permute-done.18 = f32[384,256]{1,0:T(8,128)S(1)} collective-permute-done((f32[384,256]{1,0:T(8,128)S(1)}, f32[384,256]{1,0:T(8,128)S(1)}, u32[]{:S(2)}, u32[]{:S(2)}) %collective-permute-start.18) | collective-permute-done | bytes 393248 | tf_op jit(solution)/shard_map/ppermute | solution.py:231
  121.4 11.9 %shard_map.161 = f32[3,12288]{1,0:T(4,128)} custom-call(f32[384,256]{1,0:T(8,128)} %copy-done.2, s32[1,12288]{1,0:T(1,128)} %bitcast.322), custom_call_target="tpu_custom_call" | custom-call | tf_op jit(solution)/shard_map/pallas_call | solution.py:58
  (211 shorter events, 40.9 us)
Async XLA Ops:
  1.4 8.7 %collective-permute-start = (f32[1,27,128]{2,0,1:T(1,128)S(1)}, f32[1,27,128]{2,0,1:T(1,128)S(1)}, u32[]{:S(2)}, u32[]{:S(2)}) collective-permute-start(f32[1,27,128]{2,0,1:T(1,128)S(1)} %broadcast_in_dim.24), channel_id=1, source_target_pairs={{0,1},{1,0},{2,3},{3,2},{4,5},{5,4},{6,7},{7,6},{8,9},{9,8},{10,11... | collective-permute-start | bytes 41480 | tf_op jit(solution)/shard_map/ppermute | solution.py:217
  2.4 19.9 %collective-permute-start.5 = (f32[1,96,128]{2,1,0:T(8,128)S(1)}, f32[1,96,128]{2,1,0:T(8,128)S(1)}, u32[]{:S(2)}, u32[]{:S(2)}) collective-permute-start(f32[1,96,128]{2,1,0:T(8,128)S(1)} %broadcast_in_dim_reshape.9), channel_id=1, source_target_pairs={{0,32},{32,0},{64,96},{96,64},{128,160},{160,128},{192,224},{224,1... | collective-permute-start | bytes 147464 | tf_op jit(solution)/shard_map/ppermute | solution.py:217
  4.2 52.4 %collective-permute-start.13 = (f32[1,96,128]{2,1,0:T(8,128)S(1)}, f32[1,96,128]{2,1,0:T(8,128)S(1)}, u32[]{:S(2)}, u32[]{:S(2)}) collective-permute-start(f32[1,96,128]{2,1,0:T(8,128)S(1)} %broadcast_in_dim_reshape.10), channel_id=1, source_target_pairs={{0,32},{32,0},{64,96},{96,64},{128,160},{160,128},{192,224},{224,1... | collective-permute-start | bytes 147464 | tf_op jit(solution)/shard_map/ppermute | solution.py:217
  6.3 53.2 %collective-permute-start.19 = (f32[1,96,128]{2,1,0:T(8,128)S(1)}, f32[1,96,128]{2,1,0:T(8,128)S(1)}, u32[]{:S(2)}, u32[]{:S(2)}) collective-permute-start(f32[1,96,128]{2,1,0:T(8,128)S(1)} %broadcast_in_dim_reshape.11), channel_id=1, source_target_pairs={{0,32},{32,0},{64,96},{96,64},{128,160},{160,128},{192,224},{224,1... | collective-permute-start | bytes 147464 | tf_op jit(solution)/shard_map/ppermute | solution.py:217
  10.1 5.2 %collective-permute-start.1 = (f32[2,27,128]{2,0,1:T(2,128)S(1)}, f32[2,27,128]{2,0,1:T(2,128)S(1)}, u32[]{:S(2)}, u32[]{:S(2)}) collective-permute-start(f32[2,27,128]{2,0,1:T(2,128)S(1)} %maximum_select_fusion.19), channel_id=1, source_target_pairs={{0,2},{1,3},{2,0},{3,1},{4,6},{5,7},{6,4},{7,5},{8,10},{9,11},{10,... | collective-permute-start | bytes 82952 | tf_op jit(solution)/shard_map/ppermute | solution.py:217
  15.3 9.2 %collective-permute-start.2 = (f32[4,27,128]{2,0,1:T(4,128)S(1)}, f32[4,27,128]{2,0,1:T(4,128)S(1)}, u32[]{:S(2)}, u32[]{:S(2)}) collective-permute-start(f32[4,27,128]{2,0,1:T(4,128)S(1)} %maximum_select_fusion.18), channel_id=1, source_target_pairs={{0,4},{1,5},{2,6},{3,7},{4,0},{5,1},{6,2},{7,3},{8,12},{9,13},{10,... | collective-permute-start | bytes 165896 | tf_op jit(solution)/shard_map/ppermute | solution.py:217
  22.3 6.2 %collective-permute-start.6 = (f32[2,96,128]{2,1,0:T(8,128)S(1)}, f32[2,96,128]{2,1,0:T(8,128)S(1)}, u32[]{:S(2)}, u32[]{:S(2)}) collective-permute-start(f32[2,96,128]{2,1,0:T(8,128)S(1)} %maximum_select_fusion.13), channel_id=1, source_target_pairs={{0,64},{32,96},{64,0},{96,32},{128,192},{160,224},{192,128},{224,1... | collective-permute-start | bytes 294920 | tf_op jit(solution)/shard_map/ppermute | solution.py:217
  24.5 5.1 %collective-permute-start.3 = (f32[8,27,128]{2,0,1:T(8,128)S(1)}, f32[8,27,128]{2,0,1:T(8,128)S(1)}, u32[]{:S(2)}, u32[]{:S(2)}) collective-permute-start(f32[8,27,128]{2,0,1:T(8,128)S(1)} %maximum_select_fusion.11), channel_id=1, source_target_pairs={{0,8},{1,9},{2,10},{3,11},{4,12},{5,13},{6,14},{7,15},{8,0},{9,1},... | collective-permute-start | bytes 331784 | tf_op jit(solution)/shard_map/ppermute | solution.py:217
  28.5 5.8 %collective-permute-start.7 = (f32[4,96,128]{2,1,0:T(8,128)S(1)}, f32[4,96,128]{2,1,0:T(8,128)S(1)}, u32[]{:S(2)}, u32[]{:S(2)}) collective-permute-start(f32[4,96,128]{2,1,0:T(8,128)S(1)} %maximum_select_fusion.6), channel_id=1, source_target_pairs={{0,128},{32,160},{64,192},{96,224},{128,0},{160,32},{192,64},{224,... | collective-permute-start | bytes 589832 | tf_op jit(solution)/shard_map/ppermute | solution.py:217
  29.7 17.8 %copy-start.17 = (f32[2,12288]{1,0:T(2,128)S(1)}, f32[2,12288]{1,0:T(2,128)}, u32[]{:S(2)}) copy-start(f32[2,12288]{1,0:T(2,128)} %param.16) | copy-start | bytes 294916
  29.7 20.1 %collective-permute-start.4 = (f32[16,27,128]{2,0,1:T(8,128)S(1)}, f32[16,27,128]{2,0,1:T(8,128)S(1)}, u32[]{:S(2)}, u32[]{:S(2)}) collective-permute-start(f32[16,27,128]{2,0,1:T(8,128)S(1)} %maximum_select_fusion.4), channel_id=1, source_target_pairs={{0,16},{1,17},{2,18},{3,19},{4,20},{5,21},{6,22},{7,23},{8,24},{9,... | collective-permute-start | bytes 663560 | tf_op jit(solution)/shard_map/ppermute | solution.py:217
  55.6 2.2 %collective-permute-start.8 = (f32[288,128]{1,0:T(8,128)S(1)}, f32[288,128]{1,0:T(8,128)S(1)}, u32[]{:S(2)}, u32[]{:S(2)}) collective-permute-start(f32[288,128]{1,0:T(8,128)S(1)} %reshape.1218), channel_id=1, source_target_pairs={{0,1},{1,0},{2,3},{3,2},{4,5},{5,4},{6,7},{7,6},{8,9},{9,8},{10,11... | collective-permute-start | bytes 442376 | tf_op jit(solution)/shard_map/ppermute | solution.py:231
  56.6 16.6 %collective-permute-start.14 = (f32[2,96,128]{2,1,0:T(8,128)S(1)}, f32[2,96,128]{2,1,0:T(8,128)S(1)}, u32[]{:S(2)}, u32[]{:S(2)}) collective-permute-start(f32[2,96,128]{2,1,0:T(8,128)S(1)} %maximum_select_fusion.15), channel_id=1, source_target_pairs={{0,64},{32,96},{64,0},{96,32},{128,192},{160,224},{192,128},{224,1... | collective-permute-start | bytes 294920 | tf_op jit(solution)/shard_map/ppermute | solution.py:217
  57.8 10.1 %collective-permute-start.9 = (f32[288,128]{1,0:T(8,128)S(1)}, f32[288,128]{1,0:T(8,128)S(1)}, u32[]{:S(2)}, u32[]{:S(2)}) collective-permute-start(f32[288,128]{1,0:T(8,128)S(1)} %add.357), channel_id=1, source_target_pairs={{0,2},{1,3},{2,0},{3,1},{4,6},{5,7},{6,4},{7,5},{8,10},{9,11},{10,... | collective-permute-start | bytes 442376 | tf_op jit(solution)/shard_map/ppermute | solution.py:231
  59.5 13.8 %collective-permute-start.20 = (f32[2,96,128]{2,1,0:T(8,128)S(1)}, f32[2,96,128]{2,1,0:T(8,128)S(1)}, u32[]{:S(2)}, u32[]{:S(2)}) collective-permute-start(f32[2,96,128]{2,1,0:T(8,128)S(1)} %maximum_select_fusion.17), channel_id=1, source_target_pairs={{0,64},{32,96},{64,0},{96,32},{128,192},{160,224},{192,128},{224,1... | collective-permute-start | bytes 294920 | tf_op jit(solution)/shard_map/ppermute | solution.py:217
  68.0 21.4 %collective-permute-start.10 = (f32[288,128]{1,0:T(8,128)S(1)}, f32[288,128]{1,0:T(8,128)S(1)}, u32[]{:S(2)}, u32[]{:S(2)}) collective-permute-start(f32[288,128]{1,0:T(8,128)S(1)} %add.358), channel_id=1, source_target_pairs={{0,4},{1,5},{2,6},{3,7},{4,0},{5,1},{6,2},{7,3},{8,12},{9,13},{10,... | collective-permute-start | bytes 442376 | tf_op jit(solution)/shard_map/ppermute | solution.py:231
  73.2 23.0 %collective-permute-start.15 = (f32[4,96,128]{2,1,0:T(8,128)S(1)}, f32[4,96,128]{2,1,0:T(8,128)S(1)}, u32[]{:S(2)}, u32[]{:S(2)}) collective-permute-start(f32[4,96,128]{2,1,0:T(8,128)S(1)} %maximum_select_fusion.8), channel_id=1, source_target_pairs={{0,128},{32,160},{64,192},{96,224},{128,0},{160,32},{192,64},{224,... | collective-permute-start | bytes 589832 | tf_op jit(solution)/shard_map/ppermute | solution.py:217
  73.3 23.4 %collective-permute-start.21 = (f32[4,96,128]{2,1,0:T(8,128)S(1)}, f32[4,96,128]{2,1,0:T(8,128)S(1)}, u32[]{:S(2)}, u32[]{:S(2)}) collective-permute-start(f32[4,96,128]{2,1,0:T(8,128)S(1)} %maximum_select_fusion.10), channel_id=1, source_target_pairs={{0,128},{32,160},{64,192},{96,224},{128,0},{160,32},{192,64},{224,... | collective-permute-start | bytes 589832 | tf_op jit(solution)/shard_map/ppermute | solution.py:217
  88.4 10.3 %collective-permute-start.16 = (f32[384,256]{1,0:T(8,128)}, f32[384,256]{1,0:T(8,128)S(1)}, u32[]{:S(2)}, u32[]{:S(2)}) collective-permute-start(f32[384,256]{1,0:T(8,128)} %transpose_jvp___.1), channel_id=1, source_target_pairs={{0,32},{32,0},{64,96},{96,64},{128,160},{160,128},{192,224},{224,1... | collective-permute-start | bytes 1179656 | tf_op jit(solution)/shard_map/ppermute | solution.py:231
  89.4 5.5 %collective-permute-start.11 = (f32[288,128]{1,0:T(8,128)S(1)}, f32[288,128]{1,0:T(8,128)S(1)}, u32[]{:S(2)}, u32[]{:S(2)}) collective-permute-start(f32[288,128]{1,0:T(8,128)S(1)} %add.359), channel_id=1, source_target_pairs={{0,8},{1,9},{2,10},{3,11},{4,12},{5,13},{6,14},{7,15},{8,0},{9,1},... | collective-permute-start | bytes 442376 | tf_op jit(solution)/shard_map/ppermute | solution.py:231
  94.9 7.1 %collective-permute-start.12 = (f32[288,128]{1,0:T(8,128)S(1)}, f32[288,128]{1,0:T(8,128)S(1)}, u32[]{:S(2)}, u32[]{:S(2)}) collective-permute-start(f32[288,128]{1,0:T(8,128)S(1)} %add.360), channel_id=1, source_target_pairs={{0,16},{1,17},{2,18},{3,19},{4,20},{5,21},{6,22},{7,23},{8,24},{9,... | collective-permute-start | bytes 442376 | tf_op jit(solution)/shard_map/ppermute | solution.py:231
  99.5 11.0 %collective-permute-start.17 = (f32[384,256]{1,0:T(8,128)}, f32[384,256]{1,0:T(8,128)}, u32[]{:S(2)}, u32[]{:S(2)}) collective-permute-start(f32[384,256]{1,0:T(8,128)} %add.367), channel_id=1, source_target_pairs={{0,64},{32,96},{64,0},{96,32},{128,192},{160,224},{192,128},{224,1... | collective-permute-start | bytes 1179656 | tf_op jit(solution)/shard_map/ppermute | solution.py:231
  103.0 17.3 %copy-start.1 = (f32[384,256]{1,0:T(8,128)S(1)}, f32[384,256]{1,0:T(8,128)}, u32[]{:S(2)}) copy-start(f32[384,256]{1,0:T(8,128)} %copy.121.table_ref) | copy-start | bytes 1179652
  111.7 8.7 %collective-permute-start.18 = (f32[384,256]{1,0:T(8,128)S(1)}, f32[384,256]{1,0:T(8,128)S(1)}, u32[]{:S(2)}, u32[]{:S(2)}) collective-permute-start(f32[384,256]{1,0:T(8,128)S(1)} %add.368), channel_id=1, source_target_pairs={{0,128},{32,160},{64,192},{96,224},{128,0},{160,32},{192,64},{224,... | collective-permute-start | bytes 1179656 | tf_op jit(solution)/shard_map/ppermute | solution.py:231
  (17 other events, 37.5 us)

commit v5 on v4

--- a/solution.py
+++ b/solution.py
@@ -233,10 +233,11 @@
         return value
 
     def gather_pts(local):
-        flat = local.reshape(pt_rows * pt_cols // LANES, LANES)
+        rows = local.shape[0]
+        flat = local.reshape(rows * pt_cols // LANES, LANES)
         stacked = doubling_gather(flat, "cam", n_cam)
-        stacked = stacked.reshape(n_cam, pt_rows, pt_cols // LANES, LANES)
-        return stacked.transpose(1, 3, 0, 2).reshape(pt_rows * LANES, n_cam * pt_cols // LANES)
+        stacked = stacked.reshape(n_cam, rows, pt_cols // LANES, LANES)
+        return stacked.transpose(1, 3, 0, 2).reshape(rows * LANES, n_cam * pt_cols // LANES)
 
     def own_pts(table):
         parts = table.reshape(pt_rows, LANES, n_cam, pt_cols // LANES)
@@ -251,7 +252,9 @@
     cam_state = doubling_gather(cam_state, "pt", n_pt)
     cam_state = cam_state.transpose(1, 0, 2).reshape(3, cam_rows, n_pt * cam_cols)
     camera_block, first_block, second_block = cam_state[0], cam_state[1], cam_state[2]
-    point_block = gather_pts(points)
+    pt_state = gather_pts(jnp.concatenate([points, pt_first, pt_second], axis=0))
+    pt_state = pt_state.reshape(3, pt_rows * LANES, pt_state.shape[1])
+    point_block, pt_first_block, pt_second_block = pt_state[0], pt_state[1], pt_state[2]
     residual, pullback = jax.vjp(residuals, camera_block, point_block)
     cotangent = residual * (reweight(residual) * valid_mask)
     camera_grad, point_grad = pullback(cotangent)
@@ -263,7 +266,7 @@
         camera_block, first_block, second_block, camera_grad
     )
     new_pt_block, new_pt_first, new_pt_second = adam_step(
-        point_block, gather_pts(pt_first), gather_pts(pt_second), point_grad
+        point_block, pt_first_block, pt_second_block, point_grad
     )
     new_cameras = own_cams(new_cam_block)
     new_cam_first = own_cams(new_cam_first)

time: 141 us -> 156 us (1.11)
  waiting for transfers between devices: 25.3 us -> 42 us
  starting transfers between devices: 40.5 us -> 32.8 us
  other arithmetic: 11.4 us -> 18.5 us
    ppermute x14 -> x8, waiting for transfers between devices: 5.6 us -> 20.6 us  [doubling_gather(): other = lax.ppermute(buf, axis_name, pairs)]
    ppermute x14 -> x8, starting transfers between devices: 26.6 us -> 19.4 us  [doubling_gather(): other = lax.ppermute(buf, axis_name, pairs)]
    another operation x3 -> x1, local copies, waits for them, and re-layouts: 2.63 us -> 0.03 us  [doubling_gather(): buf = local[None]]
    reduce_sum x2, other arithmetic: 0.27 us -> 2.2 us  [project(): inner = jnp.sum(axis_angle * point_obs, axis=0)]
    add x7, other arithmetic: 2.05 us -> 3.95 us  [butterfly_sum(): value = value + lax.ppermute(value, axis_name, pairs)]
    unnamed x72 -> x82, local copies, waits for them, and re-layouts: 6.48 us -> 8.17 us
    ppermute x8, waiting for transfers between devices: 19.7 us -> 21.4 us  [butterfly_sum(): value = value + lax.ppermute(value, axis_name, pairs)]
  transfers between devices with their start and end apart: 22 -> 16, of which waited for: 9 -> 13; matrix products, arithmetic and copies ran while one was open for 19% -> 14% of each run, Pallas kernels for 17% -> 8%
where the time goes in v5:
time: 156 us; the launch traced here: 155 us
  waiting for transfers between devices  42 us (27%)
  Pallas kernels  36.1 us (23%)
  starting transfers between devices  32.8 us (21%)
  local copies, waits for them, and re-layouts  24.3 us (16%)
  other arithmetic  18.5 us (12%)
  between operations  1.57 us (1%)
    pallas_call x2, Pallas kernels, gather_points(): pl.pallas_call(_gather_kernel, grid=(slots // blk,), in_specs=[pl.BlockSp...  23.8 us
    ppermute x8, waiting for transfers between devices, butterfly_sum(): value = value + lax.ppermute(value, axis_name, pairs)  21.4 us
    ppermute x8, waiting for transfers between devices, doubling_gather(): other = lax.ppermute(buf, axis_name, pairs)  20.6 us
    ppermute x8, starting transfers between devices, doubling_gather(): other = lax.ppermute(buf, axis_name, pairs)  19.4 us
    ppermute x8, starting transfers between devices, butterfly_sum(): value = value + lax.ppermute(value, axis_name, pairs)  13.4 us
    pallas_call x1, Pallas kernels, residuals(): take_points(point_block, point_index, point_block.shape[1])  12.2 us
    unnamed x82, local copies, waits for them, and re-layouts  8.17 us
    add x7, other arithmetic, butterfly_sum(): value = value + lax.ppermute(value, axis_name, pairs)  3.95 us
  transfers between devices with their start and end apart: 16, of which 13 were waited for; matrix products, arithmetic and copies ran while one was open for 14% of the time, Pallas kernels for 8%

profile of v5, /device:TPU:6, one launch (start us, length us, event | category | flops | bytes accessed | tf_op | source)
XLA Modules:
  0.0 155.2 jit_solution(6192823492805288085)
XLA Ops:
  4.6 3.4 %collective-permute-start.1 = (f32[2,27,128]{2,0,1:T(2,128)S(1)}, f32[2,27,128]{2,0,1:T(2,128)S(1)}, u32[]{:S(2)}, u32[]{:S(2)}) collective-permute-start(f32[2,27,128]{2,0,1:T(2,128)S(1)} %maximum_select_fusion.9), channel_id=1, source_target_pairs={{0,2},{1,3},{2,0},{3,1},{4,6},{5,7},{6,4},{7,5},{8,10},{9,11},{10,... | collective-permute-start | bytes 82952 | tf_op jit(solution)/shard_map/ppermute | solution.py:217
  9.9 6.9 %collective-permute-start.2 = (f32[4,27,128]{2,0,1:T(4,128)S(1)}, f32[4,27,128]{2,0,1:T(4,128)S(1)}, u32[]{:S(2)}, u32[]{:S(2)}) collective-permute-start(f32[4,27,128]{2,0,1:T(4,128)S(1)} %maximum_select_fusion.8), channel_id=1, source_target_pairs={{0,4},{1,5},{2,6},{3,7},{4,0},{5,1},{6,2},{7,3},{8,12},{9,13},{10,... | collective-permute-start | bytes 165896 | tf_op jit(solution)/shard_map/ppermute | solution.py:217
  17.5 1.6 %collective-permute-done.2 = f32[4,27,128]{2,0,1:T(4,128)S(1)} collective-permute-done((f32[4,27,128]{2,0,1:T(4,128)S(1)}, f32[4,27,128]{2,0,1:T(4,128)S(1)}, u32[]{:S(2)}, u32[]{:S(2)}) %collective-permute-start.2) | collective-permute-done | bytes 55328 | tf_op jit(solution)/shard_map/ppermute | solution.py:217
  19.1 1.7 %collective-permute-start.3 = (f32[8,27,128]{2,0,1:T(8,128)S(1)}, f32[8,27,128]{2,0,1:T(8,128)S(1)}, u32[]{:S(2)}, u32[]{:S(2)}) collective-permute-start(f32[8,27,128]{2,0,1:T(8,128)S(1)} %maximum_select_fusion.7), channel_id=1, source_target_pairs={{0,8},{1,9},{2,10},{3,11},{4,12},{5,13},{6,14},{7,15},{8,0},{9,1},... | collective-permute-start | bytes 331784 | tf_op jit(solution)/shard_map/ppermute | solution.py:217
  20.8 3.2 %collective-permute-done.3 = f32[8,27,128]{2,0,1:T(8,128)S(1)} collective-permute-done((f32[8,27,128]{2,0,1:T(8,128)S(1)}, f32[8,27,128]{2,0,1:T(8,128)S(1)}, u32[]{:S(2)}, u32[]{:S(2)}) %collective-permute-start.3) | collective-permute-done | bytes 110624 | tf_op jit(solution)/shard_map/ppermute | solution.py:217
  23.9 3.3 %collective-permute-start.4 = (f32[16,27,128]{2,0,1:T(8,128)S(1)}, f32[16,27,128]{2,0,1:T(8,128)S(1)}, u32[]{:S(2)}, u32[]{:S(2)}) collective-permute-start(f32[16,27,128]{2,0,1:T(8,128)S(1)} %maximum_select_fusion.6), channel_id=1, source_target_pairs={{0,16},{1,17},{2,18},{3,19},{4,20},{5,21},{6,22},{7,23},{8,24},{9,... | collective-permute-start | bytes 663560 | tf_op jit(solution)/shard_map/ppermute | solution.py:217
  28.5 3.0 %collective-permute-done.4 = f32[16,27,128]{2,0,1:T(8,128)S(1)} collective-permute-done((f32[16,27,128]{2,0,1:T(8,128)S(1)}, f32[16,27,128]{2,0,1:T(8,128)S(1)}, u32[]{:S(2)}, u32[]{:S(2)}) %collective-permute-start.4) | collective-permute-done | bytes 221216 | tf_op jit(solution)/shard_map/ppermute | solution.py:217
  33.8 1.8 %collective-permute-done.6 = f32[2,288,128]{2,1,0:T(8,128)S(1)} collective-permute-done((f32[2,288,128]{2,1,0:T(8,128)S(1)}, f32[2,288,128]{2,1,0:T(8,128)S(1)}, u32[]{:S(2)}, u32[]{:S(2)}) %collective-permute-start.6) | collective-permute-done | bytes 294944 | tf_op jit(solution)/shard_map/ppermute | solution.py:217
  35.6 2.0 %collective-permute-start.7 = (f32[4,288,128]{2,1,0:T(8,128)S(1)}, f32[4,288,128]{2,1,0:T(8,128)S(1)}, u32[]{:S(2)}, u32[]{:S(2)}) collective-permute-start(f32[4,288,128]{2,1,0:T(8,128)S(1)} %maximum_select_fusion.2), channel_id=1, source_target_pairs={{0,128},{32,160},{64,192},{96,224},{128,0},{160,32},{192,64},{224,... | collective-permute-start | bytes 1769480 | tf_op jit(solution)/shard_map/ppermute | solution.py:217
  37.9 8.8 %collective-permute-done.7 = f32[4,288,128]{2,1,0:T(8,128)S(1)} collective-permute-done((f32[4,288,128]{2,1,0:T(8,128)S(1)}, f32[4,288,128]{2,1,0:T(8,128)S(1)}, u32[]{:S(2)}, u32[]{:S(2)}) %collective-permute-start.7) | collective-permute-done | bytes 589856 | tf_op jit(solution)/shard_map/ppermute | solution.py:217
  48.2 11.9 %jvp__.1 = f32[3,12288]{1,0:T(4,128)} custom-call(f32[384,256]{1,0:T(8,128)} %copy.117.table_ref, s32[1,12288]{1,0:T(1,128)} %bitcast.305), custom_call_target="tpu_custom_call" | custom-call | tf_op jit(solution)/shard_map/jvp()/pallas_call | solution.py:58
  61.3 2.1 %slice_reduce_fusion.5 = (f32[12288]{0:T(1024)S(1)}, f32[12288]{0:T(1024)S(1)}, f32[12288]{0:T(1024)S(1)}, f32[1,12288]{1,0:T(1,128)S(1)}, f32[1,12288]{1,0:T(1,...) fusion(f32[3,12288]{1,0:T(4,128)} %jvp__.1, ...), kind=kLoop, calls=%fused_computation.206 | loop fusion | bytes 737280 | tf_op jit(solution)/shard_map/jvp()/slice | solution.py:146
  69.8 2.3 %collective-permute-start.9 = (f32[288,128]{1,0:T(8,128)S(1)}, f32[288,128]{1,0:T(8,128)S(1)}, u32[]{:S(2)}, u32[]{:S(2)}) collective-permute-start(f32[288,128]{1,0:T(8,128)S(1)} %add.351), channel_id=1, source_target_pairs={{0,2},{1,3},{2,0},{3,1},{4,6},{5,7},{6,4},{7,5},{8,10},{9,11},{10,... | collective-permute-start | bytes 442376 | tf_op jit(solution)/shard_map/ppermute | solution.py:231
  72.1 7.7 %collective-permute-done.9 = f32[288,128]{1,0:T(8,128)S(1)} collective-permute-done((f32[288,128]{1,0:T(8,128)S(1)}, f32[288,128]{1,0:T(8,128)S(1)}, u32[]{:S(2)}, u32[]{:S(2)}) %collective-permute-start.9) | collective-permute-done | bytes 147488 | tf_op jit(solution)/shard_map/ppermute | solution.py:231
  79.9 5.9 %collective-permute-start.10 = (f32[288,128]{1,0:T(8,128)S(1)}, f32[288,128]{1,0:T(8,128)S(1)}, u32[]{:S(2)}, u32[]{:S(2)}) collective-permute-start(f32[288,128]{1,0:T(8,128)S(1)} %add.352), channel_id=1, source_target_pairs={{0,4},{1,5},{2,6},{3,7},{4,0},{5,1},{6,2},{7,3},{8,12},{9,13},{10,... | collective-permute-start | bytes 442376 | tf_op jit(solution)/shard_map/ppermute | solution.py:231
  85.8 1.7 %copy.150 = f32[1,3,48,256]{3,1,2,0:T(4,128)} copy(f32[1,3,48,256]{3,2,1,0:T(8,128)} %get-tuple-element.85) | data formatting | bytes 294912
  87.5 12.2 %transpose_jvp___.1 = f32[384,256]{1,0:T(8,128)} custom-call(f32[3,12288]{1,0:T(4,128)} %bitcast.301, s32[1,12288]{1,0:T(1,128)} %bitcast.306), custom_call_target="tpu_custom_call" | custom-call | tf_op jit(solution)/shard_map/transpose(jvp())/pallas_call | solution.py:203
  102.9 3.3 %collective-permute-done.11 = f32[288,128]{1,0:T(8,128)S(1)} collective-permute-done((f32[288,128]{1,0:T(8,128)S(1)}, f32[288,128]{1,0:T(8,128)S(1)}, u32[]{:S(2)}, u32[]{:S(2)}) %collective-permute-start.11) | collective-permute-done | bytes 147488 | tf_op jit(solution)/shard_map/ppermute | solution.py:231
  106.2 1.5 collective-permute-start.12
  110.4 1.8 %add.361 = f32[384,256]{1,0:T(8,128)} add(f32[384,256]{1,0:T(8,128)S(1)} %copy-done.3, f32[384,256]{1,0:T(8,128)} %collective-permute-done.13) | non-fusion elementwise | flops 98304 | bytes 1179648 | tf_op jit(solution)/shard_map/add | solution.py:231
  121.0 2.5 %collective-permute-done.14 = f32[384,256]{1,0:T(8,128)} collective-permute-done((f32[384,256]{1,0:T(8,128)}, f32[384,256]{1,0:T(8,128)}, u32[]{:S(2)}, u32[]{:S(2)}) %collective-permute-start.14) | collective-permute-done | bytes 393248 | tf_op jit(solution)/shard_map/ppermute | solution.py:231
  127.3 6.0 %collective-permute-done.15 = f32[384,256]{1,0:T(8,128)S(1)} collective-permute-done((f32[384,256]{1,0:T(8,128)S(1)}, f32[384,256]{1,0:T(8,128)S(1)}, u32[]{:S(2)}, u32[]{:S(2)}) %collective-permute-start.15) | collective-permute-done | bytes 393248 | tf_op jit(solution)/shard_map/ppermute | solution.py:231
  134.3 11.9 %shard_map.161 = f32[3,12288]{1,0:T(4,128)} custom-call(f32[384,256]{1,0:T(8,128)} %get-tuple-element.60.table_ref, s32[1,12288]{1,0:T(1,128)} %bitcast.307), custom_call_target="tpu_custom_call" | custom-call | tf_op jit(solution)/shard_map/pallas_call | solution.py:58
  147.4 1.5 slice_reduce_fusion.2
  (201 shorter events, 45.7 us)
Async XLA Ops:
  1.6 25.6 %collective-permute-start.5 = (f32[1,288,128]{2,1,0:T(8,128)S(1)}, f32[1,288,128]{2,1,0:T(8,128)S(1)}, u32[]{:S(2)}, u32[]{:S(2)}) collective-permute-start(f32[1,288,128]{2,1,0:T(8,128)S(1)} %broadcast_in_dim_reshape.3), channel_id=1, source_target_pairs={{0,32},{32,0},{64,96},{96,64},{128,160},{160,128},{192,224},{224,1... | collective-permute-start | bytes 442376 | tf_op jit(solution)/shard_map/ppermute | solution.py:217
  3.3 1.3 collective-permute-start
  4.6 5.2 %collective-permute-start.1 = (f32[2,27,128]{2,0,1:T(2,128)S(1)}, f32[2,27,128]{2,0,1:T(2,128)S(1)}, u32[]{:S(2)}, u32[]{:S(2)}) collective-permute-start(f32[2,27,128]{2,0,1:T(2,128)S(1)} %maximum_select_fusion.9), channel_id=1, source_target_pairs={{0,2},{1,3},{2,0},{3,1},{4,6},{5,7},{6,4},{7,5},{8,10},{9,11},{10,... | collective-permute-start | bytes 82952 | tf_op jit(solution)/shard_map/ppermute | solution.py:217
  8.6 23.8 %copy-start.24 = (s32[48]{0:T(128)}, s32[48]{0:T(128)S(1)}, u32[]{:S(2)}) copy-start(s32[48]{0:T(128)S(1)} %compare_select_fusion) | copy-start | bytes 580
  9.9 9.2 %collective-permute-start.2 = (f32[4,27,128]{2,0,1:T(4,128)S(1)}, f32[4,27,128]{2,0,1:T(4,128)S(1)}, u32[]{:S(2)}, u32[]{:S(2)}) collective-permute-start(f32[4,27,128]{2,0,1:T(4,128)S(1)} %maximum_select_fusion.8), channel_id=1, source_target_pairs={{0,4},{1,5},{2,6},{3,7},{4,0},{5,1},{6,2},{7,3},{8,12},{9,13},{10,... | collective-permute-start | bytes 165896 | tf_op jit(solution)/shard_map/ppermute | solution.py:217
  17.5 16.3 %copy-start.22 = (pred[48]{0:T(512)(128)(4,1)}, pred[48]{0:T(512)(128)(4,1)S(1)}, u32[]{:S(2)}) copy-start(pred[48]{0:T(512)(128)(4,1)S(1)} %compare_and_fusion) | copy-start | bytes 148
  19.1 4.8 %collective-permute-start.3 = (f32[8,27,128]{2,0,1:T(8,128)S(1)}, f32[8,27,128]{2,0,1:T(8,128)S(1)}, u32[]{:S(2)}, u32[]{:S(2)}) collective-permute-start(f32[8,27,128]{2,0,1:T(8,128)S(1)} %maximum_select_fusion.7), channel_id=1, source_target_pairs={{0,8},{1,9},{2,10},{3,11},{4,12},{5,13},{6,14},{7,15},{8,0},{9,1},... | collective-permute-start | bytes 331784 | tf_op jit(solution)/shard_map/ppermute | solution.py:217
  23.9 7.5 %collective-permute-start.4 = (f32[16,27,128]{2,0,1:T(8,128)S(1)}, f32[16,27,128]{2,0,1:T(8,128)S(1)}, u32[]{:S(2)}, u32[]{:S(2)}) collective-permute-start(f32[16,27,128]{2,0,1:T(8,128)S(1)} %maximum_select_fusion.6), channel_id=1, source_target_pairs={{0,16},{1,17},{2,18},{3,19},{4,20},{5,21},{6,22},{7,23},{8,24},{9,... | collective-permute-start | bytes 663560 | tf_op jit(solution)/shard_map/ppermute | solution.py:217
  27.2 8.3 %collective-permute-start.6 = (f32[2,288,128]{2,1,0:T(8,128)S(1)}, f32[2,288,128]{2,1,0:T(8,128)S(1)}, u32[]{:S(2)}, u32[]{:S(2)}) collective-permute-start(f32[2,288,128]{2,1,0:T(8,128)S(1)} %maximum_select_fusion.5), channel_id=1, source_target_pairs={{0,64},{32,96},{64,0},{96,32},{128,192},{160,224},{192,128},{224,1... | collective-permute-start | bytes 884744 | tf_op jit(solution)/shard_map/ppermute | solution.py:217
  35.6 11.1 %collective-permute-start.7 = (f32[4,288,128]{2,1,0:T(8,128)S(1)}, f32[4,288,128]{2,1,0:T(8,128)S(1)}, u32[]{:S(2)}, u32[]{:S(2)}) collective-permute-start(f32[4,288,128]{2,1,0:T(8,128)S(1)} %maximum_select_fusion.2), channel_id=1, source_target_pairs={{0,128},{32,160},{64,192},{96,224},{128,0},{160,32},{192,64},{224,... | collective-permute-start | bytes 1769480 | tf_op jit(solution)/shard_map/ppermute | solution.py:217
  47.3 16.5 %copy-start.20 = (s32[48]{0:T(128)S(1)}, s32[48]{0:T(128)}, u32[]{:S(2)}) copy-start(s32[48]{0:T(128)} %param.19) | copy-start | bytes 580
  68.3 33.9 %copy-start.21 = (s32[48]{0:T(128)S(1)}, s32[48]{0:T(128)}, u32[]{:S(2)}) copy-start(s32[48]{0:T(128)} %param.19) | copy-start | bytes 580
  68.3 40.2 %copy-start.4 = (f32[9,32,128]{2,1,0:T(8,128)S(1)}, f32[9,32,128]{2,1,0:T(8,128)}, u32[]{:S(2)}) copy-start(f32[9,32,128]{2,1,0:T(8,128)} %get-tuple-element.81) | copy-start | bytes 442372
  68.3 1.5 collective-permute-start.8
  69.8 10.0 %collective-permute-start.9 = (f32[288,128]{1,0:T(8,128)S(1)}, f32[288,128]{1,0:T(8,128)S(1)}, u32[]{:S(2)}, u32[]{:S(2)}) collective-permute-start(f32[288,128]{1,0:T(8,128)S(1)} %add.351), channel_id=1, source_target_pairs={{0,2},{1,3},{2,0},{3,1},{4,6},{5,7},{6,4},{7,5},{8,10},{9,11},{10,... | collective-permute-start | bytes 442376 | tf_op jit(solution)/shard_map/ppermute | solution.py:231
  79.9 21.1 %collective-permute-start.10 = (f32[288,128]{1,0:T(8,128)S(1)}, f32[288,128]{1,0:T(8,128)S(1)}, u32[]{:S(2)}, u32[]{:S(2)}) collective-permute-start(f32[288,128]{1,0:T(8,128)S(1)} %add.352), channel_id=1, source_target_pairs={{0,4},{1,5},{2,6},{3,7},{4,0},{5,1},{6,2},{7,3},{8,12},{9,13},{10,... | collective-permute-start | bytes 442376 | tf_op jit(solution)/shard_map/ppermute | solution.py:231
  85.8 23.3 %copy-start.5 = (s32[6,2,8,128]{3,1,2,0:T(2,128)}, s32[6,2,8,128]{3,1,2,0:T(2,128)S(1)}, u32[]{:S(2)}) copy-start(s32[6,2,8,128]{3,1,2,0:T(2,128)S(1)} %copy.159) | copy-start | bytes 147460
  99.8 10.6 %collective-permute-start.13 = (f32[384,256]{1,0:T(8,128)}, f32[384,256]{1,0:T(8,128)}, u32[]{:S(2)}, u32[]{:S(2)}) collective-permute-start(f32[384,256]{1,0:T(8,128)} %transpose_jvp___.1), channel_id=1, source_target_pairs={{0,32},{32,0},{64,96},{96,64},{128,160},{160,128},{192,224},{224,1... | collective-permute-start | bytes 1179656 | tf_op jit(solution)/shard_map/ppermute | solution.py:231
  101.0 5.2 %collective-permute-start.11 = (f32[288,128]{1,0:T(8,128)S(1)}, f32[288,128]{1,0:T(8,128)S(1)}, u32[]{:S(2)}, u32[]{:S(2)}) collective-permute-start(f32[288,128]{1,0:T(8,128)S(1)} %add.353), channel_id=1, source_target_pairs={{0,8},{1,9},{2,10},{3,11},{4,12},{5,13},{6,14},{7,15},{8,0},{9,1},... | collective-permute-start | bytes 442376 | tf_op jit(solution)/shard_map/ppermute | solution.py:231
  106.2 7.1 %collective-permute-start.12 = (f32[288,128]{1,0:T(8,128)S(1)}, f32[288,128]{1,0:T(8,128)}, u32[]{:S(2)}, u32[]{:S(2)}) collective-permute-start(f32[288,128]{1,0:T(8,128)S(1)} %add.354), channel_id=1, source_target_pairs={{0,16},{1,17},{2,18},{3,19},{4,20},{5,21},{6,22},{7,23},{8,24},{9,... | collective-permute-start | bytes 442376 | tf_op jit(solution)/shard_map/ppermute | solution.py:231
  112.2 11.3 %collective-permute-start.14 = (f32[384,256]{1,0:T(8,128)}, f32[384,256]{1,0:T(8,128)}, u32[]{:S(2)}, u32[]{:S(2)}) collective-permute-start(f32[384,256]{1,0:T(8,128)} %add.361), channel_id=1, source_target_pairs={{0,64},{32,96},{64,0},{96,32},{128,192},{160,224},{192,128},{224,1... | collective-permute-start | bytes 1179656 | tf_op jit(solution)/shard_map/ppermute | solution.py:231
  115.2 18.1 %copy-start.1 = (f32[384,256]{1,0:T(8,128)S(1)}, f32[384,256]{1,0:T(8,128)}, u32[]{:S(2)}) copy-start(f32[384,256]{1,0:T(8,128)} %copy.117.table_ref) | copy-start | bytes 1179652
  124.6 8.7 %collective-permute-start.15 = (f32[384,256]{1,0:T(8,128)S(1)}, f32[384,256]{1,0:T(8,128)S(1)}, u32[]{:S(2)}, u32[]{:S(2)}) collective-permute-start(f32[384,256]{1,0:T(8,128)S(1)} %add.362), channel_id=1, source_target_pairs={{0,128},{32,160},{64,192},{96,224},{128,0},{160,32},{192,64},{224,... | collective-permute-start | bytes 1179656 | tf_op jit(solution)/shard_map/ppermute | solution.py:231
  134.3 16.1 %copy-start.10 = (f32[1,48,256]{2,1,0:T(8,128)S(1)}, f32[1,48,256]{2,1,0:T(8,128)}, u32[]{:S(2)}) copy-start(f32[1,48,256]{2,1,0:T(8,128)} %copy-done.9) | copy-start | bytes 147460
  (17 other events, 84.1 us)

commit v6 on v4

--- a/solution.py
+++ b/solution.py
@@ -254,7 +254,7 @@
     point_block = gather_pts(points)
     residual, pullback = jax.vjp(residuals, camera_block, point_block)
     cotangent = residual * (reweight(residual) * valid_mask)
-    camera_grad, point_grad = pullback(cotangent)
+    camera_grad, point_grad = lax.optimization_barrier(pullback(cotangent))
     camera_grad = butterfly_sum(
         camera_grad.reshape(cam_rows * n_pt, cam_cols), "pt", n_pt
     ).reshape(cam_rows, n_pt * cam_cols)

time: 141 us -> 148 us (1.050)
  local copies, waits for them, and re-layouts: 23.9 us -> 26.2 us
  other arithmetic: 11.4 us -> 13.2 us
  starting transfers between devices: 40.5 us -> 42.2 us
    unnamed x72 -> x94, local copies, waits for them, and re-layouts: 6.48 us -> 8.54 us
    ppermute x8, starting transfers between devices: 13.9 us -> 15.6 us  [butterfly_sum(): value = value + lax.ppermute(value, axis_name, pairs)]
  transfers between devices with their start and end apart: 22 -> 22, of which waited for: 9 -> 9; matrix products, arithmetic and copies ran while one was open for 19% -> 21% of each run, Pallas kernels for 17% -> 17%
where the time goes in v6:
time: 148 us; the launch traced here: 146 us
  starting transfers between devices  42.2 us (29%)
  Pallas kernels  36 us (24%)
  waiting for transfers between devices  26.3 us (18%)
  local copies, waits for them, and re-layouts  26.2 us (18%)
  other arithmetic  13.2 us (9%)
  between operations  1.76 us (1%)
    ppermute x14, starting transfers between devices, doubling_gather(): other = lax.ppermute(buf, axis_name, pairs)  26.6 us
    pallas_call x2, Pallas kernels, gather_points(): pl.pallas_call(_gather_kernel, grid=(slots // blk,), in_specs=[pl.BlockSp...  23.8 us
    ppermute x8, waiting for transfers between devices, butterfly_sum(): value = value + lax.ppermute(value, axis_name, pairs)  20.7 us
    ppermute x8, starting transfers between devices, butterfly_sum(): value = value + lax.ppermute(value, axis_name, pairs)  15.6 us
    pallas_call x1, Pallas kernels, residuals(): take_points(point_block, point_index, point_block.shape[1])  12.2 us
    unnamed x94, local copies, waits for them, and re-layouts  8.54 us
    ppermute x14, waiting for transfers between devices, doubling_gather(): other = lax.ppermute(buf, axis_name, pairs)  5.6 us
    dynamic_slice x3, local copies, waits for them, and re-layouts, own_cams(): return lax.dynamic_slice_in_dim(block, start, cam_cols, axis=1)  3.21 us
  transfers between devices with their start and end apart: 22, of which 9 were waited for; matrix products, arithmetic and copies ran while one was open for 21% of the time, Pallas kernels for 17%

profile of v6, /device:TPU:6, one launch (start us, length us, event | category | flops | bytes accessed | tf_op | source)
XLA Modules:
  0.0 145.7 jit_solution(17792199139152105781)
XLA Ops:
  10.1 3.4 %collective-permute-start.1 = (f32[2,27,128]{2,0,1:T(2,128)S(1)}, f32[2,27,128]{2,0,1:T(2,128)S(1)}, u32[]{:S(2)}, u32[]{:S(2)}) collective-permute-start(f32[2,27,128]{2,0,1:T(2,128)S(1)} %maximum_select_fusion.19), channel_id=1, source_target_pairs={{0,2},{1,3},{2,0},{3,1},{4,6},{5,7},{6,4},{7,5},{8,10},{9,11},{10,... | collective-permute-start | bytes 82952 | tf_op jit(solution)/shard_map/ppermute | solution.py:217
  15.3 6.9 %collective-permute-start.2 = (f32[4,27,128]{2,0,1:T(4,128)S(1)}, f32[4,27,128]{2,0,1:T(4,128)S(1)}, u32[]{:S(2)}, u32[]{:S(2)}) collective-permute-start(f32[4,27,128]{2,0,1:T(4,128)S(1)} %maximum_select_fusion.18), channel_id=1, source_target_pairs={{0,4},{1,5},{2,6},{3,7},{4,0},{5,1},{6,2},{7,3},{8,12},{9,13},{10,... | collective-permute-start | bytes 165896 | tf_op jit(solution)/shard_map/ppermute | solution.py:217
  24.5 1.7 %collective-permute-start.3 = (f32[8,27,128]{2,0,1:T(8,128)S(1)}, f32[8,27,128]{2,0,1:T(8,128)S(1)}, u32[]{:S(2)}, u32[]{:S(2)}) collective-permute-start(f32[8,27,128]{2,0,1:T(8,128)S(1)} %maximum_select_fusion.11), channel_id=1, source_target_pairs={{0,8},{1,9},{2,10},{3,11},{4,12},{5,13},{6,14},{7,15},{8,0},{9,1},... | collective-permute-start | bytes 331784 | tf_op jit(solution)/shard_map/ppermute | solution.py:217
  26.2 2.3 %collective-permute-done.6 = f32[2,96,128]{2,1,0:T(8,128)S(1)} collective-permute-done((f32[2,96,128]{2,1,0:T(8,128)S(1)}, f32[2,96,128]{2,1,0:T(8,128)S(1)}, u32[]{:S(2)}, u32[]{:S(2)}) %collective-permute-start.6) | collective-permute-done | bytes 98336 | tf_op jit(solution)/shard_map/ppermute | solution.py:217
  29.7 3.3 %collective-permute-start.4 = (f32[16,27,128]{2,0,1:T(8,128)S(1)}, f32[16,27,128]{2,0,1:T(8,128)S(1)}, u32[]{:S(2)}, u32[]{:S(2)}) collective-permute-start(f32[16,27,128]{2,0,1:T(8,128)S(1)} %maximum_select_fusion.4), channel_id=1, source_target_pairs={{0,16},{1,17},{2,18},{3,19},{4,20},{5,21},{6,22},{7,23},{8,24},{9,... | collective-permute-start | bytes 663560 | tf_op jit(solution)/shard_map/ppermute | solution.py:217
  33.0 1.3 collective-permute-done.7
  35.5 11.9 %jvp__.1 = f32[3,12288]{1,0:T(4,128)} custom-call(f32[384,256]{1,0:T(8,128)} %copy.121.table_ref, s32[1,12288]{1,0:T(1,128)} %bitcast.320), custom_call_target="tpu_custom_call" | custom-call | tf_op jit(solution)/shard_map/jvp()/pallas_call | solution.py:58
  47.4 2.1 %slice_reduce_fusion.5 = (f32[12288]{0:T(1024)S(1)}, f32[12288]{0:T(1024)S(1)}, f32[12288]{0:T(1024)S(1)}, f32[1,12288]{1,0:T(1,128)S(1)}, f32[1,12288]{1,0:T(1,...) fusion(f32[3,12288]{1,0:T(4,128)} %jvp__.1, ...), kind=kLoop, calls=%fused_computation.219 | loop fusion | bytes 737280 | tf_op jit(solution)/shard_map/jvp()/slice | solution.py:146
  54.3 1.4 scatter_custom_fusion
  56.5 12.2 %transpose_jvp___.1 = f32[384,256]{1,0:T(8,128)} custom-call(f32[3,12288]{1,0:T(4,128)} %bitcast.319, s32[1,12288]{1,0:T(1,128)} %bitcast.321), custom_call_target="tpu_custom_call" | custom-call | tf_op jit(solution)/shard_map/transpose(jvp())/pallas_call | solution.py:203
  71.5 1.7 %collective-permute-start.9 = (f32[288,128]{1,0:T(8,128)S(1)}, f32[288,128]{1,0:T(8,128)S(1)}, u32[]{:S(2)}, u32[]{:S(2)}) collective-permute-start(f32[288,128]{1,0:T(8,128)S(1)} %add.357), channel_id=1, source_target_pairs={{0,2},{1,3},{2,0},{3,1},{4,6},{5,7},{6,4},{7,5},{8,10},{9,11},{10,... | collective-permute-start | bytes 442376 | tf_op jit(solution)/shard_map/ppermute | solution.py:231
  73.2 2.5 %collective-permute-start.20 = (f32[2,96,128]{2,1,0:T(8,128)S(1)}, f32[2,96,128]{2,1,0:T(8,128)S(1)}, u32[]{:S(2)}, u32[]{:S(2)}) collective-permute-start(f32[2,96,128]{2,1,0:T(8,128)S(1)} %maximum_select_fusion.17), channel_id=1, source_target_pairs={{0,64},{32,96},{64,0},{96,32},{128,192},{160,224},{192,128},{224,1... | collective-permute-start | bytes 294920 | tf_op jit(solution)/shard_map/ppermute | solution.py:217
  75.7 5.9 %collective-permute-done.9 = f32[288,128]{1,0:T(8,128)S(1)} collective-permute-done((f32[288,128]{1,0:T(8,128)S(1)}, f32[288,128]{1,0:T(8,128)S(1)}, u32[]{:S(2)}, u32[]{:S(2)}) %collective-permute-start.9) | collective-permute-done | bytes 147488 | tf_op jit(solution)/shard_map/ppermute | solution.py:231
  81.6 5.2 %collective-permute-start.10 = (f32[288,128]{1,0:T(8,128)S(1)}, f32[288,128]{1,0:T(8,128)S(1)}, u32[]{:S(2)}, u32[]{:S(2)}) collective-permute-start(f32[288,128]{1,0:T(8,128)S(1)} %add.358), channel_id=1, source_target_pairs={{0,4},{1,5},{2,6},{3,7},{4,0},{5,1},{6,2},{7,3},{8,12},{9,13},{10,... | collective-permute-start | bytes 442376 | tf_op jit(solution)/shard_map/ppermute | solution.py:231
  87.0 2.1 %collective-permute-start.21 = (f32[4,96,128]{2,1,0:T(8,128)S(1)}, f32[4,96,128]{2,1,0:T(8,128)S(1)}, u32[]{:S(2)}, u32[]{:S(2)}) collective-permute-start(f32[4,96,128]{2,1,0:T(8,128)S(1)} %maximum_select_fusion.10), channel_id=1, source_target_pairs={{0,128},{32,160},{64,192},{96,224},{128,0},{160,32},{192,64},{224,... | collective-permute-start | bytes 589832 | tf_op jit(solution)/shard_map/ppermute | solution.py:217
  90.0 5.0 %collective-permute-done.10 = f32[288,128]{1,0:T(8,128)S(1)} collective-permute-done((f32[288,128]{1,0:T(8,128)S(1)}, f32[288,128]{1,0:T(8,128)S(1)}, u32[]{:S(2)}, u32[]{:S(2)}) %collective-permute-start.10) | collective-permute-done | bytes 147488 | tf_op jit(solution)/shard_map/ppermute | solution.py:231
  95.0 2.2 %collective-permute-start.11 = (f32[288,128]{1,0:T(8,128)S(1)}, f32[288,128]{1,0:T(8,128)S(1)}, u32[]{:S(2)}, u32[]{:S(2)}) collective-permute-start(f32[288,128]{1,0:T(8,128)S(1)} %add.359), channel_id=1, source_target_pairs={{0,8},{1,9},{2,10},{3,11},{4,12},{5,13},{6,14},{7,15},{8,0},{9,1},... | collective-permute-start | bytes 442376 | tf_op jit(solution)/shard_map/ppermute | solution.py:231
  97.2 3.1 %collective-permute-done.11 = f32[288,128]{1,0:T(8,128)S(1)} collective-permute-done((f32[288,128]{1,0:T(8,128)S(1)}, f32[288,128]{1,0:T(8,128)S(1)}, u32[]{:S(2)}, u32[]{:S(2)}) %collective-permute-start.11) | collective-permute-done | bytes 147488 | tf_op jit(solution)/shard_map/ppermute | solution.py:231
  100.3 2.8 %collective-permute-start.12 = (f32[288,128]{1,0:T(8,128)S(1)}, f32[288,128]{1,0:T(8,128)}, u32[]{:S(2)}, u32[]{:S(2)}) collective-permute-start(f32[288,128]{1,0:T(8,128)S(1)} %add.360), channel_id=1, source_target_pairs={{0,16},{1,17},{2,18},{3,19},{4,20},{5,21},{6,22},{7,23},{8,24},{9,... | collective-permute-start | bytes 442376 | tf_op jit(solution)/shard_map/ppermute | solution.py:231
  105.6 2.4 %collective-permute-start.17 = (f32[384,256]{1,0:T(8,128)}, f32[384,256]{1,0:T(8,128)}, u32[]{:S(2)}, u32[]{:S(2)}) collective-permute-start(f32[384,256]{1,0:T(8,128)} %add.367), channel_id=1, source_target_pairs={{0,64},{32,96},{64,0},{96,32},{128,192},{160,224},{192,128},{224,1... | collective-permute-start | bytes 1179656 | tf_op jit(solution)/shard_map/ppermute | solution.py:231
  118.4 1.3 constant_dynamic-slice_fusion.4
  119.7 1.3 constant_dynamic-slice_fusion.3
  121.1 6.0 %collective-permute-done.18 = f32[384,256]{1,0:T(8,128)S(1)} collective-permute-done((f32[384,256]{1,0:T(8,128)S(1)}, f32[384,256]{1,0:T(8,128)S(1)}, u32[]{:S(2)}, u32[]{:S(2)}) %collective-permute-start.18) | collective-permute-done | bytes 393248 | tf_op jit(solution)/shard_map/ppermute | solution.py:231
  128.0 11.9 %shard_map.161 = f32[3,12288]{1,0:T(4,128)} custom-call(f32[384,256]{1,0:T(8,128)} %copy-done.2, s32[1,12288]{1,0:T(1,128)} %bitcast.322), custom_call_target="tpu_custom_call" | custom-call | tf_op jit(solution)/shard_map/pallas_call | solution.py:58
  (233 shorter events, 44.2 us)
Async XLA Ops:
  1.4 8.7 %collective-permute-start = (f32[1,27,128]{2,0,1:T(1,128)S(1)}, f32[1,27,128]{2,0,1:T(1,128)S(1)}, u32[]{:S(2)}, u32[]{:S(2)}) collective-permute-start(f32[1,27,128]{2,0,1:T(1,128)S(1)} %broadcast_in_dim.24), channel_id=1, source_target_pairs={{0,1},{1,0},{2,3},{3,2},{4,5},{5,4},{6,7},{7,6},{8,9},{9,8},{10,11... | collective-permute-start | bytes 41480 | tf_op jit(solution)/shard_map/ppermute | solution.py:217
  2.4 19.9 %collective-permute-start.5 = (f32[1,96,128]{2,1,0:T(8,128)S(1)}, f32[1,96,128]{2,1,0:T(8,128)S(1)}, u32[]{:S(2)}, u32[]{:S(2)}) collective-permute-start(f32[1,96,128]{2,1,0:T(8,128)S(1)} %broadcast_in_dim_reshape.9), channel_id=1, source_target_pairs={{0,32},{32,0},{64,96},{96,64},{128,160},{160,128},{192,224},{224,1... | collective-permute-start | bytes 147464 | tf_op jit(solution)/shard_map/ppermute | solution.py:217
  4.2 66.1 %collective-permute-start.13 = (f32[1,96,128]{2,1,0:T(8,128)S(1)}, f32[1,96,128]{2,1,0:T(8,128)S(1)}, u32[]{:S(2)}, u32[]{:S(2)}) collective-permute-start(f32[1,96,128]{2,1,0:T(8,128)S(1)} %broadcast_in_dim_reshape.10), channel_id=1, source_target_pairs={{0,32},{32,0},{64,96},{96,64},{128,160},{160,128},{192,224},{224,1... | collective-permute-start | bytes 147464 | tf_op jit(solution)/shard_map/ppermute | solution.py:217
  6.3 66.9 %collective-permute-start.19 = (f32[1,96,128]{2,1,0:T(8,128)S(1)}, f32[1,96,128]{2,1,0:T(8,128)S(1)}, u32[]{:S(2)}, u32[]{:S(2)}) collective-permute-start(f32[1,96,128]{2,1,0:T(8,128)S(1)} %broadcast_in_dim_reshape.11), channel_id=1, source_target_pairs={{0,32},{32,0},{64,96},{96,64},{128,160},{160,128},{192,224},{224,1... | collective-permute-start | bytes 147464 | tf_op jit(solution)/shard_map/ppermute | solution.py:217
  10.1 5.2 %collective-permute-start.1 = (f32[2,27,128]{2,0,1:T(2,128)S(1)}, f32[2,27,128]{2,0,1:T(2,128)S(1)}, u32[]{:S(2)}, u32[]{:S(2)}) collective-permute-start(f32[2,27,128]{2,0,1:T(2,128)S(1)} %maximum_select_fusion.19), channel_id=1, source_target_pairs={{0,2},{1,3},{2,0},{3,1},{4,6},{5,7},{6,4},{7,5},{8,10},{9,11},{10,... | collective-permute-start | bytes 82952 | tf_op jit(solution)/shard_map/ppermute | solution.py:217
  15.3 9.2 %collective-permute-start.2 = (f32[4,27,128]{2,0,1:T(4,128)S(1)}, f32[4,27,128]{2,0,1:T(4,128)S(1)}, u32[]{:S(2)}, u32[]{:S(2)}) collective-permute-start(f32[4,27,128]{2,0,1:T(4,128)S(1)} %maximum_select_fusion.18), channel_id=1, source_target_pairs={{0,4},{1,5},{2,6},{3,7},{4,0},{5,1},{6,2},{7,3},{8,12},{9,13},{10,... | collective-permute-start | bytes 165896 | tf_op jit(solution)/shard_map/ppermute | solution.py:217
  22.3 6.2 %collective-permute-start.6 = (f32[2,96,128]{2,1,0:T(8,128)S(1)}, f32[2,96,128]{2,1,0:T(8,128)S(1)}, u32[]{:S(2)}, u32[]{:S(2)}) collective-permute-start(f32[2,96,128]{2,1,0:T(8,128)S(1)} %maximum_select_fusion.13), channel_id=1, source_target_pairs={{0,64},{32,96},{64,0},{96,32},{128,192},{160,224},{192,128},{224,1... | collective-permute-start | bytes 294920 | tf_op jit(solution)/shard_map/ppermute | solution.py:217
  24.5 5.1 %collective-permute-start.3 = (f32[8,27,128]{2,0,1:T(8,128)S(1)}, f32[8,27,128]{2,0,1:T(8,128)S(1)}, u32[]{:S(2)}, u32[]{:S(2)}) collective-permute-start(f32[8,27,128]{2,0,1:T(8,128)S(1)} %maximum_select_fusion.11), channel_id=1, source_target_pairs={{0,8},{1,9},{2,10},{3,11},{4,12},{5,13},{6,14},{7,15},{8,0},{9,1},... | collective-permute-start | bytes 331784 | tf_op jit(solution)/shard_map/ppermute | solution.py:217
  28.5 5.8 %collective-permute-start.7 = (f32[4,96,128]{2,1,0:T(8,128)S(1)}, f32[4,96,128]{2,1,0:T(8,128)S(1)}, u32[]{:S(2)}, u32[]{:S(2)}) collective-permute-start(f32[4,96,128]{2,1,0:T(8,128)S(1)} %maximum_select_fusion.6), channel_id=1, source_target_pairs={{0,128},{32,160},{64,192},{96,224},{128,0},{160,32},{192,64},{224,... | collective-permute-start | bytes 589832 | tf_op jit(solution)/shard_map/ppermute | solution.py:217
  29.7 17.8 %copy-start.21 = (f32[2,12288]{1,0:T(2,128)S(1)}, f32[2,12288]{1,0:T(2,128)}, u32[]{:S(2)}) copy-start(f32[2,12288]{1,0:T(2,128)} %param.16) | copy-start | bytes 294916
  29.7 20.1 %collective-permute-start.4 = (f32[16,27,128]{2,0,1:T(8,128)S(1)}, f32[16,27,128]{2,0,1:T(8,128)S(1)}, u32[]{:S(2)}, u32[]{:S(2)}) collective-permute-start(f32[16,27,128]{2,0,1:T(8,128)S(1)} %maximum_select_fusion.4), channel_id=1, source_target_pairs={{0,16},{1,17},{2,18},{3,19},{4,20},{5,21},{6,22},{7,23},{8,24},{9,... | collective-permute-start | bytes 663560 | tf_op jit(solution)/shard_map/ppermute | solution.py:217
  69.4 19.7 %copy-start.4 = (f32[384,256]{1,0:T(8,128)S(1)}, f32[384,256]{1,0:T(8,128)}, u32[]{:S(2)}) copy-start(f32[384,256]{1,0:T(8,128)} %transpose_jvp___.1) | copy-start | bytes 1179652
  69.4 2.1 %collective-permute-start.8 = (f32[288,128]{1,0:T(8,128)S(1)}, f32[288,128]{1,0:T(8,128)S(1)}, u32[]{:S(2)}, u32[]{:S(2)}) collective-permute-start(f32[288,128]{1,0:T(8,128)S(1)} %reshape.1219), channel_id=1, source_target_pairs={{0,1},{1,0},{2,3},{3,2},{4,5},{5,4},{6,7},{7,6},{8,9},{9,8},{10,11... | collective-permute-start | bytes 442376 | tf_op jit(solution)/shard_map/ppermute | solution.py:231
  70.3 16.6 %collective-permute-start.14 = (f32[2,96,128]{2,1,0:T(8,128)S(1)}, f32[2,96,128]{2,1,0:T(8,128)S(1)}, u32[]{:S(2)}, u32[]{:S(2)}) collective-permute-start(f32[2,96,128]{2,1,0:T(8,128)S(1)} %maximum_select_fusion.15), channel_id=1, source_target_pairs={{0,64},{32,96},{64,0},{96,32},{128,192},{160,224},{192,128},{224,1... | collective-permute-start | bytes 294920 | tf_op jit(solution)/shard_map/ppermute | solution.py:217
  71.5 10.1 %collective-permute-start.9 = (f32[288,128]{1,0:T(8,128)S(1)}, f32[288,128]{1,0:T(8,128)S(1)}, u32[]{:S(2)}, u32[]{:S(2)}) collective-permute-start(f32[288,128]{1,0:T(8,128)S(1)} %add.357), channel_id=1, source_target_pairs={{0,2},{1,3},{2,0},{3,1},{4,6},{5,7},{6,4},{7,5},{8,10},{9,11},{10,... | collective-permute-start | bytes 442376 | tf_op jit(solution)/shard_map/ppermute | solution.py:231
  73.2 13.8 %collective-permute-start.20 = (f32[2,96,128]{2,1,0:T(8,128)S(1)}, f32[2,96,128]{2,1,0:T(8,128)S(1)}, u32[]{:S(2)}, u32[]{:S(2)}) collective-permute-start(f32[2,96,128]{2,1,0:T(8,128)S(1)} %maximum_select_fusion.17), channel_id=1, source_target_pairs={{0,64},{32,96},{64,0},{96,32},{128,192},{160,224},{192,128},{224,1... | collective-permute-start | bytes 294920 | tf_op jit(solution)/shard_map/ppermute | solution.py:217
  81.6 13.3 %collective-permute-start.10 = (f32[288,128]{1,0:T(8,128)S(1)}, f32[288,128]{1,0:T(8,128)S(1)}, u32[]{:S(2)}, u32[]{:S(2)}) collective-permute-start(f32[288,128]{1,0:T(8,128)S(1)} %add.358), channel_id=1, source_target_pairs={{0,4},{1,5},{2,6},{3,7},{4,0},{5,1},{6,2},{7,3},{8,12},{9,13},{10,... | collective-permute-start | bytes 442376 | tf_op jit(solution)/shard_map/ppermute | solution.py:231
  86.9 16.3 %collective-permute-start.15 = (f32[4,96,128]{2,1,0:T(8,128)S(1)}, f32[4,96,128]{2,1,0:T(8,128)S(1)}, u32[]{:S(2)}, u32[]{:S(2)}) collective-permute-start(f32[4,96,128]{2,1,0:T(8,128)S(1)} %maximum_select_fusion.8), channel_id=1, source_target_pairs={{0,128},{32,160},{64,192},{96,224},{128,0},{160,32},{192,64},{224,... | collective-permute-start | bytes 589832 | tf_op jit(solution)/shard_map/ppermute | solution.py:217
  87.0 16.7 %collective-permute-start.21 = (f32[4,96,128]{2,1,0:T(8,128)S(1)}, f32[4,96,128]{2,1,0:T(8,128)S(1)}, u32[]{:S(2)}, u32[]{:S(2)}) collective-permute-start(f32[4,96,128]{2,1,0:T(8,128)S(1)} %maximum_select_fusion.10), channel_id=1, source_target_pairs={{0,128},{32,160},{64,192},{96,224},{128,0},{160,32},{192,64},{224,... | collective-permute-start | bytes 589832 | tf_op jit(solution)/shard_map/ppermute | solution.py:217
  89.1 15.7 %collective-permute-start.16 = (f32[384,256]{1,0:T(8,128)S(1)}, f32[384,256]{1,0:T(8,128)S(1)}, u32[]{:S(2)}, u32[]{:S(2)}) collective-permute-start(f32[384,256]{1,0:T(8,128)S(1)} %copy-done.4), channel_id=1, source_target_pairs={{0,32},{32,0},{64,96},{96,64},{128,160},{160,128},{192,224},{224,1... | collective-permute-start | bytes 1179656 | tf_op jit(solution)/shard_map/ppermute | solution.py:231
  95.0 5.3 %collective-permute-start.11 = (f32[288,128]{1,0:T(8,128)S(1)}, f32[288,128]{1,0:T(8,128)S(1)}, u32[]{:S(2)}, u32[]{:S(2)}) collective-permute-start(f32[288,128]{1,0:T(8,128)S(1)} %add.359), channel_id=1, source_target_pairs={{0,8},{1,9},{2,10},{3,11},{4,12},{5,13},{6,14},{7,15},{8,0},{9,1},... | collective-permute-start | bytes 442376 | tf_op jit(solution)/shard_map/ppermute | solution.py:231
  100.3 7.7 %collective-permute-start.12 = (f32[288,128]{1,0:T(8,128)S(1)}, f32[288,128]{1,0:T(8,128)}, u32[]{:S(2)}, u32[]{:S(2)}) collective-permute-start(f32[288,128]{1,0:T(8,128)S(1)} %add.360), channel_id=1, source_target_pairs={{0,16},{1,17},{2,18},{3,19},{4,20},{5,21},{6,22},{7,23},{8,24},{9,... | collective-permute-start | bytes 442376 | tf_op jit(solution)/shard_map/ppermute | solution.py:231
  105.6 11.3 %collective-permute-start.17 = (f32[384,256]{1,0:T(8,128)}, f32[384,256]{1,0:T(8,128)}, u32[]{:S(2)}, u32[]{:S(2)}) collective-permute-start(f32[384,256]{1,0:T(8,128)} %add.367), channel_id=1, source_target_pairs={{0,64},{32,96},{64,0},{96,32},{128,192},{160,224},{192,128},{224,1... | collective-permute-start | bytes 1179656 | tf_op jit(solution)/shard_map/ppermute | solution.py:231
  118.1 8.9 %collective-permute-start.18 = (f32[384,256]{1,0:T(8,128)S(1)}, f32[384,256]{1,0:T(8,128)S(1)}, u32[]{:S(2)}, u32[]{:S(2)}) collective-permute-start(f32[384,256]{1,0:T(8,128)S(1)} %add.368), channel_id=1, source_target_pairs={{0,128},{32,160},{64,192},{96,224},{128,0},{160,32},{192,64},{224,... | collective-permute-start | bytes 1179656 | tf_op jit(solution)/shard_map/ppermute | solution.py:231
  (28 other events, 116.5 us)

commit v7 on v5

--- a/solution.py
+++ b/solution.py
@@ -252,9 +252,7 @@
     cam_state = doubling_gather(cam_state, "pt", n_pt)
     cam_state = cam_state.transpose(1, 0, 2).reshape(3, cam_rows, n_pt * cam_cols)
     camera_block, first_block, second_block = cam_state[0], cam_state[1], cam_state[2]
-    pt_state = gather_pts(jnp.concatenate([points, pt_first, pt_second], axis=0))
-    pt_state = pt_state.reshape(3, pt_rows * LANES, pt_state.shape[1])
-    point_block, pt_first_block, pt_second_block = pt_state[0], pt_state[1], pt_state[2]
+    point_block = gather_pts(points)
     residual, pullback = jax.vjp(residuals, camera_block, point_block)
     cotangent = residual * (reweight(residual) * valid_mask)
     camera_grad, point_grad = pullback(cotangent)
@@ -265,8 +263,10 @@
     new_cam_block, new_cam_first, new_cam_second = adam_step(
         camera_block, first_block, second_block, camera_grad
     )
+    moments = gather_pts(jnp.concatenate([pt_first, pt_second], axis=0))
+    moments = moments.reshape(2, pt_rows * LANES, moments.shape[1])
     new_pt_block, new_pt_first, new_pt_second = adam_step(
-        point_block, pt_first_block, pt_second_block, point_grad
+        point_block, moments[0], moments[1], point_grad
     )
     new_cameras = own_cams(new_cam_block)
     new_cam_first = own_cams(new_cam_first)

time: 156 us -> 140 us (0.90)
  waiting for transfers between devices: 42 us -> 27.7 us
  other arithmetic: 18.5 us -> 13.2 us
  starting transfers between devices: 32.8 us -> 35.4 us
    ppermute x8 -> x11, waiting for transfers between devices: 20.6 us -> 10.3 us  [doubling_gather(): other = lax.ppermute(buf, axis_name, pairs)]
    ppermute x8, waiting for transfers between devices: 21.4 us -> 17.4 us  [butterfly_sum(): value = value + lax.ppermute(value, axis_name, pairs)]
    ppermute x8 -> x11, starting transfers between devices: 19.4 us -> 22.9 us  [doubling_gather(): other = lax.ppermute(buf, axis_name, pairs)]
    reduce_sum x2, other arithmetic: 2.2 us -> 0.27 us  [project(): inner = jnp.sum(axis_angle * point_obs, axis=0)]
    add x7, other arithmetic: 3.95 us -> 2.05 us  [butterfly_sum(): value = value + lax.ppermute(value, axis_name, pairs)]
    unnamed x82 -> x69, local copies, waits for them, and re-layouts: 8.17 us -> 6.49 us
  transfers between devices with their start and end apart: 16 -> 19, of which waited for: 13 -> 10; matrix products, arithmetic and copies ran while one was open for 14% -> 21% of each run, Pallas kernels for 8% -> 18%
where the time goes in v7:
time: 140 us; the launch traced here: 138 us
  Pallas kernels  36.1 us (26%)
  starting transfers between devices  35.4 us (25%)
  waiting for transfers between devices  27.7 us (20%)
  local copies, waits for them, and re-layouts  24.1 us (17%)
  other arithmetic  13.2 us (9%)
  between operations  1.59 us (1%)
    pallas_call x2, Pallas kernels, gather_points(): pl.pallas_call(_gather_kernel, grid=(slots // blk,), in_specs=[pl.BlockSp...  23.8 us
    ppermute x11, starting transfers between devices, doubling_gather(): other = lax.ppermute(buf, axis_name, pairs)  22.9 us
    ppermute x8, waiting for transfers between devices, butterfly_sum(): value = value + lax.ppermute(value, axis_name, pairs)  17.4 us
    ppermute x8, starting transfers between devices, butterfly_sum(): value = value + lax.ppermute(value, axis_name, pairs)  12.5 us
    pallas_call x1, Pallas kernels, residuals(): take_points(point_block, point_index, point_block.shape[1])  12.3 us
    ppermute x11, waiting for transfers between devices, doubling_gather(): other = lax.ppermute(buf, axis_name, pairs)  10.3 us
    unnamed x69, local copies, waits for them, and re-layouts  6.49 us
    dynamic_slice x3, local copies, waits for them, and re-layouts, own_cams(): return lax.dynamic_slice_in_dim(block, start, cam_cols, axis=1)  3.91 us
  transfers between devices with their start and end apart: 19, of which 10 were waited for; matrix products, arithmetic and copies ran while one was open for 21% of the time, Pallas kernels for 18%

profile of v7, /device:TPU:6, one launch (start us, length us, event | category | flops | bytes accessed | tf_op | source)
XLA Modules:
  0.0 138.0 jit_solution(6437004932478397829)
XLA Ops:
  6.9 3.4 %collective-permute-start.1 = (f32[2,27,128]{2,0,1:T(2,128)S(1)}, f32[2,27,128]{2,0,1:T(2,128)S(1)}, u32[]{:S(2)}, u32[]{:S(2)}) collective-permute-start(f32[2,27,128]{2,0,1:T(2,128)S(1)} %maximum_select_fusion.14), channel_id=1, source_target_pairs={{0,2},{1,3},{2,0},{3,1},{4,6},{5,7},{6,4},{7,5},{8,10},{9,11},{10,... | collective-permute-start | bytes 82952 | tf_op jit(solution)/shard_map/ppermute | solution.py:217
  12.2 6.9 %collective-permute-start.2 = (f32[4,27,128]{2,0,1:T(4,128)S(1)}, f32[4,27,128]{2,0,1:T(4,128)S(1)}, u32[]{:S(2)}, u32[]{:S(2)}) collective-permute-start(f32[4,27,128]{2,0,1:T(4,128)S(1)} %maximum_select_fusion.13), channel_id=1, source_target_pairs={{0,4},{1,5},{2,6},{3,7},{4,0},{5,1},{6,2},{7,3},{8,12},{9,13},{10,... | collective-permute-start | bytes 165896 | tf_op jit(solution)/shard_map/ppermute | solution.py:217
  19.1 1.5 %collective-permute-start.6 = (f32[2,96,128]{2,1,0:T(8,128)S(1)}, f32[2,96,128]{2,1,0:T(8,128)S(1)}, u32[]{:S(2)}, u32[]{:S(2)}) collective-permute-start(f32[2,96,128]{2,1,0:T(8,128)S(1)} %maximum_select_fusion.12), channel_id=1, source_target_pairs={{0,64},{32,96},{64,0},{96,32},{128,192},{160,224},{192,128},{224,1... | collective-permute-start | bytes 294920 | tf_op jit(solution)/shard_map/ppermute | solution.py:217
  21.4 1.7 %collective-permute-start.3 = (f32[8,27,128]{2,0,1:T(8,128)S(1)}, f32[8,27,128]{2,0,1:T(8,128)S(1)}, u32[]{:S(2)}, u32[]{:S(2)}) collective-permute-start(f32[8,27,128]{2,0,1:T(8,128)S(1)} %maximum_select_fusion.10), channel_id=1, source_target_pairs={{0,8},{1,9},{2,10},{3,11},{4,12},{5,13},{6,14},{7,15},{8,0},{9,1},... | collective-permute-start | bytes 331784 | tf_op jit(solution)/shard_map/ppermute | solution.py:217
  23.0 2.3 %collective-permute-done.6 = f32[2,96,128]{2,1,0:T(8,128)S(1)} collective-permute-done((f32[2,96,128]{2,1,0:T(8,128)S(1)}, f32[2,96,128]{2,1,0:T(8,128)S(1)}, u32[]{:S(2)}, u32[]{:S(2)}) %collective-permute-start.6) | collective-permute-done | bytes 98336 | tf_op jit(solution)/shard_map/ppermute | solution.py:217
  26.5 3.3 %collective-permute-start.4 = (f32[16,27,128]{2,0,1:T(8,128)S(1)}, f32[16,27,128]{2,0,1:T(8,128)S(1)}, u32[]{:S(2)}, u32[]{:S(2)}) collective-permute-start(f32[16,27,128]{2,0,1:T(8,128)S(1)} %maximum_select_fusion.5), channel_id=1, source_target_pairs={{0,16},{1,17},{2,18},{3,19},{4,20},{5,21},{6,22},{7,23},{8,24},{9,... | collective-permute-start | bytes 663560 | tf_op jit(solution)/shard_map/ppermute | solution.py:217
  32.4 11.9 %jvp__.1 = f32[3,12288]{1,0:T(4,128)} custom-call(f32[384,256]{1,0:T(8,128)} %copy.119.table_ref, s32[1,12288]{1,0:T(1,128)} %bitcast.312), custom_call_target="tpu_custom_call" | custom-call | tf_op jit(solution)/shard_map/jvp()/pallas_call | solution.py:58
  44.3 2.1 %slice_reduce_fusion.5 = (f32[12288]{0:T(1024)S(1)}, f32[12288]{0:T(1024)S(1)}, f32[12288]{0:T(1024)S(1)}, f32[1,12288]{1,0:T(1,128)S(1)}, f32[1,12288]{1,0:T(1,...) fusion(f32[3,12288]{1,0:T(4,128)} %jvp__.1, ...), kind=kLoop, calls=%fused_computation.214 | loop fusion | bytes 737280 | tf_op jit(solution)/shard_map/jvp()/slice | solution.py:146
  55.9 1.7 %collective-permute-start.14 = (f32[2,192,128]{2,1,0:T(8,128)S(1)}, f32[2,192,128]{2,1,0:T(8,128)S(1)}, u32[]{:S(2)}, u32[]{:S(2)}) collective-permute-start(f32[2,192,128]{2,1,0:T(8,128)S(1)} %maximum_select_fusion.9), channel_id=1, source_target_pairs={{0,64},{32,96},{64,0},{96,32},{128,192},{160,224},{192,128},{224,1... | collective-permute-start | bytes 589832 | tf_op jit(solution)/shard_map/ppermute | solution.py:217
  57.6 1.6 %collective-permute-start.9 = (f32[288,128]{1,0:T(8,128)S(1)}, f32[288,128]{1,0:T(8,128)S(1)}, u32[]{:S(2)}, u32[]{:S(2)}) collective-permute-start(f32[288,128]{1,0:T(8,128)S(1)} %add.354), channel_id=1, source_target_pairs={{0,2},{1,3},{2,0},{3,1},{4,6},{5,7},{6,4},{7,5},{8,10},{9,11},{10,... | collective-permute-start | bytes 442376 | tf_op jit(solution)/shard_map/ppermute | solution.py:231
  59.9 5.0 %collective-permute-done.14 = f32[2,192,128]{2,1,0:T(8,128)S(1)} collective-permute-done((f32[2,192,128]{2,1,0:T(8,128)S(1)}, f32[2,192,128]{2,1,0:T(8,128)S(1)}, u32[]{:S(2)}, u32[]{:S(2)}) %collective-permute-start.14) | collective-permute-done | bytes 196640 | tf_op jit(solution)/shard_map/ppermute | solution.py:217
  66.1 1.6 %collective-permute-done.9 = f32[288,128]{1,0:T(8,128)S(1)} collective-permute-done((f32[288,128]{1,0:T(8,128)S(1)}, f32[288,128]{1,0:T(8,128)S(1)}, u32[]{:S(2)}, u32[]{:S(2)}) %collective-permute-start.9) | collective-permute-done | bytes 147488 | tf_op jit(solution)/shard_map/ppermute | solution.py:231
  67.7 4.9 %collective-permute-start.10 = (f32[288,128]{1,0:T(8,128)S(1)}, f32[288,128]{1,0:T(8,128)S(1)}, u32[]{:S(2)}, u32[]{:S(2)}) collective-permute-start(f32[288,128]{1,0:T(8,128)S(1)} %add.355), channel_id=1, source_target_pairs={{0,4},{1,5},{2,6},{3,7},{4,0},{5,1},{6,2},{7,3},{8,12},{9,13},{10,... | collective-permute-start | bytes 442376 | tf_op jit(solution)/shard_map/ppermute | solution.py:231
  74.2 12.3 %transpose_jvp___.1 = f32[384,256]{1,0:T(8,128)} custom-call(f32[3,12288]{1,0:T(4,128)} %bitcast.311, s32[1,12288]{1,0:T(1,128)} %bitcast.313), custom_call_target="tpu_custom_call" | custom-call | tf_op jit(solution)/shard_map/transpose(jvp())/pallas_call | solution.py:203
  86.8 1.5 %collective-permute-start.11 = (f32[288,128]{1,0:T(8,128)S(1)}, f32[288,128]{1,0:T(8,128)S(1)}, u32[]{:S(2)}, u32[]{:S(2)}) collective-permute-start(f32[288,128]{1,0:T(8,128)S(1)} %add.356), channel_id=1, source_target_pairs={{0,8},{1,9},{2,10},{3,11},{4,12},{5,13},{6,14},{7,15},{8,0},{9,1},... | collective-permute-start | bytes 442376 | tf_op jit(solution)/shard_map/ppermute | solution.py:231
  88.8 3.2 %collective-permute-done.11 = f32[288,128]{1,0:T(8,128)S(1)} collective-permute-done((f32[288,128]{1,0:T(8,128)S(1)}, f32[288,128]{1,0:T(8,128)S(1)}, u32[]{:S(2)}, u32[]{:S(2)}) %collective-permute-start.11) | collective-permute-done | bytes 147488 | tf_op jit(solution)/shard_map/ppermute | solution.py:231
  92.0 1.8 %collective-permute-start.12 = (f32[288,128]{1,0:T(8,128)S(1)}, f32[288,128]{1,0:T(8,128)S(1)}, u32[]{:S(2)}, u32[]{:S(2)}) collective-permute-start(f32[288,128]{1,0:T(8,128)S(1)} %add.357), channel_id=1, source_target_pairs={{0,16},{1,17},{2,18},{3,19},{4,20},{5,21},{6,22},{7,23},{8,24},{9,... | collective-permute-start | bytes 442376 | tf_op jit(solution)/shard_map/ppermute | solution.py:231
  95.0 2.2 %collective-permute-done.16 = f32[384,256]{1,0:T(8,128)S(1)} collective-permute-done((f32[384,256]{1,0:T(8,128)}, f32[384,256]{1,0:T(8,128)S(1)}, u32[]{:S(2)}, u32[]{:S(2)}) %collective-permute-start.16) | collective-permute-done | bytes 393248 | tf_op jit(solution)/shard_map/ppermute | solution.py:231
  98.0 2.1 %collective-permute-start.17 = (f32[384,256]{1,0:T(8,128)}, f32[384,256]{1,0:T(8,128)}, u32[]{:S(2)}, u32[]{:S(2)}) collective-permute-start(f32[384,256]{1,0:T(8,128)} %add.364), channel_id=1, source_target_pairs={{0,64},{32,96},{64,0},{96,32},{128,192},{160,224},{192,128},{224,1... | collective-permute-start | bytes 1179656 | tf_op jit(solution)/shard_map/ppermute | solution.py:231
  101.1 1.6 %copy.142 = f32[9,4096]{0,1:T(8,128)S(1)} copy(f32[9,4096]{1,0:T(8,128)} %get-tuple-element.63) | data formatting | bytes 294912 | tf_op jit(solution)/shard_map/sub | solution.py:177
  105.3 4.2 %collective-permute-done.17 = f32[384,256]{1,0:T(8,128)} collective-permute-done((f32[384,256]{1,0:T(8,128)}, f32[384,256]{1,0:T(8,128)}, u32[]{:S(2)}, u32[]{:S(2)}) %collective-permute-start.17) | collective-permute-done | bytes 393248 | tf_op jit(solution)/shard_map/ppermute | solution.py:231
  112.0 1.3 constant_dynamic-slice_fusion.3
  113.3 6.2 %collective-permute-done.18 = f32[384,256]{1,0:T(8,128)S(1)} collective-permute-done((f32[384,256]{1,0:T(8,128)S(1)}, f32[384,256]{1,0:T(8,128)S(1)}, u32[]{:S(2)}, u32[]{:S(2)}) %collective-permute-start.18) | collective-permute-done | bytes 393248 | tf_op jit(solution)/shard_map/ppermute | solution.py:231
  120.5 11.9 %shard_map.161 = f32[3,12288]{1,0:T(4,128)} custom-call(f32[384,256]{1,0:T(8,128)} %copy-done.2, s32[1,12288]{1,0:T(1,128)} %bitcast.314), custom_call_target="tpu_custom_call" | custom-call | tf_op jit(solution)/shard_map/pallas_call | solution.py:58
  (199 shorter events, 40.3 us)
Async XLA Ops:
  1.4 5.5 %collective-permute-start = (f32[1,27,128]{2,0,1:T(1,128)S(1)}, f32[1,27,128]{2,0,1:T(1,128)S(1)}, u32[]{:S(2)}, u32[]{:S(2)}) collective-permute-start(f32[1,27,128]{2,0,1:T(1,128)S(1)} %broadcast_in_dim.24), channel_id=1, source_target_pairs={{0,1},{1,0},{2,3},{3,2},{4,5},{5,4},{6,7},{7,6},{8,9},{9,8},{10,11... | collective-permute-start | bytes 41480 | tf_op jit(solution)/shard_map/ppermute | solution.py:217
  2.4 16.7 %collective-permute-start.5 = (f32[1,96,128]{2,1,0:T(8,128)S(1)}, f32[1,96,128]{2,1,0:T(8,128)S(1)}, u32[]{:S(2)}, u32[]{:S(2)}) collective-permute-start(f32[1,96,128]{2,1,0:T(8,128)S(1)} %broadcast_in_dim_reshape.6), channel_id=1, source_target_pairs={{0,32},{32,0},{64,96},{96,64},{128,160},{160,128},{192,224},{224,1... | collective-permute-start | bytes 147464 | tf_op jit(solution)/shard_map/ppermute | solution.py:217
  4.3 51.6 %collective-permute-start.13 = (f32[1,192,128]{2,1,0:T(8,128)S(1)}, f32[1,192,128]{2,1,0:T(8,128)S(1)}, u32[]{:S(2)}, u32[]{:S(2)}) collective-permute-start(f32[1,192,128]{2,1,0:T(8,128)S(1)} %broadcast_in_dim_reshape.7), channel_id=1, source_target_pairs={{0,32},{32,0},{64,96},{96,64},{128,160},{160,128},{192,224},{224,1... | collective-permute-start | bytes 294920 | tf_op jit(solution)/shard_map/ppermute | solution.py:217
  6.9 5.2 %collective-permute-start.1 = (f32[2,27,128]{2,0,1:T(2,128)S(1)}, f32[2,27,128]{2,0,1:T(2,128)S(1)}, u32[]{:S(2)}, u32[]{:S(2)}) collective-permute-start(f32[2,27,128]{2,0,1:T(2,128)S(1)} %maximum_select_fusion.14), channel_id=1, source_target_pairs={{0,2},{1,3},{2,0},{3,1},{4,6},{5,7},{6,4},{7,5},{8,10},{9,11},{10,... | collective-permute-start | bytes 82952 | tf_op jit(solution)/shard_map/ppermute | solution.py:217
  12.2 9.2 %collective-permute-start.2 = (f32[4,27,128]{2,0,1:T(4,128)S(1)}, f32[4,27,128]{2,0,1:T(4,128)S(1)}, u32[]{:S(2)}, u32[]{:S(2)}) collective-permute-start(f32[4,27,128]{2,0,1:T(4,128)S(1)} %maximum_select_fusion.13), channel_id=1, source_target_pairs={{0,4},{1,5},{2,6},{3,7},{4,0},{5,1},{6,2},{7,3},{8,12},{9,13},{10,... | collective-permute-start | bytes 165896 | tf_op jit(solution)/shard_map/ppermute | solution.py:217
  19.1 6.2 %collective-permute-start.6 = (f32[2,96,128]{2,1,0:T(8,128)S(1)}, f32[2,96,128]{2,1,0:T(8,128)S(1)}, u32[]{:S(2)}, u32[]{:S(2)}) collective-permute-start(f32[2,96,128]{2,1,0:T(8,128)S(1)} %maximum_select_fusion.12), channel_id=1, source_target_pairs={{0,64},{32,96},{64,0},{96,32},{128,192},{160,224},{192,128},{224,1... | collective-permute-start | bytes 294920 | tf_op jit(solution)/shard_map/ppermute | solution.py:217
  21.4 5.1 %collective-permute-start.3 = (f32[8,27,128]{2,0,1:T(8,128)S(1)}, f32[8,27,128]{2,0,1:T(8,128)S(1)}, u32[]{:S(2)}, u32[]{:S(2)}) collective-permute-start(f32[8,27,128]{2,0,1:T(8,128)S(1)} %maximum_select_fusion.10), channel_id=1, source_target_pairs={{0,8},{1,9},{2,10},{3,11},{4,12},{5,13},{6,14},{7,15},{8,0},{9,1},... | collective-permute-start | bytes 331784 | tf_op jit(solution)/shard_map/ppermute | solution.py:217
  25.3 5.8 %collective-permute-start.7 = (f32[4,96,128]{2,1,0:T(8,128)S(1)}, f32[4,96,128]{2,1,0:T(8,128)S(1)}, u32[]{:S(2)}, u32[]{:S(2)}) collective-permute-start(f32[4,96,128]{2,1,0:T(8,128)S(1)} %maximum_select_fusion.7), channel_id=1, source_target_pairs={{0,128},{32,160},{64,192},{96,224},{128,0},{160,32},{192,64},{224,... | collective-permute-start | bytes 589832 | tf_op jit(solution)/shard_map/ppermute | solution.py:217
  26.5 17.8 %copy-start.16 = (f32[2,12288]{1,0:T(2,128)S(1)}, f32[2,12288]{1,0:T(2,128)}, u32[]{:S(2)}) copy-start(f32[2,12288]{1,0:T(2,128)} %param.16) | copy-start | bytes 294916
  26.5 22.5 %collective-permute-start.4 = (f32[16,27,128]{2,0,1:T(8,128)S(1)}, f32[16,27,128]{2,0,1:T(8,128)S(1)}, u32[]{:S(2)}, u32[]{:S(2)}) collective-permute-start(f32[16,27,128]{2,0,1:T(8,128)S(1)} %maximum_select_fusion.5), channel_id=1, source_target_pairs={{0,16},{1,17},{2,18},{3,19},{4,20},{5,21},{6,22},{7,23},{8,24},{9,... | collective-permute-start | bytes 663560 | tf_op jit(solution)/shard_map/ppermute | solution.py:217
  48.3 3.8 %copy-start.7 = (f32[1,48,256]{2,1,0:T(8,128)}, f32[1,48,256]{2,1,0:T(8,128)S(1)}, u32[]{:S(2)}) copy-start(f32[1,48,256]{2,1,0:T(8,128)S(1)} %squeeze.42) | copy-start | bytes 147460
  48.3 3.8 %copy-start.9 = (f32[1,48,256]{2,1,0:T(8,128)}, f32[1,48,256]{2,1,0:T(8,128)S(1)}, u32[]{:S(2)}) copy-start(f32[1,48,256]{2,1,0:T(8,128)S(1)} %squeeze.43) | copy-start | bytes 147460
  55.7 1.9 %collective-permute-start.8 = (f32[288,128]{1,0:T(8,128)S(1)}, f32[288,128]{1,0:T(8,128)S(1)}, u32[]{:S(2)}, u32[]{:S(2)}) collective-permute-start(f32[288,128]{1,0:T(8,128)S(1)} %reshape.1205), channel_id=1, source_target_pairs={{0,1},{1,0},{2,3},{3,2},{4,5},{5,4},{6,7},{7,6},{8,9},{9,8},{10,11... | collective-permute-start | bytes 442376 | tf_op jit(solution)/shard_map/ppermute | solution.py:231
  55.8 17.6 %copy-start.5 = (s32[6,2,8,128]{3,1,2,0:T(2,128)}, s32[6,2,8,128]{3,1,2,0:T(2,128)S(1)}, u32[]{:S(2)}) copy-start(s32[6,2,8,128]{3,1,2,0:T(2,128)S(1)} %copy.162) | copy-start | bytes 147460
  55.9 9.1 %collective-permute-start.14 = (f32[2,192,128]{2,1,0:T(8,128)S(1)}, f32[2,192,128]{2,1,0:T(8,128)S(1)}, u32[]{:S(2)}, u32[]{:S(2)}) collective-permute-start(f32[2,192,128]{2,1,0:T(8,128)S(1)} %maximum_select_fusion.9), channel_id=1, source_target_pairs={{0,64},{32,96},{64,0},{96,32},{128,192},{160,224},{192,128},{224,1... | collective-permute-start | bytes 589832 | tf_op jit(solution)/shard_map/ppermute | solution.py:217
  57.6 10.1 %collective-permute-start.9 = (f32[288,128]{1,0:T(8,128)S(1)}, f32[288,128]{1,0:T(8,128)S(1)}, u32[]{:S(2)}, u32[]{:S(2)}) collective-permute-start(f32[288,128]{1,0:T(8,128)S(1)} %add.354), channel_id=1, source_target_pairs={{0,2},{1,3},{2,0},{3,1},{4,6},{5,7},{6,4},{7,5},{8,10},{9,11},{10,... | collective-permute-start | bytes 442376 | tf_op jit(solution)/shard_map/ppermute | solution.py:231
  65.0 23.7 %collective-permute-start.15 = (f32[4,192,128]{2,1,0:T(8,128)S(1)}, f32[4,192,128]{2,1,0:T(8,128)S(1)}, u32[]{:S(2)}, u32[]{:S(2)}) collective-permute-start(f32[4,192,128]{2,1,0:T(8,128)S(1)} %maximum_select_fusion.4), channel_id=1, source_target_pairs={{0,128},{32,160},{64,192},{96,224},{128,0},{160,32},{192,64},{224,... | collective-permute-start | bytes 1179656 | tf_op jit(solution)/shard_map/ppermute | solution.py:217
  67.7 19.0 %collective-permute-start.10 = (f32[288,128]{1,0:T(8,128)S(1)}, f32[288,128]{1,0:T(8,128)S(1)}, u32[]{:S(2)}, u32[]{:S(2)}) collective-permute-start(f32[288,128]{1,0:T(8,128)S(1)} %add.355), channel_id=1, source_target_pairs={{0,4},{1,5},{2,6},{3,7},{4,0},{5,1},{6,2},{7,3},{8,12},{9,13},{10,... | collective-permute-start | bytes 442376 | tf_op jit(solution)/shard_map/ppermute | solution.py:231
  86.5 10.7 %collective-permute-start.16 = (f32[384,256]{1,0:T(8,128)}, f32[384,256]{1,0:T(8,128)S(1)}, u32[]{:S(2)}, u32[]{:S(2)}) collective-permute-start(f32[384,256]{1,0:T(8,128)} %transpose_jvp___.1), channel_id=1, source_target_pairs={{0,32},{32,0},{64,96},{96,64},{128,160},{160,128},{192,224},{224,1... | collective-permute-start | bytes 1179656 | tf_op jit(solution)/shard_map/ppermute | solution.py:231
  86.8 5.2 %collective-permute-start.11 = (f32[288,128]{1,0:T(8,128)S(1)}, f32[288,128]{1,0:T(8,128)S(1)}, u32[]{:S(2)}, u32[]{:S(2)}) collective-permute-start(f32[288,128]{1,0:T(8,128)S(1)} %add.356), channel_id=1, source_target_pairs={{0,8},{1,9},{2,10},{3,11},{4,12},{5,13},{6,14},{7,15},{8,0},{9,1},... | collective-permute-start | bytes 442376 | tf_op jit(solution)/shard_map/ppermute | solution.py:231
  92.0 8.1 %collective-permute-start.12 = (f32[288,128]{1,0:T(8,128)S(1)}, f32[288,128]{1,0:T(8,128)S(1)}, u32[]{:S(2)}, u32[]{:S(2)}) collective-permute-start(f32[288,128]{1,0:T(8,128)S(1)} %add.357), channel_id=1, source_target_pairs={{0,16},{1,17},{2,18},{3,19},{4,20},{5,21},{6,22},{7,23},{8,24},{9,... | collective-permute-start | bytes 442376 | tf_op jit(solution)/shard_map/ppermute | solution.py:231
  98.0 11.5 %collective-permute-start.17 = (f32[384,256]{1,0:T(8,128)}, f32[384,256]{1,0:T(8,128)}, u32[]{:S(2)}, u32[]{:S(2)}) collective-permute-start(f32[384,256]{1,0:T(8,128)} %add.364), channel_id=1, source_target_pairs={{0,64},{32,96},{64,0},{96,32},{128,192},{160,224},{192,128},{224,1... | collective-permute-start | bytes 1179656 | tf_op jit(solution)/shard_map/ppermute | solution.py:231
  101.1 18.4 %copy-start.1 = (f32[384,256]{1,0:T(8,128)S(1)}, f32[384,256]{1,0:T(8,128)}, u32[]{:S(2)}) copy-start(f32[384,256]{1,0:T(8,128)} %copy.119.table_ref) | copy-start | bytes 1179652
  110.6 8.9 %collective-permute-start.18 = (f32[384,256]{1,0:T(8,128)S(1)}, f32[384,256]{1,0:T(8,128)S(1)}, u32[]{:S(2)}, u32[]{:S(2)}) collective-permute-start(f32[384,256]{1,0:T(8,128)S(1)} %add.365), channel_id=1, source_target_pairs={{0,128},{32,160},{64,192},{96,224},{128,0},{160,32},{192,64},{224,... | collective-permute-start | bytes 1179656 | tf_op jit(solution)/shard_map/ppermute | solution.py:231
  (13 other events, 31.2 us)

commit v8 on v7

--- a/solution.py
+++ b/solution.py
@@ -12,7 +12,7 @@
 from jax.experimental.pallas import tpu as pltpu
 
 LANES = 128
-SLOT_BLK = 1024
+SLOT_BLK = 2048
 
 
 def _split3(x):

time: 140 us -> 137 us (0.979)
  Pallas kernels: 36.1 us -> 32.9 us
    pallas_call x2, Pallas kernels: 23.8 us -> 21.9 us  [gather_points(): pl.pallas_call(_gather_kernel, grid=(slots // blk,), in_specs=[pl.BlockSp...]
  transfers between devices with their start and end apart: 19 -> 19, of which waited for: 10 -> 10; matrix products, arithmetic and copies ran while one was open for 21% -> 21% of each run, Pallas kernels for 18% -> 16%
where the time goes in v8:
time: 137 us; the launch traced here: 135 us
  starting transfers between devices  35.8 us (26%)
  Pallas kernels  32.9 us (24%)
  waiting for transfers between devices  27.6 us (20%)
  local copies, waits for them, and re-layouts  24.1 us (18%)
  other arithmetic  13.2 us (10%)
  between operations  1.59 us (1%)
    ppermute x11, starting transfers between devices, doubling_gather(): other = lax.ppermute(buf, axis_name, pairs)  22.7 us
    pallas_call x2, Pallas kernels, gather_points(): pl.pallas_call(_gather_kernel, grid=(slots // blk,), in_specs=[pl.BlockSp...  21.9 us
    ppermute x8, waiting for transfers between devices, butterfly_sum(): value = value + lax.ppermute(value, axis_name, pairs)  17.3 us
    ppermute x8, starting transfers between devices, butterfly_sum(): value = value + lax.ppermute(value, axis_name, pairs)  13.1 us
    pallas_call x1, Pallas kernels, residuals(): take_points(point_block, point_index, point_block.shape[1])  11 us
    ppermute x11, waiting for transfers between devices, doubling_gather(): other = lax.ppermute(buf, axis_name, pairs)  10.3 us
    unnamed x69, local copies, waits for them, and re-layouts  6.49 us
    dynamic_slice x3, local copies, waits for them, and re-layouts, own_cams(): return lax.dynamic_slice_in_dim(block, start, cam_cols, axis=1)  3.91 us
  transfers between devices with their start and end apart: 19, of which 10 were waited for; matrix products, arithmetic and copies ran while one was open for 21% of the time, Pallas kernels for 16%

profile of v8, /device:TPU:6, one launch (start us, length us, event | category | flops | bytes accessed | tf_op | source)
XLA Modules:
  0.0 135.2 jit_solution(13455188822551901944)
XLA Ops:
  6.9 3.4 %collective-permute-start.1 = (f32[2,27,128]{2,0,1:T(2,128)S(1)}, f32[2,27,128]{2,0,1:T(2,128)S(1)}, u32[]{:S(2)}, u32[]{:S(2)}) collective-permute-start(f32[2,27,128]{2,0,1:T(2,128)S(1)} %maximum_select_fusion.14), channel_id=1, source_target_pairs={{0,2},{1,3},{2,0},{3,1},{4,6},{5,7},{6,4},{7,5},{8,10},{9,11},{10,... | collective-permute-start | bytes 82952 | tf_op jit(solution)/shard_map/ppermute | solution.py:217
  12.2 6.9 %collective-permute-start.2 = (f32[4,27,128]{2,0,1:T(4,128)S(1)}, f32[4,27,128]{2,0,1:T(4,128)S(1)}, u32[]{:S(2)}, u32[]{:S(2)}) collective-permute-start(f32[4,27,128]{2,0,1:T(4,128)S(1)} %maximum_select_fusion.13), channel_id=1, source_target_pairs={{0,4},{1,5},{2,6},{3,7},{4,0},{5,1},{6,2},{7,3},{8,12},{9,13},{10,... | collective-permute-start | bytes 165896 | tf_op jit(solution)/shard_map/ppermute | solution.py:217
  19.1 1.5 %collective-permute-start.6 = (f32[2,96,128]{2,1,0:T(8,128)S(1)}, f32[2,96,128]{2,1,0:T(8,128)S(1)}, u32[]{:S(2)}, u32[]{:S(2)}) collective-permute-start(f32[2,96,128]{2,1,0:T(8,128)S(1)} %maximum_select_fusion.12), channel_id=1, source_target_pairs={{0,64},{32,96},{64,0},{96,32},{128,192},{160,224},{192,128},{224,1... | collective-permute-start | bytes 294920 | tf_op jit(solution)/shard_map/ppermute | solution.py:217
  21.4 1.7 %collective-permute-start.3 = (f32[8,27,128]{2,0,1:T(8,128)S(1)}, f32[8,27,128]{2,0,1:T(8,128)S(1)}, u32[]{:S(2)}, u32[]{:S(2)}) collective-permute-start(f32[8,27,128]{2,0,1:T(8,128)S(1)} %maximum_select_fusion.10), channel_id=1, source_target_pairs={{0,8},{1,9},{2,10},{3,11},{4,12},{5,13},{6,14},{7,15},{8,0},{9,1},... | collective-permute-start | bytes 331784 | tf_op jit(solution)/shard_map/ppermute | solution.py:217
  23.0 2.3 %collective-permute-done.6 = f32[2,96,128]{2,1,0:T(8,128)S(1)} collective-permute-done((f32[2,96,128]{2,1,0:T(8,128)S(1)}, f32[2,96,128]{2,1,0:T(8,128)S(1)}, u32[]{:S(2)}, u32[]{:S(2)}) %collective-permute-start.6) | collective-permute-done | bytes 98336 | tf_op jit(solution)/shard_map/ppermute | solution.py:217
  26.5 3.3 %collective-permute-start.4 = (f32[16,27,128]{2,0,1:T(8,128)S(1)}, f32[16,27,128]{2,0,1:T(8,128)S(1)}, u32[]{:S(2)}, u32[]{:S(2)}) collective-permute-start(f32[16,27,128]{2,0,1:T(8,128)S(1)} %maximum_select_fusion.5), channel_id=1, source_target_pairs={{0,16},{1,17},{2,18},{3,19},{4,20},{5,21},{6,22},{7,23},{8,24},{9,... | collective-permute-start | bytes 663560 | tf_op jit(solution)/shard_map/ppermute | solution.py:217
  32.4 10.9 %jvp__.1 = f32[3,12288]{1,0:T(4,128)} custom-call(f32[384,256]{1,0:T(8,128)} %copy.119.table_ref, s32[1,12288]{1,0:T(1,128)} %bitcast.312), custom_call_target="tpu_custom_call" | custom-call | tf_op jit(solution)/shard_map/jvp()/pallas_call | solution.py:58
  43.3 2.1 %slice_reduce_fusion.5 = (f32[12288]{0:T(1024)S(1)}, f32[12288]{0:T(1024)S(1)}, f32[12288]{0:T(1024)S(1)}, f32[1,12288]{1,0:T(1,128)S(1)}, f32[1,12288]{1,0:T(1,...) fusion(f32[3,12288]{1,0:T(4,128)} %jvp__.1, ...), kind=kLoop, calls=%fused_computation.214 | loop fusion | bytes 737280 | tf_op jit(solution)/shard_map/jvp()/slice | solution.py:146
  55.1 1.5 %collective-permute-start.14 = (f32[2,192,128]{2,1,0:T(8,128)S(1)}, f32[2,192,128]{2,1,0:T(8,128)S(1)}, u32[]{:S(2)}, u32[]{:S(2)}) collective-permute-start(f32[2,192,128]{2,1,0:T(8,128)S(1)} %maximum_select_fusion.9), channel_id=1, source_target_pairs={{0,64},{32,96},{64,0},{96,32},{128,192},{160,224},{192,128},{224,1... | collective-permute-start | bytes 589832 | tf_op jit(solution)/shard_map/ppermute | solution.py:217
  56.6 1.6 %collective-permute-start.9 = (f32[288,128]{1,0:T(8,128)S(1)}, f32[288,128]{1,0:T(8,128)S(1)}, u32[]{:S(2)}, u32[]{:S(2)}) collective-permute-start(f32[288,128]{1,0:T(8,128)S(1)} %add.354), channel_id=1, source_target_pairs={{0,2},{1,3},{2,0},{3,1},{4,6},{5,7},{6,4},{7,5},{8,10},{9,11},{10,... | collective-permute-start | bytes 442376 | tf_op jit(solution)/shard_map/ppermute | solution.py:231
  58.9 5.0 %collective-permute-done.14 = f32[2,192,128]{2,1,0:T(8,128)S(1)} collective-permute-done((f32[2,192,128]{2,1,0:T(8,128)S(1)}, f32[2,192,128]{2,1,0:T(8,128)S(1)}, u32[]{:S(2)}, u32[]{:S(2)}) %collective-permute-start.14) | collective-permute-done | bytes 196640 | tf_op jit(solution)/shard_map/ppermute | solution.py:217
  65.1 1.6 %collective-permute-done.9 = f32[288,128]{1,0:T(8,128)S(1)} collective-permute-done((f32[288,128]{1,0:T(8,128)S(1)}, f32[288,128]{1,0:T(8,128)S(1)}, u32[]{:S(2)}, u32[]{:S(2)}) %collective-permute-start.9) | collective-permute-done | bytes 147488 | tf_op jit(solution)/shard_map/ppermute | solution.py:231
  66.8 4.9 %collective-permute-start.10 = (f32[288,128]{1,0:T(8,128)S(1)}, f32[288,128]{1,0:T(8,128)S(1)}, u32[]{:S(2)}, u32[]{:S(2)}) collective-permute-start(f32[288,128]{1,0:T(8,128)S(1)} %add.355), channel_id=1, source_target_pairs={{0,4},{1,5},{2,6},{3,7},{4,0},{5,1},{6,2},{7,3},{8,12},{9,13},{10,... | collective-permute-start | bytes 442376 | tf_op jit(solution)/shard_map/ppermute | solution.py:231
  73.2 11.0 %transpose_jvp___.1 = f32[384,256]{1,0:T(8,128)} custom-call(f32[3,12288]{1,0:T(4,128)} %bitcast.311, s32[1,12288]{1,0:T(1,128)} %bitcast.313), custom_call_target="tpu_custom_call" | custom-call | tf_op jit(solution)/shard_map/transpose(jvp())/pallas_call | solution.py:203
  84.7 1.5 %collective-permute-start.11 = (f32[288,128]{1,0:T(8,128)S(1)}, f32[288,128]{1,0:T(8,128)S(1)}, u32[]{:S(2)}, u32[]{:S(2)}) collective-permute-start(f32[288,128]{1,0:T(8,128)S(1)} %add.356), channel_id=1, source_target_pairs={{0,8},{1,9},{2,10},{3,11},{4,12},{5,13},{6,14},{7,15},{8,0},{9,1},... | collective-permute-start | bytes 442376 | tf_op jit(solution)/shard_map/ppermute | solution.py:231
  86.8 3.2 %collective-permute-done.11 = f32[288,128]{1,0:T(8,128)S(1)} collective-permute-done((f32[288,128]{1,0:T(8,128)S(1)}, f32[288,128]{1,0:T(8,128)S(1)}, u32[]{:S(2)}, u32[]{:S(2)}) %collective-permute-start.11) | collective-permute-done | bytes 147488 | tf_op jit(solution)/shard_map/ppermute | solution.py:231
  90.0 1.8 %collective-permute-start.12 = (f32[288,128]{1,0:T(8,128)S(1)}, f32[288,128]{1,0:T(8,128)S(1)}, u32[]{:S(2)}, u32[]{:S(2)}) collective-permute-start(f32[288,128]{1,0:T(8,128)S(1)} %add.357), channel_id=1, source_target_pairs={{0,16},{1,17},{2,18},{3,19},{4,20},{5,21},{6,22},{7,23},{8,24},{9,... | collective-permute-start | bytes 442376 | tf_op jit(solution)/shard_map/ppermute | solution.py:231
  92.9 2.0 %collective-permute-done.16 = f32[384,256]{1,0:T(8,128)S(1)} collective-permute-done((f32[384,256]{1,0:T(8,128)}, f32[384,256]{1,0:T(8,128)S(1)}, u32[]{:S(2)}, u32[]{:S(2)}) %collective-permute-start.16) | collective-permute-done | bytes 393248 | tf_op jit(solution)/shard_map/ppermute | solution.py:231
  95.8 2.1 %collective-permute-start.17 = (f32[384,256]{1,0:T(8,128)}, f32[384,256]{1,0:T(8,128)}, u32[]{:S(2)}, u32[]{:S(2)}) collective-permute-start(f32[384,256]{1,0:T(8,128)} %add.364), channel_id=1, source_target_pairs={{0,64},{32,96},{64,0},{96,32},{128,192},{160,224},{192,128},{224,1... | collective-permute-start | bytes 1179656 | tf_op jit(solution)/shard_map/ppermute | solution.py:231
  98.9 1.6 %copy.142 = f32[9,4096]{0,1:T(8,128)S(1)} copy(f32[9,4096]{1,0:T(8,128)} %get-tuple-element.63) | data formatting | bytes 294912 | tf_op jit(solution)/shard_map/sub | solution.py:177
  103.1 4.2 %collective-permute-done.17 = f32[384,256]{1,0:T(8,128)} collective-permute-done((f32[384,256]{1,0:T(8,128)}, f32[384,256]{1,0:T(8,128)}, u32[]{:S(2)}, u32[]{:S(2)}) %collective-permute-start.17) | collective-permute-done | bytes 393248 | tf_op jit(solution)/shard_map/ppermute | solution.py:231
  110.1 1.3 constant_dynamic-slice_fusion.3
  111.4 6.2 %collective-permute-done.18 = f32[384,256]{1,0:T(8,128)S(1)} collective-permute-done((f32[384,256]{1,0:T(8,128)S(1)}, f32[384,256]{1,0:T(8,128)S(1)}, u32[]{:S(2)}, u32[]{:S(2)}) %collective-permute-start.18) | collective-permute-done | bytes 393248 | tf_op jit(solution)/shard_map/ppermute | solution.py:231
  118.6 10.9 %shard_map.161 = f32[3,12288]{1,0:T(4,128)} custom-call(f32[384,256]{1,0:T(8,128)} %copy-done.2, s32[1,12288]{1,0:T(1,128)} %bitcast.314), custom_call_target="tpu_custom_call" | custom-call | tf_op jit(solution)/shard_map/pallas_call | solution.py:58
  (199 shorter events, 40.9 us)
Async XLA Ops:
  1.4 5.5 %collective-permute-start = (f32[1,27,128]{2,0,1:T(1,128)S(1)}, f32[1,27,128]{2,0,1:T(1,128)S(1)}, u32[]{:S(2)}, u32[]{:S(2)}) collective-permute-start(f32[1,27,128]{2,0,1:T(1,128)S(1)} %broadcast_in_dim.24), channel_id=1, source_target_pairs={{0,1},{1,0},{2,3},{3,2},{4,5},{5,4},{6,7},{7,6},{8,9},{9,8},{10,11... | collective-permute-start | bytes 41480 | tf_op jit(solution)/shard_map/ppermute | solution.py:217
  2.4 16.7 %collective-permute-start.5 = (f32[1,96,128]{2,1,0:T(8,128)S(1)}, f32[1,96,128]{2,1,0:T(8,128)S(1)}, u32[]{:S(2)}, u32[]{:S(2)}) collective-permute-start(f32[1,96,128]{2,1,0:T(8,128)S(1)} %broadcast_in_dim_reshape.6), channel_id=1, source_target_pairs={{0,32},{32,0},{64,96},{96,64},{128,160},{160,128},{192,224},{224,1... | collective-permute-start | bytes 147464 | tf_op jit(solution)/shard_map/ppermute | solution.py:217
  4.3 50.8 %collective-permute-start.13 = (f32[1,192,128]{2,1,0:T(8,128)S(1)}, f32[1,192,128]{2,1,0:T(8,128)S(1)}, u32[]{:S(2)}, u32[]{:S(2)}) collective-permute-start(f32[1,192,128]{2,1,0:T(8,128)S(1)} %broadcast_in_dim_reshape.7), channel_id=1, source_target_pairs={{0,32},{32,0},{64,96},{96,64},{128,160},{160,128},{192,224},{224,1... | collective-permute-start | bytes 294920 | tf_op jit(solution)/shard_map/ppermute | solution.py:217
  6.9 5.2 %collective-permute-start.1 = (f32[2,27,128]{2,0,1:T(2,128)S(1)}, f32[2,27,128]{2,0,1:T(2,128)S(1)}, u32[]{:S(2)}, u32[]{:S(2)}) collective-permute-start(f32[2,27,128]{2,0,1:T(2,128)S(1)} %maximum_select_fusion.14), channel_id=1, source_target_pairs={{0,2},{1,3},{2,0},{3,1},{4,6},{5,7},{6,4},{7,5},{8,10},{9,11},{10,... | collective-permute-start | bytes 82952 | tf_op jit(solution)/shard_map/ppermute | solution.py:217
  12.2 9.2 %collective-permute-start.2 = (f32[4,27,128]{2,0,1:T(4,128)S(1)}, f32[4,27,128]{2,0,1:T(4,128)S(1)}, u32[]{:S(2)}, u32[]{:S(2)}) collective-permute-start(f32[4,27,128]{2,0,1:T(4,128)S(1)} %maximum_select_fusion.13), channel_id=1, source_target_pairs={{0,4},{1,5},{2,6},{3,7},{4,0},{5,1},{6,2},{7,3},{8,12},{9,13},{10,... | collective-permute-start | bytes 165896 | tf_op jit(solution)/shard_map/ppermute | solution.py:217
  19.1 6.2 %collective-permute-start.6 = (f32[2,96,128]{2,1,0:T(8,128)S(1)}, f32[2,96,128]{2,1,0:T(8,128)S(1)}, u32[]{:S(2)}, u32[]{:S(2)}) collective-permute-start(f32[2,96,128]{2,1,0:T(8,128)S(1)} %maximum_select_fusion.12), channel_id=1, source_target_pairs={{0,64},{32,96},{64,0},{96,32},{128,192},{160,224},{192,128},{224,1... | collective-permute-start | bytes 294920 | tf_op jit(solution)/shard_map/ppermute | solution.py:217
  21.4 5.1 %collective-permute-start.3 = (f32[8,27,128]{2,0,1:T(8,128)S(1)}, f32[8,27,128]{2,0,1:T(8,128)S(1)}, u32[]{:S(2)}, u32[]{:S(2)}) collective-permute-start(f32[8,27,128]{2,0,1:T(8,128)S(1)} %maximum_select_fusion.10), channel_id=1, source_target_pairs={{0,8},{1,9},{2,10},{3,11},{4,12},{5,13},{6,14},{7,15},{8,0},{9,1},... | collective-permute-start | bytes 331784 | tf_op jit(solution)/shard_map/ppermute | solution.py:217
  25.3 5.8 %collective-permute-start.7 = (f32[4,96,128]{2,1,0:T(8,128)S(1)}, f32[4,96,128]{2,1,0:T(8,128)S(1)}, u32[]{:S(2)}, u32[]{:S(2)}) collective-permute-start(f32[4,96,128]{2,1,0:T(8,128)S(1)} %maximum_select_fusion.7), channel_id=1, source_target_pairs={{0,128},{32,160},{64,192},{96,224},{128,0},{160,32},{192,64},{224,... | collective-permute-start | bytes 589832 | tf_op jit(solution)/shard_map/ppermute | solution.py:217
  26.5 16.8 %copy-start.16 = (f32[2,12288]{1,0:T(2,128)S(1)}, f32[2,12288]{1,0:T(2,128)}, u32[]{:S(2)}) copy-start(f32[2,12288]{1,0:T(2,128)} %param.16) | copy-start | bytes 294916
  26.5 21.5 %collective-permute-start.4 = (f32[16,27,128]{2,0,1:T(8,128)S(1)}, f32[16,27,128]{2,0,1:T(8,128)S(1)}, u32[]{:S(2)}, u32[]{:S(2)}) collective-permute-start(f32[16,27,128]{2,0,1:T(8,128)S(1)} %maximum_select_fusion.5), channel_id=1, source_target_pairs={{0,16},{1,17},{2,18},{3,19},{4,20},{5,21},{6,22},{7,23},{8,24},{9,... | collective-permute-start | bytes 663560 | tf_op jit(solution)/shard_map/ppermute | solution.py:217
  47.3 3.8 %copy-start.7 = (f32[1,48,256]{2,1,0:T(8,128)}, f32[1,48,256]{2,1,0:T(8,128)S(1)}, u32[]{:S(2)}) copy-start(f32[1,48,256]{2,1,0:T(8,128)S(1)} %squeeze.42) | copy-start | bytes 147460
  47.4 3.8 %copy-start.9 = (f32[1,48,256]{2,1,0:T(8,128)}, f32[1,48,256]{2,1,0:T(8,128)S(1)}, u32[]{:S(2)}) copy-start(f32[1,48,256]{2,1,0:T(8,128)S(1)} %squeeze.43) | copy-start | bytes 147460
  54.7 1.9 %collective-permute-start.8 = (f32[288,128]{1,0:T(8,128)S(1)}, f32[288,128]{1,0:T(8,128)S(1)}, u32[]{:S(2)}, u32[]{:S(2)}) collective-permute-start(f32[288,128]{1,0:T(8,128)S(1)} %reshape.1205), channel_id=1, source_target_pairs={{0,1},{1,0},{2,3},{3,2},{4,5},{5,4},{6,7},{7,6},{8,9},{9,8},{10,11... | collective-permute-start | bytes 442376 | tf_op jit(solution)/shard_map/ppermute | solution.py:231
  55.0 17.4 %copy-start.5 = (s32[6,2,8,128]{3,1,2,0:T(2,128)}, s32[6,2,8,128]{3,1,2,0:T(2,128)S(1)}, u32[]{:S(2)}) copy-start(s32[6,2,8,128]{3,1,2,0:T(2,128)S(1)} %copy.162) | copy-start | bytes 147460
  55.1 8.9 %collective-permute-start.14 = (f32[2,192,128]{2,1,0:T(8,128)S(1)}, f32[2,192,128]{2,1,0:T(8,128)S(1)}, u32[]{:S(2)}, u32[]{:S(2)}) collective-permute-start(f32[2,192,128]{2,1,0:T(8,128)S(1)} %maximum_select_fusion.9), channel_id=1, source_target_pairs={{0,64},{32,96},{64,0},{96,32},{128,192},{160,224},{192,128},{224,1... | collective-permute-start | bytes 589832 | tf_op jit(solution)/shard_map/ppermute | solution.py:217
  56.6 10.1 %collective-permute-start.9 = (f32[288,128]{1,0:T(8,128)S(1)}, f32[288,128]{1,0:T(8,128)S(1)}, u32[]{:S(2)}, u32[]{:S(2)}) collective-permute-start(f32[288,128]{1,0:T(8,128)S(1)} %add.354), channel_id=1, source_target_pairs={{0,2},{1,3},{2,0},{3,1},{4,6},{5,7},{6,4},{7,5},{8,10},{9,11},{10,... | collective-permute-start | bytes 442376 | tf_op jit(solution)/shard_map/ppermute | solution.py:231
  64.0 22.7 %collective-permute-start.15 = (f32[4,192,128]{2,1,0:T(8,128)S(1)}, f32[4,192,128]{2,1,0:T(8,128)S(1)}, u32[]{:S(2)}, u32[]{:S(2)}) collective-permute-start(f32[4,192,128]{2,1,0:T(8,128)S(1)} %maximum_select_fusion.4), channel_id=1, source_target_pairs={{0,128},{32,160},{64,192},{96,224},{128,0},{160,32},{192,64},{224,... | collective-permute-start | bytes 1179656 | tf_op jit(solution)/shard_map/ppermute | solution.py:217
  66.8 18.0 %collective-permute-start.10 = (f32[288,128]{1,0:T(8,128)S(1)}, f32[288,128]{1,0:T(8,128)S(1)}, u32[]{:S(2)}, u32[]{:S(2)}) collective-permute-start(f32[288,128]{1,0:T(8,128)S(1)} %add.355), channel_id=1, source_target_pairs={{0,4},{1,5},{2,6},{3,7},{4,0},{5,1},{6,2},{7,3},{8,12},{9,13},{10,... | collective-permute-start | bytes 442376 | tf_op jit(solution)/shard_map/ppermute | solution.py:231
  84.2 10.8 %collective-permute-start.16 = (f32[384,256]{1,0:T(8,128)}, f32[384,256]{1,0:T(8,128)S(1)}, u32[]{:S(2)}, u32[]{:S(2)}) collective-permute-start(f32[384,256]{1,0:T(8,128)} %transpose_jvp___.1), channel_id=1, source_target_pairs={{0,32},{32,0},{64,96},{96,64},{128,160},{160,128},{192,224},{224,1... | collective-permute-start | bytes 1179656 | tf_op jit(solution)/shard_map/ppermute | solution.py:231
  84.7 5.2 %collective-permute-start.11 = (f32[288,128]{1,0:T(8,128)S(1)}, f32[288,128]{1,0:T(8,128)S(1)}, u32[]{:S(2)}, u32[]{:S(2)}) collective-permute-start(f32[288,128]{1,0:T(8,128)S(1)} %add.356), channel_id=1, source_target_pairs={{0,8},{1,9},{2,10},{3,11},{4,12},{5,13},{6,14},{7,15},{8,0},{9,1},... | collective-permute-start | bytes 442376 | tf_op jit(solution)/shard_map/ppermute | solution.py:231
  90.0 7.9 %collective-permute-start.12 = (f32[288,128]{1,0:T(8,128)S(1)}, f32[288,128]{1,0:T(8,128)S(1)}, u32[]{:S(2)}, u32[]{:S(2)}) collective-permute-start(f32[288,128]{1,0:T(8,128)S(1)} %add.357), channel_id=1, source_target_pairs={{0,16},{1,17},{2,18},{3,19},{4,20},{5,21},{6,22},{7,23},{8,24},{9,... | collective-permute-start | bytes 442376 | tf_op jit(solution)/shard_map/ppermute | solution.py:231
  95.8 11.5 %collective-permute-start.17 = (f32[384,256]{1,0:T(8,128)}, f32[384,256]{1,0:T(8,128)}, u32[]{:S(2)}, u32[]{:S(2)}) collective-permute-start(f32[384,256]{1,0:T(8,128)} %add.364), channel_id=1, source_target_pairs={{0,64},{32,96},{64,0},{96,32},{128,192},{160,224},{192,128},{224,1... | collective-permute-start | bytes 1179656 | tf_op jit(solution)/shard_map/ppermute | solution.py:231
  98.9 18.7 %copy-start.1 = (f32[384,256]{1,0:T(8,128)S(1)}, f32[384,256]{1,0:T(8,128)}, u32[]{:S(2)}) copy-start(f32[384,256]{1,0:T(8,128)} %copy.119.table_ref) | copy-start | bytes 1179652
  108.4 9.1 %collective-permute-start.18 = (f32[384,256]{1,0:T(8,128)S(1)}, f32[384,256]{1,0:T(8,128)S(1)}, u32[]{:S(2)}, u32[]{:S(2)}) collective-permute-start(f32[384,256]{1,0:T(8,128)S(1)} %add.365), channel_id=1, source_target_pairs={{0,128},{32,160},{64,192},{96,224},{128,0},{160,32},{192,64},{224,... | collective-permute-start | bytes 1179656 | tf_op jit(solution)/shard_map/ppermute | solution.py:231
  (13 other events, 31.0 us)

commit v9 on v8

--- a/solution.py
+++ b/solution.py
@@ -12,7 +12,7 @@
 from jax.experimental.pallas import tpu as pltpu
 
 LANES = 128
-SLOT_BLK = 2048
+SLOT_BLK = 4096
 
 
 def _split3(x):

time: 137 us -> 135 us (0.985)
  Pallas kernels: 32.9 us -> 31.3 us
  transfers between devices with their start and end apart: 19 -> 19, of which waited for: 10 -> 10; matrix products, arithmetic and copies ran while one was open for 21% -> 22% of each run, Pallas kernels for 16% -> 16%
where the time goes in v9:
time: 135 us; the launch traced here: 134 us
  starting transfers between devices  36.3 us (27%)
  Pallas kernels  31.3 us (23%)
  waiting for transfers between devices  27.2 us (20%)
  local copies, waits for them, and re-layouts  24.1 us (18%)
  other arithmetic  13.2 us (10%)
  between operations  1.59 us (1%)
    ppermute x11, starting transfers between devices, doubling_gather(): other = lax.ppermute(buf, axis_name, pairs)  22.9 us
    pallas_call x2, Pallas kernels, gather_points(): pl.pallas_call(_gather_kernel, grid=(slots // blk,), in_specs=[pl.BlockSp...  21 us
    ppermute x8, waiting for transfers between devices, butterfly_sum(): value = value + lax.ppermute(value, axis_name, pairs)  17 us
    ppermute x8, starting transfers between devices, butterfly_sum(): value = value + lax.ppermute(value, axis_name, pairs)  13.4 us
    pallas_call x1, Pallas kernels, residuals(): take_points(point_block, point_index, point_block.shape[1])  10.3 us
    ppermute x11, waiting for transfers between devices, doubling_gather(): other = lax.ppermute(buf, axis_name, pairs)  10.1 us
    unnamed x69, local copies, waits for them, and re-layouts  6.49 us
    dynamic_slice x3, local copies, waits for them, and re-layouts, own_cams(): return lax.dynamic_slice_in_dim(block, start, cam_cols, axis=1)  3.91 us
  transfers between devices with their start and end apart: 19, of which 10 were waited for; matrix products, arithmetic and copies ran while one was open for 22% of the time, Pallas kernels for 16%

profile of v9, /device:TPU:6, one launch (start us, length us, event | category | flops | bytes accessed | tf_op | source)
XLA Modules:
  0.0 133.6 jit_solution(10106684455907203287)
XLA Ops:
  6.9 3.4 %collective-permute-start.1 = (f32[2,27,128]{2,0,1:T(2,128)S(1)}, f32[2,27,128]{2,0,1:T(2,128)S(1)}, u32[]{:S(2)}, u32[]{:S(2)}) collective-permute-start(f32[2,27,128]{2,0,1:T(2,128)S(1)} %maximum_select_fusion.14), channel_id=1, source_target_pairs={{0,2},{1,3},{2,0},{3,1},{4,6},{5,7},{6,4},{7,5},{8,10},{9,11},{10,... | collective-permute-start | bytes 82952 | tf_op jit(solution)/shard_map/ppermute | solution.py:217
  12.2 6.9 %collective-permute-start.2 = (f32[4,27,128]{2,0,1:T(4,128)S(1)}, f32[4,27,128]{2,0,1:T(4,128)S(1)}, u32[]{:S(2)}, u32[]{:S(2)}) collective-permute-start(f32[4,27,128]{2,0,1:T(4,128)S(1)} %maximum_select_fusion.13), channel_id=1, source_target_pairs={{0,4},{1,5},{2,6},{3,7},{4,0},{5,1},{6,2},{7,3},{8,12},{9,13},{10,... | collective-permute-start | bytes 165896 | tf_op jit(solution)/shard_map/ppermute | solution.py:217
  19.1 1.5 %collective-permute-start.6 = (f32[2,96,128]{2,1,0:T(8,128)S(1)}, f32[2,96,128]{2,1,0:T(8,128)S(1)}, u32[]{:S(2)}, u32[]{:S(2)}) collective-permute-start(f32[2,96,128]{2,1,0:T(8,128)S(1)} %maximum_select_fusion.12), channel_id=1, source_target_pairs={{0,64},{32,96},{64,0},{96,32},{128,192},{160,224},{192,128},{224,1... | collective-permute-start | bytes 294920 | tf_op jit(solution)/shard_map/ppermute | solution.py:217
  21.4 1.7 %collective-permute-start.3 = (f32[8,27,128]{2,0,1:T(8,128)S(1)}, f32[8,27,128]{2,0,1:T(8,128)S(1)}, u32[]{:S(2)}, u32[]{:S(2)}) collective-permute-start(f32[8,27,128]{2,0,1:T(8,128)S(1)} %maximum_select_fusion.10), channel_id=1, source_target_pairs={{0,8},{1,9},{2,10},{3,11},{4,12},{5,13},{6,14},{7,15},{8,0},{9,1},... | collective-permute-start | bytes 331784 | tf_op jit(solution)/shard_map/ppermute | solution.py:217
  23.0 2.3 %collective-permute-done.6 = f32[2,96,128]{2,1,0:T(8,128)S(1)} collective-permute-done((f32[2,96,128]{2,1,0:T(8,128)S(1)}, f32[2,96,128]{2,1,0:T(8,128)S(1)}, u32[]{:S(2)}, u32[]{:S(2)}) %collective-permute-start.6) | collective-permute-done | bytes 98336 | tf_op jit(solution)/shard_map/ppermute | solution.py:217
  26.5 3.5 %collective-permute-start.4 = (f32[16,27,128]{2,0,1:T(8,128)S(1)}, f32[16,27,128]{2,0,1:T(8,128)S(1)}, u32[]{:S(2)}, u32[]{:S(2)}) collective-permute-start(f32[16,27,128]{2,0,1:T(8,128)S(1)} %maximum_select_fusion.5), channel_id=1, source_target_pairs={{0,16},{1,17},{2,18},{3,19},{4,20},{5,21},{6,22},{7,23},{8,24},{9,... | collective-permute-start | bytes 663560 | tf_op jit(solution)/shard_map/ppermute | solution.py:217
  32.4 10.5 %jvp__.1 = f32[3,12288]{1,0:T(4,128)} custom-call(f32[384,256]{1,0:T(8,128)} %copy.119.table_ref, s32[1,12288]{1,0:T(1,128)} %bitcast.312), custom_call_target="tpu_custom_call" | custom-call | tf_op jit(solution)/shard_map/jvp()/pallas_call | solution.py:58
  42.8 2.1 %slice_reduce_fusion.5 = (f32[12288]{0:T(1024)S(1)}, f32[12288]{0:T(1024)S(1)}, f32[12288]{0:T(1024)S(1)}, f32[1,12288]{1,0:T(1,128)S(1)}, f32[1,12288]{1,0:T(1,...) fusion(f32[3,12288]{1,0:T(4,128)} %jvp__.1, ...), kind=kLoop, calls=%fused_computation.214 | loop fusion | bytes 737280 | tf_op jit(solution)/shard_map/jvp()/slice | solution.py:146
  54.4 1.5 %collective-permute-start.14 = (f32[2,192,128]{2,1,0:T(8,128)S(1)}, f32[2,192,128]{2,1,0:T(8,128)S(1)}, u32[]{:S(2)}, u32[]{:S(2)}) collective-permute-start(f32[2,192,128]{2,1,0:T(8,128)S(1)} %maximum_select_fusion.9), channel_id=1, source_target_pairs={{0,64},{32,96},{64,0},{96,32},{128,192},{160,224},{192,128},{224,1... | collective-permute-start | bytes 589832 | tf_op jit(solution)/shard_map/ppermute | solution.py:217
  56.0 1.6 %collective-permute-start.9 = (f32[288,128]{1,0:T(8,128)S(1)}, f32[288,128]{1,0:T(8,128)S(1)}, u32[]{:S(2)}, u32[]{:S(2)}) collective-permute-start(f32[288,128]{1,0:T(8,128)S(1)} %add.354), channel_id=1, source_target_pairs={{0,2},{1,3},{2,0},{3,1},{4,6},{5,7},{6,4},{7,5},{8,10},{9,11},{10,... | collective-permute-start | bytes 442376 | tf_op jit(solution)/shard_map/ppermute | solution.py:231
  58.3 5.0 %collective-permute-done.14 = f32[2,192,128]{2,1,0:T(8,128)S(1)} collective-permute-done((f32[2,192,128]{2,1,0:T(8,128)S(1)}, f32[2,192,128]{2,1,0:T(8,128)S(1)}, u32[]{:S(2)}, u32[]{:S(2)}) %collective-permute-start.14) | collective-permute-done | bytes 196640 | tf_op jit(solution)/shard_map/ppermute | solution.py:217
  64.5 1.6 %collective-permute-done.9 = f32[288,128]{1,0:T(8,128)S(1)} collective-permute-done((f32[288,128]{1,0:T(8,128)S(1)}, f32[288,128]{1,0:T(8,128)S(1)}, u32[]{:S(2)}, u32[]{:S(2)}) %collective-permute-start.9) | collective-permute-done | bytes 147488 | tf_op jit(solution)/shard_map/ppermute | solution.py:231
  66.1 5.1 %collective-permute-start.10 = (f32[288,128]{1,0:T(8,128)S(1)}, f32[288,128]{1,0:T(8,128)S(1)}, u32[]{:S(2)}, u32[]{:S(2)}) collective-permute-start(f32[288,128]{1,0:T(8,128)S(1)} %add.355), channel_id=1, source_target_pairs={{0,4},{1,5},{2,6},{3,7},{4,0},{5,1},{6,2},{7,3},{8,12},{9,13},{10,... | collective-permute-start | bytes 442376 | tf_op jit(solution)/shard_map/ppermute | solution.py:231
  72.8 10.3 %transpose_jvp___.1 = f32[384,256]{1,0:T(8,128)} custom-call(f32[3,12288]{1,0:T(4,128)} %bitcast.311, s32[1,12288]{1,0:T(1,128)} %bitcast.313), custom_call_target="tpu_custom_call" | custom-call | tf_op jit(solution)/shard_map/transpose(jvp())/pallas_call | solution.py:203
  83.7 1.7 %collective-permute-start.11 = (f32[288,128]{1,0:T(8,128)S(1)}, f32[288,128]{1,0:T(8,128)S(1)}, u32[]{:S(2)}, u32[]{:S(2)}) collective-permute-start(f32[288,128]{1,0:T(8,128)S(1)} %add.356), channel_id=1, source_target_pairs={{0,8},{1,9},{2,10},{3,11},{4,12},{5,13},{6,14},{7,15},{8,0},{9,1},... | collective-permute-start | bytes 442376 | tf_op jit(solution)/shard_map/ppermute | solution.py:231
  85.9 3.0 %collective-permute-done.11 = f32[288,128]{1,0:T(8,128)S(1)} collective-permute-done((f32[288,128]{1,0:T(8,128)S(1)}, f32[288,128]{1,0:T(8,128)S(1)}, u32[]{:S(2)}, u32[]{:S(2)}) %collective-permute-start.11) | collective-permute-done | bytes 147488 | tf_op jit(solution)/shard_map/ppermute | solution.py:231
  88.9 1.8 %collective-permute-start.12 = (f32[288,128]{1,0:T(8,128)S(1)}, f32[288,128]{1,0:T(8,128)S(1)}, u32[]{:S(2)}, u32[]{:S(2)}) collective-permute-start(f32[288,128]{1,0:T(8,128)S(1)} %add.357), channel_id=1, source_target_pairs={{0,16},{1,17},{2,18},{3,19},{4,20},{5,21},{6,22},{7,23},{8,24},{9,... | collective-permute-start | bytes 442376 | tf_op jit(solution)/shard_map/ppermute | solution.py:231
  91.9 2.0 %collective-permute-done.16 = f32[384,256]{1,0:T(8,128)S(1)} collective-permute-done((f32[384,256]{1,0:T(8,128)}, f32[384,256]{1,0:T(8,128)S(1)}, u32[]{:S(2)}, u32[]{:S(2)}) %collective-permute-start.16) | collective-permute-done | bytes 393248 | tf_op jit(solution)/shard_map/ppermute | solution.py:231
  94.7 2.2 %collective-permute-start.17 = (f32[384,256]{1,0:T(8,128)}, f32[384,256]{1,0:T(8,128)}, u32[]{:S(2)}, u32[]{:S(2)}) collective-permute-start(f32[384,256]{1,0:T(8,128)} %add.364), channel_id=1, source_target_pairs={{0,64},{32,96},{64,0},{96,32},{128,192},{160,224},{192,128},{224,1... | collective-permute-start | bytes 1179656 | tf_op jit(solution)/shard_map/ppermute | solution.py:231
  97.9 1.6 %copy.142 = f32[9,4096]{0,1:T(8,128)S(1)} copy(f32[9,4096]{1,0:T(8,128)} %get-tuple-element.63) | data formatting | bytes 294912 | tf_op jit(solution)/shard_map/sub | solution.py:177
  102.0 4.1 %collective-permute-done.17 = f32[384,256]{1,0:T(8,128)} collective-permute-done((f32[384,256]{1,0:T(8,128)}, f32[384,256]{1,0:T(8,128)}, u32[]{:S(2)}, u32[]{:S(2)}) %collective-permute-start.17) | collective-permute-done | bytes 393248 | tf_op jit(solution)/shard_map/ppermute | solution.py:231
  109.0 1.3 constant_dynamic-slice_fusion.3
  110.3 6.2 %collective-permute-done.18 = f32[384,256]{1,0:T(8,128)S(1)} collective-permute-done((f32[384,256]{1,0:T(8,128)S(1)}, f32[384,256]{1,0:T(8,128)S(1)}, u32[]{:S(2)}, u32[]{:S(2)}) %collective-permute-start.18) | collective-permute-done | bytes 393248 | tf_op jit(solution)/shard_map/ppermute | solution.py:231
  117.5 10.5 %shard_map.161 = f32[3,12288]{1,0:T(4,128)} custom-call(f32[384,256]{1,0:T(8,128)} %copy-done.2, s32[1,12288]{1,0:T(1,128)} %bitcast.314), custom_call_target="tpu_custom_call" | custom-call | tf_op jit(solution)/shard_map/pallas_call | solution.py:58
  (199 shorter events, 40.6 us)
Async XLA Ops:
  1.4 5.5 %collective-permute-start = (f32[1,27,128]{2,0,1:T(1,128)S(1)}, f32[1,27,128]{2,0,1:T(1,128)S(1)}, u32[]{:S(2)}, u32[]{:S(2)}) collective-permute-start(f32[1,27,128]{2,0,1:T(1,128)S(1)} %broadcast_in_dim.24), channel_id=1, source_target_pairs={{0,1},{1,0},{2,3},{3,2},{4,5},{5,4},{6,7},{7,6},{8,9},{9,8},{10,11... | collective-permute-start | bytes 41480 | tf_op jit(solution)/shard_map/ppermute | solution.py:217
  2.4 16.7 %collective-permute-start.5 = (f32[1,96,128]{2,1,0:T(8,128)S(1)}, f32[1,96,128]{2,1,0:T(8,128)S(1)}, u32[]{:S(2)}, u32[]{:S(2)}) collective-permute-start(f32[1,96,128]{2,1,0:T(8,128)S(1)} %broadcast_in_dim_reshape.6), channel_id=1, source_target_pairs={{0,32},{32,0},{64,96},{96,64},{128,160},{160,128},{192,224},{224,1... | collective-permute-start | bytes 147464 | tf_op jit(solution)/shard_map/ppermute | solution.py:217
  4.3 50.1 %collective-permute-start.13 = (f32[1,192,128]{2,1,0:T(8,128)S(1)}, f32[1,192,128]{2,1,0:T(8,128)S(1)}, u32[]{:S(2)}, u32[]{:S(2)}) collective-permute-start(f32[1,192,128]{2,1,0:T(8,128)S(1)} %broadcast_in_dim_reshape.7), channel_id=1, source_target_pairs={{0,32},{32,0},{64,96},{96,64},{128,160},{160,128},{192,224},{224,1... | collective-permute-start | bytes 294920 | tf_op jit(solution)/shard_map/ppermute | solution.py:217
  6.9 5.2 %collective-permute-start.1 = (f32[2,27,128]{2,0,1:T(2,128)S(1)}, f32[2,27,128]{2,0,1:T(2,128)S(1)}, u32[]{:S(2)}, u32[]{:S(2)}) collective-permute-start(f32[2,27,128]{2,0,1:T(2,128)S(1)} %maximum_select_fusion.14), channel_id=1, source_target_pairs={{0,2},{1,3},{2,0},{3,1},{4,6},{5,7},{6,4},{7,5},{8,10},{9,11},{10,... | collective-permute-start | bytes 82952 | tf_op jit(solution)/shard_map/ppermute | solution.py:217
  12.2 9.2 %collective-permute-start.2 = (f32[4,27,128]{2,0,1:T(4,128)S(1)}, f32[4,27,128]{2,0,1:T(4,128)S(1)}, u32[]{:S(2)}, u32[]{:S(2)}) collective-permute-start(f32[4,27,128]{2,0,1:T(4,128)S(1)} %maximum_select_fusion.13), channel_id=1, source_target_pairs={{0,4},{1,5},{2,6},{3,7},{4,0},{5,1},{6,2},{7,3},{8,12},{9,13},{10,... | collective-permute-start | bytes 165896 | tf_op jit(solution)/shard_map/ppermute | solution.py:217
  19.1 6.2 %collective-permute-start.6 = (f32[2,96,128]{2,1,0:T(8,128)S(1)}, f32[2,96,128]{2,1,0:T(8,128)S(1)}, u32[]{:S(2)}, u32[]{:S(2)}) collective-permute-start(f32[2,96,128]{2,1,0:T(8,128)S(1)} %maximum_select_fusion.12), channel_id=1, source_target_pairs={{0,64},{32,96},{64,0},{96,32},{128,192},{160,224},{192,128},{224,1... | collective-permute-start | bytes 294920 | tf_op jit(solution)/shard_map/ppermute | solution.py:217
  21.4 5.1 %collective-permute-start.3 = (f32[8,27,128]{2,0,1:T(8,128)S(1)}, f32[8,27,128]{2,0,1:T(8,128)S(1)}, u32[]{:S(2)}, u32[]{:S(2)}) collective-permute-start(f32[8,27,128]{2,0,1:T(8,128)S(1)} %maximum_select_fusion.10), channel_id=1, source_target_pairs={{0,8},{1,9},{2,10},{3,11},{4,12},{5,13},{6,14},{7,15},{8,0},{9,1},... | collective-permute-start | bytes 331784 | tf_op jit(solution)/shard_map/ppermute | solution.py:217
  25.3 5.8 %collective-permute-start.7 = (f32[4,96,128]{2,1,0:T(8,128)S(1)}, f32[4,96,128]{2,1,0:T(8,128)S(1)}, u32[]{:S(2)}, u32[]{:S(2)}) collective-permute-start(f32[4,96,128]{2,1,0:T(8,128)S(1)} %maximum_select_fusion.7), channel_id=1, source_target_pairs={{0,128},{32,160},{64,192},{96,224},{128,0},{160,32},{192,64},{224,... | collective-permute-start | bytes 589832 | tf_op jit(solution)/shard_map/ppermute | solution.py:217
  26.5 16.3 %copy-start.16 = (f32[2,12288]{1,0:T(2,128)S(1)}, f32[2,12288]{1,0:T(2,128)}, u32[]{:S(2)}) copy-start(f32[2,12288]{1,0:T(2,128)} %param.16) | copy-start | bytes 294916
  26.5 21.1 %collective-permute-start.4 = (f32[16,27,128]{2,0,1:T(8,128)S(1)}, f32[16,27,128]{2,0,1:T(8,128)S(1)}, u32[]{:S(2)}, u32[]{:S(2)}) collective-permute-start(f32[16,27,128]{2,0,1:T(8,128)S(1)} %maximum_select_fusion.5), channel_id=1, source_target_pairs={{0,16},{1,17},{2,18},{3,19},{4,20},{5,21},{6,22},{7,23},{8,24},{9,... | collective-permute-start | bytes 663560 | tf_op jit(solution)/shard_map/ppermute | solution.py:217
  46.9 3.8 %copy-start.7 = (f32[1,48,256]{2,1,0:T(8,128)}, f32[1,48,256]{2,1,0:T(8,128)S(1)}, u32[]{:S(2)}) copy-start(f32[1,48,256]{2,1,0:T(8,128)S(1)} %squeeze.42) | copy-start | bytes 147460
  46.9 3.8 %copy-start.9 = (f32[1,48,256]{2,1,0:T(8,128)}, f32[1,48,256]{2,1,0:T(8,128)S(1)}, u32[]{:S(2)}) copy-start(f32[1,48,256]{2,1,0:T(8,128)S(1)} %squeeze.43) | copy-start | bytes 147460
  54.2 1.7 %collective-permute-start.8 = (f32[288,128]{1,0:T(8,128)S(1)}, f32[288,128]{1,0:T(8,128)S(1)}, u32[]{:S(2)}, u32[]{:S(2)}) collective-permute-start(f32[288,128]{1,0:T(8,128)S(1)} %reshape.1205), channel_id=1, source_target_pairs={{0,1},{1,0},{2,3},{3,2},{4,5},{5,4},{6,7},{7,6},{8,9},{9,8},{10,11... | collective-permute-start | bytes 442376 | tf_op jit(solution)/shard_map/ppermute | solution.py:231
  54.4 17.6 %copy-start.5 = (s32[6,2,8,128]{3,1,2,0:T(2,128)}, s32[6,2,8,128]{3,1,2,0:T(2,128)S(1)}, u32[]{:S(2)}) copy-start(s32[6,2,8,128]{3,1,2,0:T(2,128)S(1)} %copy.162) | copy-start | bytes 147460
  54.4 8.9 %collective-permute-start.14 = (f32[2,192,128]{2,1,0:T(8,128)S(1)}, f32[2,192,128]{2,1,0:T(8,128)S(1)}, u32[]{:S(2)}, u32[]{:S(2)}) collective-permute-start(f32[2,192,128]{2,1,0:T(8,128)S(1)} %maximum_select_fusion.9), channel_id=1, source_target_pairs={{0,64},{32,96},{64,0},{96,32},{128,192},{160,224},{192,128},{224,1... | collective-permute-start | bytes 589832 | tf_op jit(solution)/shard_map/ppermute | solution.py:217
  56.0 10.2 %collective-permute-start.9 = (f32[288,128]{1,0:T(8,128)S(1)}, f32[288,128]{1,0:T(8,128)S(1)}, u32[]{:S(2)}, u32[]{:S(2)}) collective-permute-start(f32[288,128]{1,0:T(8,128)S(1)} %add.354), channel_id=1, source_target_pairs={{0,2},{1,3},{2,0},{3,1},{4,6},{5,7},{6,4},{7,5},{8,10},{9,11},{10,... | collective-permute-start | bytes 442376 | tf_op jit(solution)/shard_map/ppermute | solution.py:231
  63.4 22.4 %collective-permute-start.15 = (f32[4,192,128]{2,1,0:T(8,128)S(1)}, f32[4,192,128]{2,1,0:T(8,128)S(1)}, u32[]{:S(2)}, u32[]{:S(2)}) collective-permute-start(f32[4,192,128]{2,1,0:T(8,128)S(1)} %maximum_select_fusion.4), channel_id=1, source_target_pairs={{0,128},{32,160},{64,192},{96,224},{128,0},{160,32},{192,64},{224,... | collective-permute-start | bytes 1179656 | tf_op jit(solution)/shard_map/ppermute | solution.py:217
  66.1 17.5 %collective-permute-start.10 = (f32[288,128]{1,0:T(8,128)S(1)}, f32[288,128]{1,0:T(8,128)S(1)}, u32[]{:S(2)}, u32[]{:S(2)}) collective-permute-start(f32[288,128]{1,0:T(8,128)S(1)} %add.355), channel_id=1, source_target_pairs={{0,4},{1,5},{2,6},{3,7},{4,0},{5,1},{6,2},{7,3},{8,12},{9,13},{10,... | collective-permute-start | bytes 442376 | tf_op jit(solution)/shard_map/ppermute | solution.py:231
  83.2 10.7 %collective-permute-start.16 = (f32[384,256]{1,0:T(8,128)}, f32[384,256]{1,0:T(8,128)S(1)}, u32[]{:S(2)}, u32[]{:S(2)}) collective-permute-start(f32[384,256]{1,0:T(8,128)} %transpose_jvp___.1), channel_id=1, source_target_pairs={{0,32},{32,0},{64,96},{96,64},{128,160},{160,128},{192,224},{224,1... | collective-permute-start | bytes 1179656 | tf_op jit(solution)/shard_map/ppermute | solution.py:231
  83.7 5.2 %collective-permute-start.11 = (f32[288,128]{1,0:T(8,128)S(1)}, f32[288,128]{1,0:T(8,128)S(1)}, u32[]{:S(2)}, u32[]{:S(2)}) collective-permute-start(f32[288,128]{1,0:T(8,128)S(1)} %add.356), channel_id=1, source_target_pairs={{0,8},{1,9},{2,10},{3,11},{4,12},{5,13},{6,14},{7,15},{8,0},{9,1},... | collective-permute-start | bytes 442376 | tf_op jit(solution)/shard_map/ppermute | solution.py:231
  88.9 7.9 %collective-permute-start.12 = (f32[288,128]{1,0:T(8,128)S(1)}, f32[288,128]{1,0:T(8,128)S(1)}, u32[]{:S(2)}, u32[]{:S(2)}) collective-permute-start(f32[288,128]{1,0:T(8,128)S(1)} %add.357), channel_id=1, source_target_pairs={{0,16},{1,17},{2,18},{3,19},{4,20},{5,21},{6,22},{7,23},{8,24},{9,... | collective-permute-start | bytes 442376 | tf_op jit(solution)/shard_map/ppermute | solution.py:231
  94.7 11.5 %collective-permute-start.17 = (f32[384,256]{1,0:T(8,128)}, f32[384,256]{1,0:T(8,128)}, u32[]{:S(2)}, u32[]{:S(2)}) collective-permute-start(f32[384,256]{1,0:T(8,128)} %add.364), channel_id=1, source_target_pairs={{0,64},{32,96},{64,0},{96,32},{128,192},{160,224},{192,128},{224,1... | collective-permute-start | bytes 1179656 | tf_op jit(solution)/shard_map/ppermute | solution.py:231
  97.9 18.6 %copy-start.1 = (f32[384,256]{1,0:T(8,128)S(1)}, f32[384,256]{1,0:T(8,128)}, u32[]{:S(2)}) copy-start(f32[384,256]{1,0:T(8,128)} %copy.119.table_ref) | copy-start | bytes 1179652
  107.4 9.2 %collective-permute-start.18 = (f32[384,256]{1,0:T(8,128)S(1)}, f32[384,256]{1,0:T(8,128)S(1)}, u32[]{:S(2)}, u32[]{:S(2)}) collective-permute-start(f32[384,256]{1,0:T(8,128)S(1)} %add.365), channel_id=1, source_target_pairs={{0,128},{32,160},{64,192},{96,224},{128,0},{160,32},{192,64},{224,... | collective-permute-start | bytes 1179656 | tf_op jit(solution)/shard_map/ppermute | solution.py:231
  (13 other events, 31.0 us)
